TPU v7x, 512 devices: a whole 4x8x8 slice. The times are simulated.
512 devices in a mesh: patch: 128 (over y, z_lo, x), chan: 4 (over z_hi, core).
Axes of the slice: x: 4, y: 8, z: 8 (z_hi: 2, z_lo: 4; z = z_hi * 4 + z_lo), core: 2. Of those that a mesh axis runs over, the one named last changes fastest.
Arguments:
- latent: bfloat16 [8192, 1280], P('patch', 'chan'), may hold values from -6 to 6
- timestep: int32 [1], replicated, may hold values from 0 to 999
- norm_gain: float32 [1280], P('chan'), may hold values from 0.25 to 1.75
- norm_bias: float32 [1280], P('chan'), may hold values from -3 to 3
- w_time: bfloat16 [320, 1280], P(None, 'chan'), may hold values from -0.3125 to 0.3125
- w_query: bfloat16 [1280, 1024], P(None, 'chan'), may hold values from -0.15625 to 0.15625
- w_key: bfloat16 [1280, 1024], P(None, 'chan'), may hold values from -0.3125 to 0.3125
- w_value: bfloat16 [1280, 1024], P(None, 'chan'), may hold values from -0.15625 to 0.15625
- w_out: bfloat16 [1024, 1280], P('chan'), may hold values from -0.1875 to 0.1875
- stale_keys: bfloat16 [8192, 1024], P('patch', 'chan'), may hold values from -12 to 12
- stale_values: bfloat16 [8192, 1024], P('patch', 'chan'), may hold values from -6 to 6
Outputs:
- mixed: bfloat16 [8192, 1280], P('patch', 'chan')
- fresh_keys: bfloat16 [8192, 1024], P('patch', 'chan')
- fresh_values: bfloat16 [8192, 1024], P('patch', 'chan')
All inputs are finite; a program needn't handle non-finite values.
Results may differ from a plain program's by a relative error of at most 0.006.
Values may be sent and summed in bfloat16 or wider, within the bound.
No kernel may reach another device: no remote copies, remote signals or barrier semaphores. Data moves between devices by JAX's collectives and lax.ppermute only.
A program may use at most 64 MiB of HBM per device.

v0:
```python
import math

import jax
import jax.numpy as jnp
from jax import lax
from jax.sharding import PartitionSpec as P

D = 1280
HEAD_DIM = 64
GROUPS = 32


def timestep_shift(timestep, w_time):
    half_dim = w_time.shape[0] // 2
    frequency = jnp.exp(-math.log(10000.0) * jnp.arange(half_dim, dtype=jnp.float32) / half_dim)
    angles = timestep[0].astype(jnp.float32) * frequency
    embedding = jnp.concatenate([jnp.cos(angles), jnp.sin(angles)])
    return jnp.dot(
        jax.nn.silu(embedding)[None, :], w_time.astype(jnp.float32), precision=lax.Precision.HIGHEST
    )[0]


def local(
    latent,
    timestep,
    norm_gain,
    norm_bias,
    w_time,
    w_query,
    w_key,
    w_value,
    w_out,
    stale_keys,
    stale_values,
):
    rows_here, chan_width = latent.shape
    patch_count = lax.axis_size("patch")
    chan_count = lax.axis_size("chan")
    device = lax.axis_index("patch")
    local_groups = GROUPS // chan_count
    width = D // GROUPS
    values = latent.astype(jnp.float32).reshape(rows_here, local_groups, width)
    amount = rows_here * patch_count * width
    group_total = lax.psum(jnp.sum(values, axis=(0, 2)), "patch")
    group_mean = group_total / amount
    centered = values - group_mean[None, :, None]
    spread = lax.psum(jnp.sum(centered * centered, axis=(0, 2)), "patch")
    variance = spread / amount
    scaled = (centered * lax.rsqrt(variance + 1e-05)[None, :, None]).reshape(rows_here, chan_width)
    normed = (scaled * norm_gain + norm_bias + timestep_shift(timestep, w_time)).astype(
        jnp.bfloat16
    )
    inner = w_query.shape[1]
    shard_piece = lax.all_gather(normed, "chan", axis=1, tiled=True)
    outputs = []
    for index, weight_matrix in enumerate((w_query, w_key, w_value)):
        outputs.append(jnp.dot(shard_piece, weight_matrix, preferred_element_type=jnp.float32))
    summed = tuple(outputs)
    queries = summed[0].astype(jnp.bfloat16)
    fresh_keys = summed[1].astype(jnp.bfloat16)
    fresh_values = summed[2].astype(jnp.bfloat16)
    heads_here = inner // HEAD_DIM
    score_scale = HEAD_DIM ** (-0.5)
    query_heads = queries.reshape(rows_here, heads_here, HEAD_DIM)

    def slab_stats(key_block, value_block):
        score = (
            jnp.einsum("qhd,skhd->hqsk", query_heads, key_block, preferred_element_type=jnp.float32)
            * score_scale
        )
        block_max = jnp.max(score, axis=-1)
        weight = jnp.exp(score - block_max[..., None]).astype(jnp.bfloat16)
        block_num = jnp.einsum(
            "hqsk,skhd->hqsd", weight, value_block, preferred_element_type=jnp.float32
        )
        block_den = jnp.sum(weight.astype(jnp.float32), axis=-1)
        return (block_max, block_num, block_den)

    def combine(running, block_max, block_num, block_den):
        run_max, run_num, run_den = running
        new_max = jnp.maximum(run_max, jnp.max(block_max, axis=-1))
        keep_old = jnp.exp(run_max - new_max)
        factor = jnp.exp(block_max - new_max[..., None])
        run_num = keep_old[..., None] * run_num + jnp.sum(factor[..., None] * block_num, axis=2)
        run_den = keep_old * run_den + jnp.sum(factor * block_den, axis=2)
        return (new_max, run_num, run_den)

    home_max, home_num, home_den = slab_stats(
        fresh_keys.reshape(1, rows_here, heads_here, HEAD_DIM),
        fresh_values.reshape(1, rows_here, heads_here, HEAD_DIM),
    )
    start_state = (home_max[..., 0], home_num[:, :, 0], home_den[..., 0])
    key_piece = lax.all_gather(stale_keys, "patch", axis=0, tiled=True)
    value_piece = lax.all_gather(stale_values, "patch", axis=0, tiled=True)
    slab_count = key_piece.shape[0] // rows_here
    per_step = math.gcd(slab_count, 8)
    key_steps = key_piece.reshape(slab_count // per_step, per_step, rows_here, heads_here, HEAD_DIM)
    value_steps = value_piece.reshape(
        slab_count // per_step, per_step, rows_here, heads_here, HEAD_DIM
    )

    def advance(state, inputs):
        key_block, value_block, index = inputs
        block_max, block_num, block_den = slab_stats(key_block, value_block)
        slab_ids = index * per_step + jnp.arange(per_step, dtype=jnp.int32)
        is_home = slab_ids == device
        block_max = jnp.where(is_home[None, None, :], -1e30, block_max)
        return (combine(state, block_max, block_num, block_den), None)

    step_ids = jnp.arange(slab_count // per_step, dtype=jnp.int32)
    result, unused = lax.scan(advance, start_state, (key_steps, value_steps, step_ids))
    final_max, final_num, final_den = result
    attended = (
        jnp.transpose(final_num / final_den[..., None], (1, 0, 2))
        .reshape(rows_here, inner)
        .astype(jnp.bfloat16)
    )
    projected = lax.psum_scatter(
        jnp.dot(attended, w_out, preferred_element_type=jnp.float32).T,
        "chan",
        scatter_dimension=0,
        tiled=True,
    ).T
    mixed = (latent.astype(jnp.float32) + projected).astype(jnp.bfloat16)
    return (mixed, fresh_keys, fresh_values)


def solution(mesh):
    in_specs = (
        P("patch", "chan"),
        P(),
        P("chan"),
        P("chan"),
        P(None, "chan"),
        P(None, "chan"),
        P(None, "chan"),
        P(None, "chan"),
        P("chan", None),
        P("patch", "chan"),
        P("patch", "chan"),
    )
    out_specs = (P("patch", "chan"), P("patch", "chan"), P("patch", "chan"))
    return jax.shard_map(local, mesh=mesh, in_specs=in_specs, out_specs=out_specs, check_vma=False)
```

profile of v0, /device:TPU:1, one launch (start us, length us, event | category | flops | bytes accessed | tf_op | source)
XLA Modules:
  0.0 1531.6 jit_solution(9358067000586807633)
XLA Ops:
  7.2 0.7 all-gather.4.cloned.1.call-update
  8.0 0.7 all-gather.6.cloned.1.call-update
  8.7 0.8 convert_reduce_fusion.1
  9.7 319.5 %psum.14 = f32[8]{0:T(128)S(1)} all-reduce(f32[8]{0:T(128)S(1)} %reduce_sum.70), channel_id=1, replica_groups=mesh['patch'=128,'chan'=4] {'patch'}, use_global_device_ids=true, to_apply=%region_2.0 | all-reduce | flops 8 | bytes 64 | tf_op jit(solution)/shard_map/psum | solution.py:44
  329.4 0.8 fusion.7
  330.4 309.2 %psum.15 = f32[8]{0:T(128)S(1)} all-reduce(f32[8]{0:T(128)S(1)} %reduce_sum.73), channel_id=1, replica_groups=mesh['patch'=128,'chan'=4] {'patch'}, use_global_device_ids=true, to_apply=%region_5.6 | all-reduce | flops 8 | bytes 64 | tf_op jit(solution)/shard_map/psum | solution.py:47
  640.5 1.2 convolution_reduce_fusion
  641.7 0.8 fusion.14
  642.6 116.3 %all-gather = bf16[4,320,64]{1,2,0:T(8,128)(2,1)S(1)} all-gather(bf16[1,320,64]{1,2,0:T(8,128)(2,1)S(1)} %fusion.14), channel_id=1, replica_groups=mesh['patch'=128,'chan'=4] {'chan'}, dimensions={0}, use_global_device_ids=true | all-gather | bytes 204800 | tf_op jit(solution)/shard_map/all_gather | solution.py:54
  759.2 1.3 convolution_convert_fusion.2
  760.6 1.3 convolution_convert_fusion.1
  762.1 1.3 convolution_convert_fusion
  764.0 12.9 reshape.91
  776.9 528.4 %all-gather.6.cloned.1.call-done = bf16[8192,256]{1,0:T(8,128)(2,1)} async-done(((bf16[64,256]{1,0:T(8,128)(2,1)}), bf16[8192,256]{1,0:T(8,128)(2,1)}) %all-gather.6.cloned.1.call-update) | async-done | bytes 4194320 | tf_op jit(solution)/shard_map/all_gather | solution.py:94
  1305.2 12.9 reshape.92
  1318.1 68.4 %while.14 = (s32[]{:T(128)}, f32[4,64]{1,0:T(4,128)S(1)}, f32[4,64,64]{1,2,0:T(8,128)S(1)}, f32[4,64]{1,0:T(4,128)S(1)}, s32[16]{0:T(128)S(1)}, /*index=5*/s32[]...) while((s32[]{:T(128)}, f32[4,64]{1,0:T(4,128)S(1)}, ...), condition=%wide.region_14.15_spmd, body=%wide.region_8.14_spmd.sunk | while | flops 34890256 | bytes 4054185 | solution.py:111
  1318.2 1.6 constant_dynamic-slice_fusion.3
  1320.1 0.6 dynamic_slice.16
  1321.6 0.4 copy.86
  1322.4 1.6 constant_dynamic-slice_fusion.3
  1324.3 0.6 dynamic_slice.16
  1325.9 0.4 copy.86
  1326.7 1.6 constant_dynamic-slice_fusion.3
  1328.6 0.6 dynamic_slice.16
  1330.2 0.4 copy.86
  1331.0 1.6 constant_dynamic-slice_fusion.3
  1332.9 0.6 dynamic_slice.16
  1334.5 0.4 copy.86
  1335.3 1.6 constant_dynamic-slice_fusion.3
  1337.2 0.6 dynamic_slice.16
  1339.5 1.6 constant_dynamic-slice_fusion.3
  1341.4 0.6 dynamic_slice.16
  1343.0 0.4 copy.86
  1343.8 1.6 constant_dynamic-slice_fusion.3
  1345.7 0.6 dynamic_slice.16
  1347.3 0.4 copy.86
  1348.1 1.6 constant_dynamic-slice_fusion.3
  1350.0 0.6 dynamic_slice.16
  1351.6 0.4 copy.86
  1352.4 1.6 constant_dynamic-slice_fusion.3
  1354.3 0.6 dynamic_slice.16
  1356.6 1.6 constant_dynamic-slice_fusion.3
  1358.5 0.6 dynamic_slice.16
  1360.1 0.4 copy.86
  1360.9 1.6 constant_dynamic-slice_fusion.3
  1362.8 0.6 dynamic_slice.16
  1364.4 0.4 copy.86
  1365.2 1.6 constant_dynamic-slice_fusion.3
  1367.1 0.6 dynamic_slice.16
  1369.5 1.6 constant_dynamic-slice_fusion.3
  1371.4 0.6 dynamic_slice.16
  1373.0 0.4 copy.86
  1373.8 1.6 constant_dynamic-slice_fusion.3
  1375.7 0.6 dynamic_slice.16
  1377.2 0.4 copy.86
  1378.0 1.6 constant_dynamic-slice_fusion.3
  1379.9 0.6 dynamic_slice.16
  1381.5 0.4 copy.86
  1382.3 1.6 constant_dynamic-slice_fusion.3
  1384.2 0.6 dynamic_slice.16
  1386.9 1.1 copy.67
  1388.0 135.4 %reduce-scatter.4.cloned.1.call-done = f32[320,64]{1,0:T(8,128)} async-done(((f32[1280,64]{1,0:T(8,128)}), f32[320,64]{1,0:T(8,128)}) %reduce-scatter.4.cloned.1.call-update) | async-done | bytes 81936
  1523.4 1.0 copy.68
  1524.4 0.6 fusion.12
  (202 shorter events, 21.1 us)
Async XLA Ops:
  7.2 1379.4 %copy-start = (bf16[256,1280]{1,0:T(8,128)(2,1)S(1)}, bf16[256,1280]{1,0:T(8,128)(2,1)}, u32[]{:S(2)}) copy-start(bf16[256,1280]{1,0:T(8,128)(2,1)} %param.21) | copy-start | bytes 1966084
  7.2 756.8 %all-gather.4.cloned.1.call-start = ((), (), s32[]{:S(2)}) async-start(), calls=%async_computation.1 | async-start | bytes 4227072 | tf_op jit(solution)/shard_map/all_gather | solution.py:93
  7.9 1297.3 %all-gather.6.cloned.1.call-start = ((), (), s32[]{:S(2)}) async-start(), calls=%async_computation.2 | async-start | bytes 4227072 | tf_op jit(solution)/shard_map/all_gather | solution.py:94
  8.7 1514.7 %reduce-scatter.4.cloned.1.call-start = ((), (), s32[]{:S(2)}) async-start(), calls=%async_computation.3 | async-start | bytes 819200
  762.0 556.2 %copy-start.2 = (bf16[64,256]{1,0:T(8,128)(2,1)}, bf16[64,256]{1,0:T(8,128)(2,1)S(1)}, u32[]{:S(2)}) copy-start(bf16[64,256]{1,0:T(8,128)(2,1)S(1)} %convolution_convert_fusion.1) | copy-start | bytes 98308
  763.4 554.7 %copy-start.3 = (bf16[64,256]{1,0:T(8,128)(2,1)}, bf16[64,256]{1,0:T(8,128)(2,1)S(1)}, u32[]{:S(2)}) copy-start(bf16[64,256]{1,0:T(8,128)(2,1)S(1)} %convolution_convert_fusion) | copy-start | bytes 98308
  1318.1 206.3 %copy-start.1 = (bf16[64,320]{1,0:T(8,128)(2,1)S(1)}, bf16[64,320]{1,0:T(8,128)(2,1)}, u32[]{:S(2)}) copy-start(bf16[64,320]{1,0:T(8,128)(2,1)} %param.13) | copy-start | bytes 122884
Sparse Core Ops, SparseCore 0:
  10.1 606.6 all-gather.3
  618.9 686.3 all-gather.5
  1388.1 135.2 reduce-scatter.3
where the time goes:
time: 1530 us
  blocking collectives  745 us (49%)
  waiting for transfers between devices  665 us (43%)
  local copies, waits for them, and re-layouts  69.9 us (5%)
  matrix products  15.5 us (1%)
    all_gather x1, waiting for transfers between devices, local(): value_piece = lax.all_gather(stale_values, 'patch', axis=0, tiled=True)  528 us
    psum x1, blocking collectives, local(): group_total = lax.psum(jnp.sum(values, axis=(0, 2)), 'patch')  319 us
    psum x1, blocking collectives, local(): spread = lax.psum(jnp.sum(centered * centered, axis=(0, 2)), 'patch')  309 us
    unnamed x4, waiting for transfers between devices  137 us
    all_gather x1, blocking collectives, local(): shard_piece = lax.all_gather(normed, 'chan', axis=1, tiled=True)  116 us
    dynamic_slice x48, local copies, waits for them, and re-layouts, local(): lax.scan(advance, start_state, (key_steps, value_steps, step_ids))  40.8 us
  transfers between devices with their start and end apart: 3, of which 2 were waited for; matrix products, arithmetic and copies ran while one was open for 1% of the time, Pallas kernels for 0%

commit v1 on v0

--- a/solution.py
+++ b/solution.py
@@ -3,11 +3,14 @@
 import jax
 import jax.numpy as jnp
 from jax import lax
+from jax.sharding import Mesh
 from jax.sharding import PartitionSpec as P
 
 D = 1280
 HEAD_DIM = 64
 GROUPS = 32
+PATCH_AXES = ("py", "pz", "px")
+PATCH_SPLIT = (8, 4, 4)
 
 
 def timestep_shift(timestep, w_time):
@@ -18,6 +21,12 @@
     return jnp.dot(
         jax.nn.silu(embedding)[None, :], w_time.astype(jnp.float32), precision=lax.Precision.HIGHEST
     )[0]
+
+
+def patch_sum(partial):
+    for name in reversed(PATCH_AXES):
+        partial = lax.optimization_barrier(lax.psum(partial, name))
+    return partial
 
 
 def local(
@@ -34,17 +43,17 @@
     stale_values,
 ):
     rows_here, chan_width = latent.shape
-    patch_count = lax.axis_size("patch")
+    patch_count = math.prod(lax.axis_size(name) for name in PATCH_AXES)
     chan_count = lax.axis_size("chan")
-    device = lax.axis_index("patch")
+    device = lax.axis_index(PATCH_AXES)
     local_groups = GROUPS // chan_count
     width = D // GROUPS
     values = latent.astype(jnp.float32).reshape(rows_here, local_groups, width)
     amount = rows_here * patch_count * width
-    group_total = lax.psum(jnp.sum(values, axis=(0, 2)), "patch")
+    group_total = patch_sum(jnp.sum(values, axis=(0, 2)))
     group_mean = group_total / amount
     centered = values - group_mean[None, :, None]
-    spread = lax.psum(jnp.sum(centered * centered, axis=(0, 2)), "patch")
+    spread = patch_sum(jnp.sum(centered * centered, axis=(0, 2)))
     variance = spread / amount
     scaled = (centered * lax.rsqrt(variance + 1e-05)[None, :, None]).reshape(rows_here, chan_width)
     normed = (scaled * norm_gain + norm_bias + timestep_shift(timestep, w_time)).astype(
@@ -90,8 +99,11 @@
         fresh_values.reshape(1, rows_here, heads_here, HEAD_DIM),
     )
     start_state = (home_max[..., 0], home_num[:, :, 0], home_den[..., 0])
-    key_piece = lax.all_gather(stale_keys, "patch", axis=0, tiled=True)
-    value_piece = lax.all_gather(stale_values, "patch", axis=0, tiled=True)
+    stacked = jnp.stack([stale_keys, stale_values])
+    for name in reversed(PATCH_AXES):
+        stacked = lax.all_gather(stacked, name, axis=1, tiled=True)
+    key_piece = stacked[0]
+    value_piece = stacked[1]
     slab_count = key_piece.shape[0] // rows_here
     per_step = math.gcd(slab_count, 8)
     key_steps = key_piece.reshape(slab_count // per_step, per_step, rows_here, heads_here, HEAD_DIM)
@@ -126,8 +138,11 @@
 
 
 def solution(mesh):
+    devices = mesh.devices.reshape(PATCH_SPLIT + (mesh.shape["chan"],))
+    split_mesh = Mesh(devices, PATCH_AXES + ("chan",))
+    rows = PATCH_AXES
     in_specs = (
-        P("patch", "chan"),
+        P(rows, "chan"),
         P(),
         P("chan"),
         P("chan"),
@@ -136,8 +151,10 @@
         P(None, "chan"),
         P(None, "chan"),
         P("chan", None),
-        P("patch", "chan"),
-        P("patch", "chan"),
+        P(rows, "chan"),
+        P(rows, "chan"),
     )
-    out_specs = (P("patch", "chan"), P("patch", "chan"), P("patch", "chan"))
-    return jax.shard_map(local, mesh=mesh, in_specs=in_specs, out_specs=out_specs, check_vma=False)
+    out_specs = (P(rows, "chan"), P(rows, "chan"), P(rows, "chan"))
+    return jax.shard_map(
+        local, mesh=split_mesh, in_specs=in_specs, out_specs=out_specs, check_vma=False
+    )

time: 1530 us -> 318 us (0.21)
  blocking collectives: 745 us -> 92.8 us
  waiting for transfers between devices: 665 us -> 95.7 us
    psum x2 -> x6, blocking collectives: 629 us -> 59.9 us  [patch_sum(): partial = lax.optimization_barrier(lax.psum(partial, name))]
    all_gather x2, waiting for transfers between devices: 528 us -> 49.8 us  [local(): stacked = lax.all_gather(stacked, name, axis=1, tiled=True)]
    all_gather x1, blocking collectives: 116 us -> 21.6 us  [local(): shard_piece = lax.all_gather(normed, 'chan', axis=1, tiled=True)]
    unnamed x4, waiting for transfers between devices: 137 us -> 46 us
    reshape x2 -> x0, local copies, waits for them, and re-layouts: 25.8 us -> none  [the longest x1 12.9 us: local(): key_piece.reshape(slab_count // per_step, per_step, rows_here, heads_here...]
    another operation x2 -> x4, local copies, waits for them, and re-layouts: 0.21 us -> 26 us  [the longest x1 12.9 us: local(): key_piece.reshape(slab_count // per_step, per_step, rows_here, heads_here...]
  transfers between devices with their start and end apart: 3 -> 3, of which waited for: 2 -> 3; matrix products, arithmetic and copies ran while one was open for 1% -> 3% of each run, Pallas kernels for 0% -> 0%
where the time goes in v1:
time: 318 us; the launch traced here: 317 us
  waiting for transfers between devices  95.7 us (30%)
  blocking collectives  92.8 us (29%)
  local copies, waits for them, and re-layouts  75.6 us (24%)
  matrix products  15.5 us (5%)
  between operations  14.6 us (5%)
  other arithmetic  12 us (4%)
  loops' own time  10.3 us (3%)
    psum x6, blocking collectives, patch_sum(): partial = lax.optimization_barrier(lax.psum(partial, name))  59.9 us
    all_gather x2, waiting for transfers between devices, local(): stacked = lax.all_gather(stacked, name, axis=1, tiled=True)  49.8 us
    unnamed x4, waiting for transfers between devices  46 us
    dynamic_slice x48, local copies, waits for them, and re-layouts, local(): lax.scan(advance, start_state, (key_steps, value_steps, step_ids))  40.8 us
    all_gather x1, blocking collectives, local(): shard_piece = lax.all_gather(normed, 'chan', axis=1, tiled=True)  21.6 us
    another operation x1, local copies, waits for them, and re-layouts, local(): key_piece.reshape(slab_count // per_step, per_step, rows_here, heads_here...  12.9 us
    another operation x1, local copies, waits for them, and re-layouts, local(): value_piece.reshape(slab_count // per_step, per_step, rows_here, heads_he...  12.9 us
    all_gather x1, blocking collectives, local(): stacked = lax.all_gather(stacked, name, axis=1, tiled=True)  11.3 us
  transfers between devices with their start and end apart: 3, of which 3 were waited for; matrix products, arithmetic and copies ran while one was open for 3% of the time, Pallas kernels for 0%

profile of v1, /device:TPU:1, one launch (start us, length us, event | category | flops | bytes accessed | tf_op | source)
XLA Modules:
  0.0 316.6 jit_solution(5863257001115727896)
XLA Ops:
  7.2 0.8 pad_maximum_fusion
  8.1 11.3 %all_gather.13 = bf16[2,256,256]{2,1,0:T(8,128)(2,1)} all-gather(bf16[2,64,256]{2,1,0:T(8,128)(2,1)S(1)} %pad_maximum_fusion), channel_id=1, replica_groups=mesh['py'=8,'pz'=4,'px'=4,'chan'=4] {'px'}, dimensions={1}, use_global_device_ids=true | all-gather | bytes 327680 | tf_op jit(solution)/shard_map/all_gather | solution.py:104
  19.4 43.1 %all-gather.4.cloned.1.call-done = bf16[2,1024,256]{2,1,0:T(8,128)(2,1)} async-done(((bf16[2,256,256]{2,1,0:T(8,128)(2,1)}), bf16[2,1024,256]{2,1,0:T(8,128)(2,1)}) %all-gather.4.cloned.1.call-update) | async-done | bytes 1048592 | tf_op jit(solution)/shard_map/all_gather | solution.py:104
  62.6 0.8 convert_reduce_fusion.1
  63.6 8.4 %psum.42 = f32[8]{0:T(128)S(1)} all-reduce(f32[8]{0:T(128)S(1)} %reduce_sum.70), channel_id=1, replica_groups=mesh['py'=8,'pz'=4,'px'=4,'chan'=4] {'px'}, use_global_device_ids=true, to_apply=%region_2.0 | all-reduce | flops 8 | bytes 64 | tf_op jit(solution)/shard_map/psum | solution.py:28
  72.0 7.5 %psum.43 = f32[8]{0:T(128)S(1)} all-reduce(f32[8]{0:T(128)S(1)} %psum.42), channel_id=1, replica_groups=mesh['py'=8,'pz'=4,'px'=4,'chan'=4] {'pz'}, use_global_device_ids=true, to_apply=%region_3.0 | all-reduce | flops 8 | bytes 64 | tf_op jit(solution)/shard_map/psum | solution.py:28
  79.6 15.7 %psum.44 = f32[8]{0:T(128)S(1)} all-reduce(f32[8]{0:T(128)S(1)} %psum.43), channel_id=1, replica_groups=mesh['py'=8,'pz'=4,'px'=4,'chan'=4] {'py'}, use_global_device_ids=true, to_apply=%region_4.0 | all-reduce | flops 8 | bytes 64 | tf_op jit(solution)/shard_map/psum | solution.py:28
  95.4 0.8 fusion.7
  96.5 6.8 %psum.45 = f32[8]{0:T(128)S(1)} all-reduce(f32[8]{0:T(128)S(1)} %reduce_sum.73), channel_id=1, replica_groups=mesh['py'=8,'pz'=4,'px'=4,'chan'=4] {'px'}, use_global_device_ids=true, to_apply=%region_7.0 | all-reduce | flops 8 | bytes 64 | tf_op jit(solution)/shard_map/psum | solution.py:28
  103.3 7.6 %psum.46 = f32[8]{0:T(128)S(1)} all-reduce(f32[8]{0:T(128)S(1)} %psum.45), channel_id=1, replica_groups=mesh['py'=8,'pz'=4,'px'=4,'chan'=4] {'pz'}, use_global_device_ids=true, to_apply=%region_8.9 | all-reduce | flops 8 | bytes 64 | tf_op jit(solution)/shard_map/psum | solution.py:28
  110.8 13.9 %psum.47 = f32[8]{0:T(128)S(1)} all-reduce(f32[8]{0:T(128)S(1)} %psum.46), channel_id=1, replica_groups=mesh['py'=8,'pz'=4,'px'=4,'chan'=4] {'py'}, use_global_device_ids=true, to_apply=%region_9.10 | all-reduce | flops 8 | bytes 64 | tf_op jit(solution)/shard_map/psum | solution.py:28
  125.7 1.2 convolution_reduce_fusion
  126.9 0.8 fusion.14
  127.7 21.6 %all-gather = bf16[4,320,64]{1,2,0:T(8,128)(2,1)S(1)} all-gather(bf16[1,320,64]{1,2,0:T(8,128)(2,1)S(1)} %fusion.14), channel_id=1, replica_groups=mesh['py'=8,'pz'=4,'px'=4,'chan'=4] {'chan'}, dimensions={0}, use_global_device_ids=true | all-gather | bytes 204800 | tf_op jit(solution)/shard_map/all_gather | solution.py:63
  149.7 1.3 convolution_convert_fusion.2
  151.1 1.3 convolution_convert_fusion.1
  152.6 1.3 convolution_convert_fusion
  154.5 6.6 %all-gather.6.cloned.1.call-done = bf16[2,8192,256]{2,1,0:T(8,128)(2,1)} async-done(((bf16[2,1024,256]{2,1,0:T(8,128)(2,1)}), bf16[2,8192,256]{2,1,0:T(8,128)(2,1)}) %all-gather.6.cloned.1.call-update) | async-done | bytes 8388624 | tf_op jit(solution)/shard_map/all_gather | solution.py:104
  161.1 5.8 %fusion.19 = (bf16[1,8192,256]{2,1,0:T(8,128)(2,1)}, bf16[1,8192,256]{2,1,0:T(8,128)(2,1)}) fusion(bf16[2,8192,256]{2,1,0:T(8,128)(2,1)} %all-gather.6.cloned.1.call-done), kind=kLoop, calls=%fused_computation.52 | loop fusion | bytes 16777216 | tf_op jit(solution)/shard_map/slice | solution.py:106
  166.9 12.9 %reshape.83 = bf16[16,8,64,4,64]{4,3,2,1,0:T(4,128)(2,1)} reshape(bf16[1,8192,256]{2,1,0:T(8,128)(2,1)} %get-tuple-element.116) | data formatting | bytes 8388608 | tf_op jit(solution)/shard_map/reshape;squeeze | solution.py:109
  179.8 12.9 %reshape.84 = bf16[16,8,64,4,64]{4,3,2,1,0:T(4,128)(2,1)} reshape(bf16[1,8192,256]{2,1,0:T(8,128)(2,1)} %get-tuple-element.115) | data formatting | bytes 8388608 | tf_op jit(solution)/shard_map/reshape;squeeze | solution.py:110
  192.7 68.4 %while.14 = (s32[]{:T(128)}, f32[4,64]{1,0:T(4,128)S(1)}, f32[4,64,64]{1,2,0:T(8,128)S(1)}, f32[4,64]{1,0:T(4,128)S(1)}, s32[16]{0:T(128)S(1)}, /*index=5*/s32[]...) while((s32[]{:T(128)}, f32[4,64]{1,0:T(4,128)S(1)}, ...), condition=%wide.region_18.19_spmd, body=%wide.region_12.18_spmd.sunk | while | flops 34890256 | bytes 4054185 | solution.py:123
  192.7 1.6 constant_dynamic-slice_fusion.3
  194.6 0.6 dynamic_slice.16
  196.1 0.4 copy.86
  196.9 1.6 constant_dynamic-slice_fusion.3
  198.8 0.6 dynamic_slice.16
  200.4 0.4 copy.86
  201.2 1.6 constant_dynamic-slice_fusion.3
  203.1 0.6 dynamic_slice.16
  204.7 0.4 copy.86
  205.5 1.6 constant_dynamic-slice_fusion.3
  207.4 0.6 dynamic_slice.16
  209.0 0.4 copy.86
  209.8 1.6 constant_dynamic-slice_fusion.3
  211.7 0.6 dynamic_slice.16
  213.3 0.4 copy.86
  214.0 1.6 constant_dynamic-slice_fusion.3
  216.0 0.6 dynamic_slice.16
  217.5 0.4 copy.86
  218.3 1.6 constant_dynamic-slice_fusion.3
  220.2 0.6 dynamic_slice.16
  222.6 1.6 constant_dynamic-slice_fusion.3
  224.5 0.6 dynamic_slice.16
  226.9 1.6 constant_dynamic-slice_fusion.3
  228.8 0.6 dynamic_slice.16
  231.2 1.6 constant_dynamic-slice_fusion.3
  233.1 0.6 dynamic_slice.16
  235.4 1.6 constant_dynamic-slice_fusion.3
  237.3 0.6 dynamic_slice.16
  239.7 1.6 constant_dynamic-slice_fusion.3
  241.6 0.6 dynamic_slice.16
  244.0 1.6 constant_dynamic-slice_fusion.3
  245.9 0.6 dynamic_slice.16
  248.3 1.6 constant_dynamic-slice_fusion.3
  250.2 0.6 dynamic_slice.16
  252.5 1.6 constant_dynamic-slice_fusion.3
  254.5 0.6 dynamic_slice.16
  256.8 1.6 constant_dynamic-slice_fusion.3
  258.7 0.6 dynamic_slice.16
  261.4 1.1 copy.67
  262.5 45.9 %reduce-scatter.4.cloned.1.call-done = f32[320,64]{1,0:T(8,128)} async-done(((f32[1280,64]{1,0:T(8,128)}), f32[320,64]{1,0:T(8,128)}) %reduce-scatter.4.cloned.1.call-update) | async-done | bytes 81936
  308.4 1.0 copy.68
  309.4 0.6 fusion.12
  (209 shorter events, 23.4 us)
Async XLA Ops:
  7.2 254.0 %copy-start = (bf16[256,1280]{1,0:T(8,128)(2,1)S(1)}, bf16[256,1280]{1,0:T(8,128)(2,1)}, u32[]{:S(2)}) copy-start(bf16[256,1280]{1,0:T(8,128)(2,1)} %param.21) | copy-start | bytes 1966084
  7.2 55.4 %all-gather.4.cloned.1.call-start = ((), (), s32[]{:S(2)}) async-start(), calls=%async_computation.1 | async-start | bytes 1310720 | tf_op jit(solution)/shard_map/all_gather | solution.py:104
  19.4 141.8 %all-gather.6.cloned.1.call-start = ((), (), s32[]{:S(2)}) async-start(), calls=%async_computation.2 | async-start | bytes 9437184 | tf_op jit(solution)/shard_map/all_gather | solution.py:104
  62.6 245.9 %reduce-scatter.4.cloned.1.call-start = ((), (), s32[]{:S(2)}) async-start(), calls=%async_computation.3 | async-start | bytes 819200
  152.5 14.4 %copy-start.2 = (bf16[64,256]{1,0:T(8,128)(2,1)}, bf16[64,256]{1,0:T(8,128)(2,1)S(1)}, u32[]{:S(2)}) copy-start(bf16[64,256]{1,0:T(8,128)(2,1)S(1)} %convolution_convert_fusion.1) | copy-start | bytes 98308
  153.9 13.0 %copy-start.3 = (bf16[64,256]{1,0:T(8,128)(2,1)}, bf16[64,256]{1,0:T(8,128)(2,1)S(1)}, u32[]{:S(2)}) copy-start(bf16[64,256]{1,0:T(8,128)(2,1)S(1)} %convolution_convert_fusion) | copy-start | bytes 98308
  192.7 116.8 %copy-start.1 = (bf16[64,320]{1,0:T(8,128)(2,1)S(1)}, bf16[64,320]{1,0:T(8,128)(2,1)}, u32[]{:S(2)}) copy-start(bf16[64,320]{1,0:T(8,128)(2,1)} %param.13) | copy-start | bytes 122884
Sparse Core Ops, SparseCore 0:
  19.5 43.0 all-gather.3
  64.6 96.4 all-gather.5
  262.6 45.7 reduce-scatter.3

commit v2 on v1

--- a/solution.py
+++ b/solution.py
@@ -70,63 +70,58 @@
     fresh_values = summed[2].astype(jnp.bfloat16)
     heads_here = inner // HEAD_DIM
     score_scale = HEAD_DIM ** (-0.5)
-    query_heads = queries.reshape(rows_here, heads_here, HEAD_DIM)
+    split = lax.axis_size("px")
+    own_head = lax.axis_index("px")
 
-    def slab_stats(key_block, value_block):
-        score = (
-            jnp.einsum("qhd,skhd->hqsk", query_heads, key_block, preferred_element_type=jnp.float32)
-            * score_scale
-        )
-        block_max = jnp.max(score, axis=-1)
-        weight = jnp.exp(score - block_max[..., None]).astype(jnp.bfloat16)
-        block_num = jnp.einsum(
-            "hqsk,skhd->hqsd", weight, value_block, preferred_element_type=jnp.float32
-        )
-        block_den = jnp.sum(weight.astype(jnp.float32), axis=-1)
-        return (block_max, block_num, block_den)
+    stacked = lax.all_gather(jnp.stack([stale_keys, stale_values]), "px", axis=1, tiled=True)
+    stacked = lax.dynamic_slice_in_dim(stacked, own_head * HEAD_DIM, HEAD_DIM, axis=2)
+    for name in reversed(PATCH_AXES[:-1]):
+        stacked = lax.all_gather(stacked, name, axis=1, tiled=True)
+    slab_count = stacked.shape[1] // rows_here
+    stale_k = stacked[0].reshape(slab_count, rows_here, HEAD_DIM)
+    stale_v = stacked[1].reshape(slab_count, rows_here, HEAD_DIM)
 
-    def combine(running, block_max, block_num, block_den):
-        run_max, run_num, run_den = running
-        new_max = jnp.maximum(run_max, jnp.max(block_max, axis=-1))
-        keep_old = jnp.exp(run_max - new_max)
-        factor = jnp.exp(block_max - new_max[..., None])
-        run_num = keep_old[..., None] * run_num + jnp.sum(factor[..., None] * block_num, axis=2)
-        run_den = keep_old * run_den + jnp.sum(factor * block_den, axis=2)
-        return (new_max, run_num, run_den)
+    fresh = jnp.stack([queries, fresh_keys, fresh_values]).reshape(
+        3, rows_here, heads_here, HEAD_DIM
+    )
+    fresh = lax.all_to_all(fresh, "px", 2, 1, tiled=True).reshape(3, split, rows_here, HEAD_DIM)
+    query_rows = fresh[0].reshape(split * rows_here, HEAD_DIM)
 
-    home_max, home_num, home_den = slab_stats(
-        fresh_keys.reshape(1, rows_here, heads_here, HEAD_DIM),
-        fresh_values.reshape(1, rows_here, heads_here, HEAD_DIM),
+    score = (
+        jnp.einsum("qd,skd->qsk", query_rows, stale_k, preferred_element_type=jnp.float32)
+        * score_scale
     )
-    start_state = (home_max[..., 0], home_num[:, :, 0], home_den[..., 0])
-    stacked = jnp.stack([stale_keys, stale_values])
-    for name in reversed(PATCH_AXES):
-        stacked = lax.all_gather(stacked, name, axis=1, tiled=True)
-    key_piece = stacked[0]
-    value_piece = stacked[1]
-    slab_count = key_piece.shape[0] // rows_here
-    per_step = math.gcd(slab_count, 8)
-    key_steps = key_piece.reshape(slab_count // per_step, per_step, rows_here, heads_here, HEAD_DIM)
-    value_steps = value_piece.reshape(
-        slab_count // per_step, per_step, rows_here, heads_here, HEAD_DIM
+    block_max = jnp.max(score, axis=-1)
+    weight = jnp.exp(score - block_max[..., None]).astype(jnp.bfloat16)
+    block_num = jnp.einsum("qsk,skd->qsd", weight, stale_v, preferred_element_type=jnp.float32)
+    block_den = jnp.sum(weight.astype(jnp.float32), axis=-1)
+
+    home_score = (
+        jnp.einsum("gqd,gkd->gqk", fresh[0], fresh[1], preferred_element_type=jnp.float32)
+        * score_scale
     )
+    home_max = jnp.max(home_score, axis=-1)
+    home_weight = jnp.exp(home_score - home_max[..., None]).astype(jnp.bfloat16)
+    home_num = jnp.einsum("gqk,gkd->gqd", home_weight, fresh[2], preferred_element_type=jnp.float32)
+    home_den = jnp.sum(home_weight.astype(jnp.float32), axis=-1)
+    home_max = home_max.reshape(split * rows_here, 1)
+    home_num = home_num.reshape(split * rows_here, 1, HEAD_DIM)
+    home_den = home_den.reshape(split * rows_here, 1)
 
-    def advance(state, inputs):
-        key_block, value_block, index = inputs
-        block_max, block_num, block_den = slab_stats(key_block, value_block)
-        slab_ids = index * per_step + jnp.arange(per_step, dtype=jnp.int32)
-        is_home = slab_ids == device
-        block_max = jnp.where(is_home[None, None, :], -1e30, block_max)
-        return (combine(state, block_max, block_num, block_den), None)
+    first_slab = (device // split) * split
+    query_slab = first_slab + jnp.arange(split * rows_here, dtype=jnp.int32) // rows_here
+    is_home = query_slab[:, None] == jnp.arange(slab_count, dtype=jnp.int32)[None, :]
+    block_max = jnp.where(is_home, home_max, block_max)
+    block_den = jnp.where(is_home, home_den, block_den)
+    block_num = jnp.where(is_home[..., None], home_num, block_num)
 
-    step_ids = jnp.arange(slab_count // per_step, dtype=jnp.int32)
-    result, unused = lax.scan(advance, start_state, (key_steps, value_steps, step_ids))
-    final_max, final_num, final_den = result
-    attended = (
-        jnp.transpose(final_num / final_den[..., None], (1, 0, 2))
-        .reshape(rows_here, inner)
-        .astype(jnp.bfloat16)
-    )
+    top = jnp.max(block_max, axis=-1)
+    factor = jnp.exp(block_max - top[:, None])
+    numer = jnp.sum(factor[..., None] * block_num, axis=1)
+    denom = jnp.sum(factor * block_den, axis=1)
+    result = (numer / denom[:, None]).astype(jnp.bfloat16)
+    result = result.reshape(split, rows_here, 1, HEAD_DIM)
+    attended = lax.all_to_all(result, "px", 0, 2, tiled=True).reshape(rows_here, inner)
     projected = lax.psum_scatter(
         jnp.dot(attended, w_out, preferred_element_type=jnp.float32).T,
         "chan",

time: 318 us -> 223 us (0.70)
  local copies, waits for them, and re-layouts: 75.6 us -> 14.7 us
  waiting for transfers between devices: 95.7 us -> 51 us
  blocking collectives: 92.8 us -> 121 us
  loops' own time: 10.3 us -> 0 us
  matrix products: 15.5 us -> 9.52 us
  other arithmetic: 12 us -> 8.26 us
  starting transfers between devices: 0.12 us -> 3.38 us
    all_gather x2 -> x1, waiting for transfers between devices: 49.8 us -> 0.02 us  [local(): stacked = lax.all_gather(stacked, name, axis=1, tiled=True)]
    dynamic_slice x48 -> x1, local copies, waits for them, and re-layouts: 40.8 us -> 0.1 us  [local(): lax.dynamic_slice_in_dim(stacked, own_head * HEAD_DIM, HEAD_DIM, axis=2)]
    another operation x4 -> x6, local copies, waits for them, and re-layouts: 26 us -> 0.33 us  [local(): jnp.stack([queries, fresh_keys, fresh_values])]
    all_gather x0 -> x1, blocking collectives: none -> 10.5 us  [local(): lax.all_gather(jnp.stack([stale_keys, stale_values]), 'px', axis=1, tiled...]
    another operation x1 -> x0, loops' own time: 10.3 us -> none  [local(): lax.scan(advance, start_state, (key_steps, value_steps, step_ids))]
    convert_element_type x0 -> x2, local copies, waits for them, and re-layouts: none -> 6.85 us  [the longest x1 6.84 us: local(): weight = jnp.exp(score - block_max[..., None]).astype(jnp.bfloat16)]
    all_to_all x0 -> x1, blocking collectives: none -> 6.69 us  [local(): lax.all_to_all(result, 'px', 0, 2, tiled=True).reshape(rows_here, inner)]
    all_gather x1, blocking collectives: 11.3 us -> 16.8 us  [local(): stacked = lax.all_gather(stacked, name, axis=1, tiled=True)]
  transfers between devices with their start and end apart: 3 -> 3, of which waited for: 3 -> 2; matrix products, arithmetic and copies ran while one was open for 3% -> 4% of each run, Pallas kernels for 0% -> 0%
where the time goes in v2:
time: 223 us; the launch traced here: 222 us
  blocking collectives  121 us (54%)
  waiting for transfers between devices  51 us (23%)
  between operations  15 us (7%)
  local copies, waits for them, and re-layouts  14.7 us (7%)
  matrix products  9.52 us (4%)
  other arithmetic  8.26 us (4%)
  starting transfers between devices  3.38 us (2%)
    psum x6, blocking collectives, patch_sum(): partial = lax.optimization_barrier(lax.psum(partial, name))  60.9 us
    unnamed x3, waiting for transfers between devices  46.6 us
    all_gather x1, blocking collectives, local(): shard_piece = lax.all_gather(normed, 'chan', axis=1, tiled=True)  25.7 us
    all_gather x1, blocking collectives, local(): stacked = lax.all_gather(stacked, name, axis=1, tiled=True)  16.8 us
    all_gather x1, blocking collectives, local(): lax.all_gather(jnp.stack([stale_keys, stale_values]), 'px', axis=1, tiled...  10.5 us
    convert_element_type x1, local copies, waits for them, and re-layouts, local(): weight = jnp.exp(score - block_max[..., None]).astype(jnp.bfloat16)  6.84 us
    all_to_all x1, blocking collectives, local(): lax.all_to_all(result, 'px', 0, 2, tiled=True).reshape(rows_here, inner)  6.69 us
  transfers between devices with their start and end apart: 3, of which 2 were waited for; matrix products, arithmetic and copies ran while one was open for 4% of the time, Pallas kernels for 0%

profile of v2, /device:TPU:1, one launch (start us, length us, event | category | flops | bytes accessed | tf_op | source)
XLA Modules:
  0.0 222.4 jit_solution(16611743712112252567)
XLA Ops:
  7.2 0.0 all-gather.3.cloned.1.call-start
  7.3 0.9 pad_maximum_fusion.1
  8.2 10.5 %all_gather.13 = bf16[2,256,256]{2,1,0:T(8,128)(2,1)S(1)} all-gather(bf16[2,64,256]{2,1,0:T(8,128)(2,1)S(1)} %pad_maximum_fusion.1), channel_id=1, replica_groups=mesh['py'=8,'pz'=4,'px'=4,'chan'=4] {'px'}, dimensions={1}, use_global_device_ids=true | all-gather | bytes 327680 | tf_op jit(solution)/shard_map/all_gather | solution.py:76
  18.7 0.1 constant_dynamic-slice_fusion
  18.8 16.8 %all_gather.14 = bf16[2,1024,64]{2,1,0:T(8,128)(2,1)} all-gather(bf16[2,256,64]{2,1,0:T(8,128)(2,1)S(1)} %constant_dynamic-slice_fusion), channel_id=1, replica_groups=mesh['py'=8,'pz'=4,'px'=4,'chan'=4] {'pz'}, dimensions={1}, use_global_device_ids=true | all-gather | bytes 327680 | tf_op jit(solution)/shard_map/all_gather | solution.py:79
  35.6 0.8 convert_reduce_fusion.1
  36.4 0.1 reduce_sum.71
  36.5 0.1 reduce_sum.72
  36.6 7.6 %psum.42 = f32[8]{0:T(128)S(1)} all-reduce(f32[8]{0:T(128)S(1)} %reduce_sum.72), channel_id=1, replica_groups=mesh['py'=8,'pz'=4,'px'=4,'chan'=4] {'px'}, use_global_device_ids=true, to_apply=%region_2.0 | all-reduce | flops 8 | bytes 64 | tf_op jit(solution)/shard_map/psum | solution.py:28
  44.2 10.3 %psum.43 = f32[8]{0:T(128)S(1)} all-reduce(f32[8]{0:T(128)S(1)} %psum.42), channel_id=1, replica_groups=mesh['py'=8,'pz'=4,'px'=4,'chan'=4] {'pz'}, use_global_device_ids=true, to_apply=%region_3.0 | all-reduce | flops 8 | bytes 64 | tf_op jit(solution)/shard_map/psum | solution.py:28
  54.6 15.5 %psum.44 = f32[8]{0:T(128)S(1)} all-reduce(f32[8]{0:T(128)S(1)} %psum.43), channel_id=1, replica_groups=mesh['py'=8,'pz'=4,'px'=4,'chan'=4] {'py'}, use_global_device_ids=true, to_apply=%region_4.0 | all-reduce | flops 8 | bytes 64 | tf_op jit(solution)/shard_map/psum | solution.py:28
  70.1 0.1 sub.54
  70.1 0.1 sub.55
  70.2 0.8 fusion.6
  71.1 0.1 reduce_sum.74
  71.1 0.1 reduce_sum.75
  71.3 6.8 %psum.45 = f32[8]{0:T(128)S(1)} all-reduce(f32[8]{0:T(128)S(1)} %reduce_sum.75), channel_id=1, replica_groups=mesh['py'=8,'pz'=4,'px'=4,'chan'=4] {'px'}, use_global_device_ids=true, to_apply=%region_7.0 | all-reduce | flops 8 | bytes 64 | tf_op jit(solution)/shard_map/psum | solution.py:28
  78.1 7.0 %psum.46 = f32[8]{0:T(128)S(1)} all-reduce(f32[8]{0:T(128)S(1)} %psum.45), channel_id=1, replica_groups=mesh['py'=8,'pz'=4,'px'=4,'chan'=4] {'pz'}, use_global_device_ids=true, to_apply=%region_8.9 | all-reduce | flops 8 | bytes 64 | tf_op jit(solution)/shard_map/psum | solution.py:28
  85.1 13.6 %psum.47 = f32[8]{0:T(128)S(1)} all-reduce(f32[8]{0:T(128)S(1)} %psum.46), channel_id=1, replica_groups=mesh['py'=8,'pz'=4,'px'=4,'chan'=4] {'py'}, use_global_device_ids=true, to_apply=%region_9.10 | all-reduce | flops 8 | bytes 64 | tf_op jit(solution)/shard_map/psum | solution.py:28
  99.4 0.1 divide_multiply_fusion
  99.5 0.1 mul.78
  99.6 0.1 mul.79
  99.7 1.2 convolution_reduce_fusion
  100.9 0.8 fusion.16
  101.7 25.7 %all-gather = bf16[4,320,64]{1,2,0:T(8,128)(2,1)S(1)} all-gather(bf16[1,320,64]{1,2,0:T(8,128)(2,1)S(1)} %fusion.16), channel_id=1, replica_groups=mesh['py'=8,'pz'=4,'px'=4,'chan'=4] {'chan'}, dimensions={0}, use_global_device_ids=true | all-gather | bytes 204800 | tf_op jit(solution)/shard_map/all_gather | solution.py:63
  127.4 0.2 copy.69
  127.6 0.2 reshape.168
  127.8 1.3 convolution_convert_fusion.2
  129.1 0.1 stack.21
  129.2 0.2 convolution_convert_fusion
  129.5 0.1 stack.23
  129.6 0.2 convolution_convert_fusion.1
  129.9 0.1 stack.22
  130.0 0.8 reshape.175
  130.9 3.3 %all-to-all-start = ((bf16[4,2,6144]{2,1,0:T(2,128)(2,1)}), bf16[4,2,6144]{2,1,0:T(2,128)(2,1)S(1)}, u32[]{:S(2)}, u32[]{:S(2)}) async-start(bf16[4,2,6144]{2,1,0:T(2,128)(2,1)} %reshape.175), calls=%async_computation | async-start | bytes 196608 | tf_op jit(solution)/shard_map/all_to_all | solution.py:87
  134.2 0.0 reduce-scatter.4.cloned.1.call-start
  134.3 0.1 iota_compare_fusion
  134.4 0.1 copy.78
  134.5 4.3 %all-to-all-done = bf16[4,2,6144]{2,1,0:T(2,128)(2,1)S(1)} async-done(((bf16[4,2,6144]{2,1,0:T(2,128)(2,1)}), bf16[4,2,6144]{2,1,0:T(2,128)(2,1)S(1)}, u32[]{:S(2)}, u32[]{:S(2)}) %all-to-all-start) | async-done | bytes 98336 | tf_op jit(solution)/shard_map/all_to_all | solution.py:87
  138.8 0.2 reshape.176
  139.1 0.2 fusion.22
  139.2 0.1 broadcast_in_dim.48
  139.4 0.1 broadcast_in_dim.53
  139.5 0.2 fusion.14
  139.7 0.1 copy.80
  139.8 0.0 all-gather.3.cloned.1.call-done
  139.8 2.5 %fusion.21 = (bf16[1,8192,64]{2,1,0:T(8,128)(2,1)S(1)}, bf16[1,8192,64]{2,1,0:T(8,128)(2,1)S(1)}) fusion(bf16[2,8192,64]{2,1,0:T(8,128)(2,1)} %all-gather.3.cloned.1.call-done), kind=kLoop, calls=%fused_computation.55 | loop fusion | bytes 4194304 | tf_op jit(solution)/shard_map/slice | solution.py:82
  142.3 2.2 multiply_reduce_fusion
  144.5 3.1 %convert_reduce_fusion = (f32[256,128]{1,0:T(8,128)S(1)}, bf16[256,128,64]{1,0,2:T(8,128)(2,1)}) fusion(f32[256,128]{1,0:T(8,128)S(1)} %get-tuple-element.11, f32[256,128,64]{1,0,2:T(8,128)S(1)} %get-tuple-element.12), kind=kLoop, calls=%fused_computation.3 | loop fusion | flops 10452992 | bytes 12845056 | tf_op jit(solution)/shard_map/reduce_sum | solution.py:97
  147.6 0.2 fusion.13
  147.8 0.3 multiply_reduce_fusion.1
  148.1 0.1 div.61
  148.2 0.1 copy.77
  148.3 6.8 %copy.83 = bf16[256,128,64]{0,2,1:T(8,128)(2,1)} copy(bf16[256,128,64]{1,0,2:T(8,128)(2,1)} %get-tuple-element.6) | data formatting | bytes 8388608 | tf_op jit(solution)/shard_map/convert_element_type | solution.py:95
  155.1 3.7 %fusion.1 = f32[256,64]{0,1:T(8,128)S(1)} fusion(f32[256,64]{0,1:T(8,128)S(1)} %copy.80, f32[256,128]{0,1:T(8,128)S(1)} %copy.77, pred[256,128]{0,1:T(8,128)(4,1)S(1)} %copy.78, bf16[128,64,64]{2,1,0:T(8,128)(2,1)S(1)} %bitcast.73, bf16[256,128,64]{0,2,1:T(8,128)(2,1)} %copy.83), kind=kOutput, calls=%fused_computation.2 | convolution fusion | flops 274710528 | bytes 5537792 | tf_op jit(solution)/shard_map/qsk,skd->qsd/dot_general | solution.py:96
  158.9 0.1 reduce_sum.77
  159.0 0.1 reshape.177
  159.2 6.7 %all_to_all.30 = bf16[4,2,2048]{2,1,0:T(2,128)(2,1)S(1)} all-to-all(bf16[4,2,2048]{2,1,0:T(2,128)(2,1)S(1)} %reshape.177), channel_id=1, replica_groups=mesh['py'=8,'pz'=4,'px'=4,'chan'=4] {'px'}, dimensions={0} | all-to-all | bytes 65536 | tf_op jit(solution)/shard_map/all_to_all | solution.py:124
  165.8 0.1 reshape.178
  166.0 0.3 convolution_bitcast_fusion
  166.2 1.1 copy.94
  167.3 46.6 %reduce-scatter.4.cloned.1.call-done = f32[320,64]{1,0:T(8,128)} async-done(((f32[1280,64]{1,0:T(8,128)}), f32[320,64]{1,0:T(8,128)}) %reduce-scatter.4.cloned.1.call-update) | async-done | bytes 81936
  213.9 1.0 copy.95
  215.0 0.6 fusion.11
  (28 shorter events, 0.3 us)
Async XLA Ops:
  7.2 158.8 %copy-start = (bf16[256,1280]{1,0:T(8,128)(2,1)S(1)}, bf16[256,1280]{1,0:T(8,128)(2,1)}, u32[]{:S(2)}) copy-start(bf16[256,1280]{1,0:T(8,128)(2,1)} %param.19) | copy-start | bytes 1966084
  7.2 122.0 %copy-start.2 = (bf16[1280,256]{1,0:T(8,128)(2,1)S(1)}, bf16[1280,256]{1,0:T(8,128)(2,1)}, u32[]{:S(2)}) copy-start(bf16[1280,256]{1,0:T(8,128)(2,1)} %param.18) | copy-start | bytes 1966084
  7.2 122.4 %copy-start.3 = (bf16[1280,256]{1,0:T(8,128)(2,1)S(1)}, bf16[1280,256]{1,0:T(8,128)(2,1)}, u32[]{:S(2)}) copy-start(bf16[1280,256]{1,0:T(8,128)(2,1)} %param.17) | copy-start | bytes 1966084
  7.2 132.6 %all-gather.3.cloned.1.call-start = ((), (), s32[]{:S(2)}) async-start(), calls=%async_computation.3 | async-start | bytes 4718592 | tf_op jit(solution)/shard_map/all_gather | solution.py:79
  129.5 12.8 %copy-start.4 = (bf16[64,256]{1,0:T(8,128)(2,1)}, bf16[64,256]{1,0:T(8,128)(2,1)S(1)}, u32[]{:S(2)}) copy-start(bf16[64,256]{1,0:T(8,128)(2,1)S(1)} %convolution_convert_fusion) | copy-start | bytes 98308
  129.9 12.5 %copy-start.5 = (bf16[64,256]{1,0:T(8,128)(2,1)}, bf16[64,256]{1,0:T(8,128)(2,1)S(1)}, u32[]{:S(2)}) copy-start(bf16[64,256]{1,0:T(8,128)(2,1)S(1)} %convolution_convert_fusion.1) | copy-start | bytes 98308
  130.9 7.9 %all-to-all-start = ((bf16[4,2,6144]{2,1,0:T(2,128)(2,1)}), bf16[4,2,6144]{2,1,0:T(2,128)(2,1)S(1)}, u32[]{:S(2)}, u32[]{:S(2)}) async-start(bf16[4,2,6144]{2,1,0:T(2,128)(2,1)} %reshape.175), calls=%async_computation | async-start | bytes 196608 | tf_op jit(solution)/shard_map/all_to_all | solution.py:87
  134.2 79.7 %reduce-scatter.4.cloned.1.call-start = ((), (), s32[]{:S(2)}) async-start(), calls=%async_computation.4 | async-start | bytes 819200
  155.1 59.8 %copy-start.1 = (bf16[64,320]{1,0:T(8,128)(2,1)S(1)}, bf16[64,320]{1,0:T(8,128)(2,1)}, u32[]{:S(2)}) copy-start(bf16[64,320]{1,0:T(8,128)(2,1)} %param.11) | copy-start | bytes 122884
Sparse Core Ops, SparseCore 0:
  35.7 64.3 all-gather.2
  167.4 46.4 reduce-scatter.3

commit v3 on v2

--- a/solution.py
+++ b/solution.py
@@ -49,12 +49,17 @@
     local_groups = GROUPS // chan_count
     width = D // GROUPS
     values = latent.astype(jnp.float32).reshape(rows_here, local_groups, width)
-    amount = rows_here * patch_count * width
-    group_total = patch_sum(jnp.sum(values, axis=(0, 2)))
-    group_mean = group_total / amount
+    here = rows_here * width
+    local_mean = jnp.sum(values, axis=(0, 2)) / here
+    local_spread = jnp.sum(jnp.square(values - local_mean[None, :, None]), axis=(0, 2))
+    gathered = jnp.stack([local_mean, local_spread])[None]
+    for name in reversed(PATCH_AXES):
+        gathered = lax.all_gather(gathered, name, axis=0, tiled=True)
+    group_mean = jnp.mean(gathered[:, 0], axis=0)
+    offset = gathered[:, 0] - group_mean[None, :]
+    spread = jnp.sum(gathered[:, 1], axis=0) + here * jnp.sum(offset * offset, axis=0)
+    variance = spread / (here * patch_count)
     centered = values - group_mean[None, :, None]
-    spread = patch_sum(jnp.sum(centered * centered, axis=(0, 2)))
-    variance = spread / amount
     scaled = (centered * lax.rsqrt(variance + 1e-05)[None, :, None]).reshape(rows_here, chan_width)
     normed = (scaled * norm_gain + norm_bias + timestep_shift(timestep, w_time)).astype(
         jnp.bfloat16
@@ -75,7 +80,7 @@
 
     stacked = lax.all_gather(jnp.stack([stale_keys, stale_values]), "px", axis=1, tiled=True)
     stacked = lax.dynamic_slice_in_dim(stacked, own_head * HEAD_DIM, HEAD_DIM, axis=2)
-    for name in reversed(PATCH_AXES[:-1]):
+    for name in PATCH_AXES[:-1]:
         stacked = lax.all_gather(stacked, name, axis=1, tiled=True)
     slab_count = stacked.shape[1] // rows_here
     stale_k = stacked[0].reshape(slab_count, rows_here, HEAD_DIM)
@@ -108,7 +113,7 @@
     home_num = home_num.reshape(split * rows_here, 1, HEAD_DIM)
     home_den = home_den.reshape(split * rows_here, 1)
 
-    first_slab = (device // split) * split
+    first_slab = (lax.axis_index("pz") * lax.axis_size("py") + lax.axis_index("py")) * split
     query_slab = first_slab + jnp.arange(split * rows_here, dtype=jnp.int32) // rows_here
     is_home = query_slab[:, None] == jnp.arange(slab_count, dtype=jnp.int32)[None, :]
     block_max = jnp.where(is_home, home_max, block_max)
@@ -122,12 +127,9 @@
     result = (numer / denom[:, None]).astype(jnp.bfloat16)
     result = result.reshape(split, rows_here, 1, HEAD_DIM)
     attended = lax.all_to_all(result, "px", 0, 2, tiled=True).reshape(rows_here, inner)
-    projected = lax.psum_scatter(
-        jnp.dot(attended, w_out, preferred_element_type=jnp.float32).T,
-        "chan",
-        scatter_dimension=0,
-        tiled=True,
-    ).T
+    attended = lax.all_gather(attended, "chan", axis=1, tiled=True)
+    out_columns = lax.all_to_all(w_out, "chan", 1, 0, tiled=True)
+    projected = jnp.dot(attended, out_columns, preferred_element_type=jnp.float32)
     mixed = (latent.astype(jnp.float32) + projected).astype(jnp.bfloat16)
     return (mixed, fresh_keys, fresh_values)
 

time: 223 us -> 205 us (0.919)
  the two profiles are of different devices: /device:TPU:1 before, /device:TPU:41 now
where the time goes in v3:
time: 205 us; the launch traced here: 204 us
  blocking collectives  118 us (58%)
  local copies, waits for them, and re-layouts  18.8 us (9%)
  starting transfers between devices  18.8 us (9%)
  between operations  15 us (7%)
  waiting for transfers between devices  13 us (6%)
  matrix products  10.6 us (5%)
  other arithmetic  9.95 us (5%)
    all_gather x3, blocking collectives, local(): gathered = lax.all_gather(gathered, name, axis=0, tiled=True)  39 us
    all_gather x1, blocking collectives, local(): shard_piece = lax.all_gather(normed, 'chan', axis=1, tiled=True)  31.2 us
    all_gather x1, blocking collectives, local(): stacked = lax.all_gather(stacked, name, axis=1, tiled=True)  22.4 us
    all_gather x1, blocking collectives, local(): attended = lax.all_gather(attended, 'chan', axis=1, tiled=True)  15.1 us
    all_gather x1, blocking collectives, local(): lax.all_gather(jnp.stack([stale_keys, stale_values]), 'px', axis=1, tiled...  10.1 us
    all_to_all x1, starting transfers between devices, local(): out_columns = lax.all_to_all(w_out, 'chan', 1, 0, tiled=True)  7.96 us
    all_to_all x1, starting transfers between devices, local(): lax.all_to_all(result, 'px', 0, 2, tiled=True).reshape(rows_here, inner)  7.46 us
    convert_element_type x1, local copies, waits for them, and re-layouts, local(): weight = jnp.exp(score - block_max[..., None]).astype(jnp.bfloat16)  6.8 us
  transfers between devices with their start and end apart: 4, of which 3 were waited for; matrix products, arithmetic and copies ran while one was open for 17% of the time, Pallas kernels for 0%

profile of v3, /device:TPU:41, one launch (start us, length us, event | category | flops | bytes accessed | tf_op | source)
XLA Modules:
  0.0 203.9 jit_solution(8617160732467280088)
XLA Ops:
  7.3 0.9 pad_maximum_fusion.1
  8.2 10.1 %all_gather.28 = bf16[2,256,256]{2,1,0:T(8,128)(2,1)S(1)} all-gather(bf16[2,64,256]{2,1,0:T(8,128)(2,1)S(1)} %pad_maximum_fusion.1), channel_id=1, replica_groups=mesh['py'=8,'pz'=4,'px'=4,'chan'=4] {'px'}, dimensions={1}, use_global_device_ids=true | all-gather | bytes 327680 | tf_op jit(solution)/shard_map/all_gather | solution.py:81
  18.3 0.1 constant_dynamic-slice_fusion
  18.4 22.4 %all_gather.29 = bf16[2,2048,64]{2,1,0:T(8,128)(2,1)} all-gather(bf16[2,256,64]{2,1,0:T(8,128)(2,1)S(1)} %constant_dynamic-slice_fusion), channel_id=1, replica_groups=mesh['py'=8,'pz'=4,'px'=4,'chan'=4] {'py'}, dimensions={1}, use_global_device_ids=true | all-gather | bytes 589824 | tf_op jit(solution)/shard_map/all_gather | solution.py:84
  40.8 0.8 convert_reduce_fusion.1
  41.7 0.1 reduce_sum.98
  41.7 0.1 reduce_sum.99
  41.9 0.1 sub.69
  41.9 0.1 sub.70
  42.0 0.8 fusion.6
  42.9 0.1 reduce_sum.101
  43.0 0.1 reduce_sum.102
  43.1 7.3 %all-gather.1 = f32[4,2,8]{2,1,0:T(2,128)S(1)} all-gather(f32[1,2,8]{2,1,0:T(2,128)S(1)} %maximum_bitcast_fusion), channel_id=2, replica_groups=mesh['py'=8,'pz'=4,'px'=4,'chan'=4] {'px'}, dimensions={0}, use_global_device_ids=true | all-gather | bytes 320 | tf_op jit(solution)/shard_map/all_gather | solution.py:57
  50.4 12.8 %all_gather.25 = f32[16,2,8]{2,1,0:T(2,128)S(1)} all-gather(f32[4,2,8]{2,1,0:T(2,128)S(1)} %all-gather.1), channel_id=1, replica_groups=mesh['py'=8,'pz'=4,'px'=4,'chan'=4] {'pz'}, dimensions={0}, use_global_device_ids=true | all-gather | bytes 1280 | tf_op jit(solution)/shard_map/all_gather | solution.py:57
  63.2 18.9 %all_gather.26 = f32[128,2,8]{2,1,0:T(2,128)S(1)} all-gather(f32[16,2,8]{2,1,0:T(2,128)S(1)} %all_gather.25), channel_id=1, replica_groups=mesh['py'=8,'pz'=4,'px'=4,'chan'=4] {'py'}, dimensions={0}, use_global_device_ids=true | all-gather | bytes 9216 | tf_op jit(solution)/shard_map/all_gather | solution.py:57
  82.1 0.2 slice_reduce_fusion.1
  82.3 0.1 mul.81
  82.4 0.1 mul.82
  82.5 0.1 sub.74
  83.3 0.1 divide_multiply_fusion
  83.4 1.2 convolution_reduce_fusion
  84.6 0.8 fusion.16
  85.5 31.2 %all-gather.2 = bf16[4,320,64]{1,2,0:T(8,128)(2,1)S(1)} all-gather(bf16[1,320,64]{1,2,0:T(8,128)(2,1)S(1)} %fusion.16), channel_id=1, replica_groups=mesh['py'=8,'pz'=4,'px'=4,'chan'=4] {'chan'}, dimensions={0}, use_global_device_ids=true | all-gather | bytes 204800 | tf_op jit(solution)/shard_map/all_gather | solution.py:68
  116.6 0.2 copy.75
  116.8 0.2 reshape.199
  117.0 0.2 convolution_convert_fusion.1
  117.2 0.6 copy-done.5
  117.8 0.1 stack.31
  118.0 0.2 convolution_convert_fusion
  118.2 0.6 copy-done.6
  118.8 0.1 stack.32
  119.0 0.2 convolution_convert_fusion.2
  119.2 0.1 stack.30
  119.4 0.8 reshape.205
  120.2 3.3 %all-to-all-start = ((bf16[4,2,6144]{2,1,0:T(2,128)(2,1)}), bf16[4,2,6144]{2,1,0:T(2,128)(2,1)S(1)}, u32[]{:S(2)}, u32[]{:S(2)}) async-start(bf16[4,2,6144]{2,1,0:T(2,128)(2,1)} %reshape.205), calls=%async_computation | async-start | bytes 196608 | tf_op jit(solution)/shard_map/all_to_all | solution.py:92
  123.6 0.1 iota_compare_fusion
  123.7 0.7 copy.84
  124.4 1.1 copy.92
  125.5 3.0 %all-to-all-done = bf16[4,2,6144]{2,1,0:T(2,128)(2,1)S(1)} async-done(((bf16[4,2,6144]{2,1,0:T(2,128)(2,1)}), bf16[4,2,6144]{2,1,0:T(2,128)(2,1)S(1)}, u32[]{:S(2)}, u32[]{:S(2)}) %all-to-all-start) | async-done | bytes 98336 | tf_op jit(solution)/shard_map/all_to_all | solution.py:92
  128.5 8.0 %all-to-all-start.2 = ((bf16[256,4,320]{0,2,1:T(8,128)(2,1)}), bf16[256,4,320]{0,2,1:T(8,128)(2,1)S(1)}, u32[]{:S(2)}, u32[]{:S(2)}) async-start(bf16[256,4,320]{0,2,1:T(8,128)(2,1)} %bitcast.24), calls=%async_computation.2 | async-start | bytes 1310720 | tf_op jit(solution)/shard_map/all_to_all | solution.py:131
  136.5 0.2 reshape.206
  136.7 0.2 fusion.23
  136.9 0.1 broadcast_in_dim.54
  137.0 0.1 broadcast_in_dim.59
  137.1 0.2 fusion.14
  137.3 0.7 copy.86
  138.0 5.8 %all-gather.5.cloned.1.call-done = bf16[2,8192,64]{2,1,0:T(8,128)(2,1)} async-done(((bf16[2,2048,64]{2,1,0:T(8,128)(2,1)}), bf16[2,8192,64]{2,1,0:T(8,128)(2,1)}) %all-gather.5.cloned.1.call-update) | async-done | bytes 2097168 | tf_op jit(solution)/shard_map/all_gather | solution.py:84
  143.8 2.5 %fusion.22 = (bf16[1,8192,64]{2,1,0:T(8,128)(2,1)S(1)}, bf16[1,8192,64]{2,1,0:T(8,128)(2,1)S(1)}) fusion(bf16[2,8192,64]{2,1,0:T(8,128)(2,1)} %all-gather.5.cloned.1.call-done), kind=kLoop, calls=%fused_computation.61 | loop fusion | bytes 4194304 | tf_op jit(solution)/shard_map/slice | solution.py:87
  146.4 2.2 %multiply_reduce_fusion = (f32[256,128]{1,0:T(8,128)S(1)}, f32[256,128,64]{1,0,2:T(8,128)S(1)}) fusion(bf16[256,64,1]{1,0,2:T(8,128)(2,1)S(1)} %bitcast.81, bf16[128,64,64]{2,1,0:T(8,128)(2,1)S(1)} %bitcast.77), kind=kOutput, calls=%fused_computation.5 | convolution fusion | flops 272596992 | bytes 9601024 | tf_op jit(solution)/shard_map/qd,skd->qsk/dot_general | solution.py:96
  148.5 3.7 %convert_reduce_fusion = (f32[256,128]{1,0:T(8,128)}, bf16[256,128,64]{1,0,2:T(8,128)(2,1)}) fusion(f32[256,128]{1,0:T(8,128)S(1)} %get-tuple-element.16, f32[256,128,64]{1,0,2:T(8,128)S(1)} %get-tuple-element.17), kind=kLoop, calls=%fused_computation.3 | loop fusion | flops 10452992 | bytes 12845056 | tf_op jit(solution)/shard_map/reduce_sum | solution.py:102
  152.2 6.8 %copy.89 = bf16[256,128,64]{0,2,1:T(8,128)(2,1)} copy(bf16[256,128,64]{1,0,2:T(8,128)(2,1)} %get-tuple-element.8) | data formatting | bytes 8388608 | tf_op jit(solution)/shard_map/convert_element_type | solution.py:100
  159.0 0.2 fusion.13
  159.3 1.8 multiply_reduce_fusion.1
  161.0 1.0 copy.83
  162.0 4.4 %fusion.1 = f32[256,64]{0,1:T(8,128)} fusion(f32[256,64]{0,1:T(8,128)} %copy.86, f32[256,128]{0,1:T(8,128)S(1)} %copy.83, pred[256,128]{0,1:T(8,128)(4,1)} %copy.84, bf16[128,64,64]{2,1,0:T(8,128)(2,1)S(1)} %bitcast.80, bf16[256,128,64]{0,2,1:T(8,128)(2,1)} %copy.89), kind=kOutput, calls=%fused_computation.2 | convolution fusion | flops 274710528 | bytes 5537792 | tf_op jit(solution)/shard_map/qsk,skd->qsd/dot_general | solution.py:101
  166.4 0.9 reduce_sum.107
  167.3 0.1 div.57
  167.5 0.7 reshape.207
  168.2 7.5 %all-to-all-start.1 = ((bf16[4,2,2048]{2,1,0:T(2,128)(2,1)}), bf16[4,2,2048]{2,1,0:T(2,128)(2,1)S(1)}, u32[]{:S(2)}, u32[]{:S(2)}) async-start(bf16[4,2,2048]{2,1,0:T(2,128)(2,1)} %reshape.207), calls=%async_computation.1 | async-start | bytes 65536 | tf_op jit(solution)/shard_map/all_to_all | solution.py:129
  175.8 4.2 %all-to-all-done.1 = bf16[4,2,2048]{2,1,0:T(2,128)(2,1)S(1)} async-done(((bf16[4,2,2048]{2,1,0:T(2,128)(2,1)}), bf16[4,2,2048]{2,1,0:T(2,128)(2,1)S(1)}, u32[]{:S(2)}, u32[]{:S(2)}) %all-to-all-start.1) | async-done | bytes 32800 | tf_op jit(solution)/shard_map/all_to_all | solution.py:129
  180.0 0.1 reshape.208
  180.1 0.1 copy.101
  180.2 15.1 %all_gather.31 = bf16[64,1024]{1,0:T(8,128)(2,1)S(1)} all-gather(bf16[64,256]{1,0:T(8,128)(2,1)S(1)} %copy.101), channel_id=1, replica_groups=mesh['py'=8,'pz'=4,'px'=4,'chan'=4] {'chan'}, dimensions={1}, use_global_device_ids=true | all-gather | bytes 163840 | tf_op jit(solution)/shard_map/all_gather | solution.py:130
  195.3 1.8 fusion.4
  (35 shorter events, 0.6 us)
Async XLA Ops:
  7.2 109.8 %copy-start = (bf16[1280,256]{1,0:T(8,128)(2,1)S(1)}, bf16[1280,256]{1,0:T(8,128)(2,1)}, u32[]{:S(2)}) copy-start(bf16[1280,256]{1,0:T(8,128)(2,1)} %param.17) | copy-start | bytes 1966084
  7.2 110.8 %copy-start.3 = (bf16[1280,256]{1,0:T(8,128)(2,1)S(1)}, bf16[1280,256]{1,0:T(8,128)(2,1)}, u32[]{:S(2)}) copy-start(bf16[1280,256]{1,0:T(8,128)(2,1)} %param.18) | copy-start | bytes 1966084
  7.2 111.8 %copy-start.4 = (bf16[1280,256]{1,0:T(8,128)(2,1)S(1)}, bf16[1280,256]{1,0:T(8,128)(2,1)}, u32[]{:S(2)}) copy-start(bf16[1280,256]{1,0:T(8,128)(2,1)} %param.16) | copy-start | bytes 1966084
  7.2 136.6 %all-gather.5.cloned.1.call-start = ((), (), s32[]{:S(2)}) async-start(), calls=%async_computation.3 | async-start | bytes 5242880 | tf_op jit(solution)/shard_map/all_gather | solution.py:84
  18.4 106.0 %copy-start.2 = (bf16[256,1280]{1,0:T(8,128)(2,1)S(1)}, bf16[256,1280]{1,0:T(8,128)(2,1)}, u32[]{:S(2)}) copy-start(bf16[256,1280]{1,0:T(8,128)(2,1)} %param.19) | copy-start | bytes 1966084
  117.2 0.6 copy-start.5
  118.2 0.6 copy-start.6
  120.2 8.3 %all-to-all-start = ((bf16[4,2,6144]{2,1,0:T(2,128)(2,1)}), bf16[4,2,6144]{2,1,0:T(2,128)(2,1)S(1)}, u32[]{:S(2)}, u32[]{:S(2)}) async-start(bf16[4,2,6144]{2,1,0:T(2,128)(2,1)} %reshape.205), calls=%async_computation | async-start | bytes 196608 | tf_op jit(solution)/shard_map/all_to_all | solution.py:92
  128.5 39.7 %all-to-all-start.2 = ((bf16[256,4,320]{0,2,1:T(8,128)(2,1)}), bf16[256,4,320]{0,2,1:T(8,128)(2,1)S(1)}, u32[]{:S(2)}, u32[]{:S(2)}) async-start(bf16[256,4,320]{0,2,1:T(8,128)(2,1)} %bitcast.24), calls=%async_computation.2 | async-start | bytes 1310720 | tf_op jit(solution)/shard_map/all_to_all | solution.py:131
  136.7 1.3 copy-start.1
  143.8 2.5 %slice-start = ((bf16[3,4,64,1,64]{4,2,1,3,0:T(8,128)(2,1)}), bf16[1,4,64,1,64]{4,2,1,3,0:T(8,128)(2,1)S(1)}, s32[]{:S(2)}) async-start(bf16[3,4,64,1,64]{4,2,1,3,0:T(8,128)(2,1)} %copy-done.1), calls=%async_computation.4 | async-start | bytes 131072 | tf_op jit(solution)/shard_map/slice | solution.py:105
  168.2 11.8 %all-to-all-start.1 = ((bf16[4,2,2048]{2,1,0:T(2,128)(2,1)}), bf16[4,2,2048]{2,1,0:T(2,128)(2,1)S(1)}, u32[]{:S(2)}, u32[]{:S(2)}) async-start(bf16[4,2,2048]{2,1,0:T(2,128)(2,1)} %reshape.207), calls=%async_computation.1 | async-start | bytes 65536 | tf_op jit(solution)/shard_map/all_to_all | solution.py:129
Sparse Core Ops, SparseCore 0:
  41.0 102.8 all-gather.4

commit v4 on v3

--- a/solution.py
+++ b/solution.py
@@ -80,8 +80,7 @@
 
     stacked = lax.all_gather(jnp.stack([stale_keys, stale_values]), "px", axis=1, tiled=True)
     stacked = lax.dynamic_slice_in_dim(stacked, own_head * HEAD_DIM, HEAD_DIM, axis=2)
-    for name in PATCH_AXES[:-1]:
-        stacked = lax.all_gather(stacked, name, axis=1, tiled=True)
+    stacked = lax.all_gather(stacked, PATCH_AXES[:-1], axis=1, tiled=True)
     slab_count = stacked.shape[1] // rows_here
     stale_k = stacked[0].reshape(slab_count, rows_here, HEAD_DIM)
     stale_v = stacked[1].reshape(slab_count, rows_here, HEAD_DIM)
@@ -113,7 +112,7 @@
     home_num = home_num.reshape(split * rows_here, 1, HEAD_DIM)
     home_den = home_den.reshape(split * rows_here, 1)
 
-    first_slab = (lax.axis_index("pz") * lax.axis_size("py") + lax.axis_index("py")) * split
+    first_slab = (device // split) * split
     query_slab = first_slab + jnp.arange(split * rows_here, dtype=jnp.int32) // rows_here
     is_home = query_slab[:, None] == jnp.arange(slab_count, dtype=jnp.int32)[None, :]
     block_max = jnp.where(is_home, home_max, block_max)
@@ -125,9 +124,11 @@
     numer = jnp.sum(factor[..., None] * block_num, axis=1)
     denom = jnp.sum(factor * block_den, axis=1)
     result = (numer / denom[:, None]).astype(jnp.bfloat16)
-    result = result.reshape(split, rows_here, 1, HEAD_DIM)
-    attended = lax.all_to_all(result, "px", 0, 2, tiled=True).reshape(rows_here, inner)
-    attended = lax.all_gather(attended, "chan", axis=1, tiled=True)
+    result = result.reshape(1, split, rows_here, HEAD_DIM)
+    result = jnp.broadcast_to(result, (chan_count, split, rows_here, HEAD_DIM))
+    result = result.reshape(chan_count * split, rows_here, HEAD_DIM)
+    attended = lax.all_to_all(result, ("chan", "px"), 0, 0, tiled=True)
+    attended = jnp.transpose(attended, (1, 0, 2)).reshape(rows_here, chan_count * inner)
     out_columns = lax.all_to_all(w_out, "chan", 1, 0, tiled=True)
     projected = jnp.dot(attended, out_columns, preferred_element_type=jnp.float32)
     mixed = (latent.astype(jnp.float32) + projected).astype(jnp.bfloat16)

time: 205 us -> 245 us (1.20)
  the two profiles are of different devices: /device:TPU:41 before, /device:TPU:1 now
where the time goes in v4:
time: 245 us; the launch traced here: 244 us
  blocking collectives  78.9 us (32%)
  waiting for transfers between devices  72.3 us (30%)
  starting transfers between devices  36.4 us (15%)
  local copies, waits for them, and re-layouts  20.1 us (8%)
  between operations  15 us (6%)
  matrix products  11.7 us (5%)
  other arithmetic  9.95 us (4%)
    all_gather x1, waiting for transfers between devices, local(): stacked = lax.all_gather(stacked, PATCH_AXES[:-1], axis=1, tiled=True)  59.3 us
    all_gather x3, blocking collectives, local(): gathered = lax.all_gather(gathered, name, axis=0, tiled=True)  42.3 us
    all_to_all x1, starting transfers between devices, local(): attended = lax.all_to_all(result, ('chan', 'px'), 0, 0, tiled=True)  27.1 us
    all_gather x1, blocking collectives, local(): shard_piece = lax.all_gather(normed, 'chan', axis=1, tiled=True)  26.2 us
    all_gather x1, blocking collectives, local(): lax.all_gather(jnp.stack([stale_keys, stale_values]), 'px', axis=1, tiled...  10.5 us
    all_to_all x1, waiting for transfers between devices, local(): attended = lax.all_to_all(result, ('chan', 'px'), 0, 0, tiled=True)  9.88 us
    convert_element_type x1, local copies, waits for them, and re-layouts, local(): weight = jnp.exp(score - block_max[..., None]).astype(jnp.bfloat16)  6.8 us
    all_to_all x1, starting transfers between devices, local(): out_columns = lax.all_to_all(w_out, 'chan', 1, 0, tiled=True)  5.94 us
  transfers between devices with their start and end apart: 4, of which 3 were waited for; matrix products, arithmetic and copies ran while one was open for 15% of the time, Pallas kernels for 0%

profile of v4, /device:TPU:1, one launch (start us, length us, event | category | flops | bytes accessed | tf_op | source)
XLA Modules:
  0.0 244.4 jit_solution(10345975317338812675)
XLA Ops:
  7.3 0.9 pad_maximum_fusion.1
  8.2 10.5 %all_gather.22 = bf16[2,256,256]{2,1,0:T(8,128)(2,1)S(1)} all-gather(bf16[2,64,256]{2,1,0:T(8,128)(2,1)S(1)} %pad_maximum_fusion.1), channel_id=1, replica_groups=mesh['py'=8,'pz'=4,'px'=4,'chan'=4] {'px'}, dimensions={1}, use_global_device_ids=true | all-gather | bytes 327680 | tf_op jit(solution)/shard_map/all_gather | solution.py:81
  18.7 0.8 constant_dynamic-slice_fusion
  19.5 0.8 convert_reduce_fusion.1
  20.3 0.1 reduce_sum.98
  20.4 0.1 reduce_sum.99
  20.5 0.1 sub.74
  20.6 0.1 sub.75
  20.7 0.8 fusion.6
  21.5 0.1 reduce_sum.101
  21.6 0.1 reduce_sum.102
  21.7 7.4 %all-gather.1 = f32[4,2,8]{2,1,0:T(2,128)S(1)} all-gather(f32[1,2,8]{2,1,0:T(2,128)S(1)} %maximum_bitcast_fusion), channel_id=2, replica_groups=mesh['py'=8,'pz'=4,'px'=4,'chan'=4] {'px'}, dimensions={0}, use_global_device_ids=true | all-gather | bytes 320 | tf_op jit(solution)/shard_map/all_gather | solution.py:57
  29.1 12.8 %all_gather.19 = f32[16,2,8]{2,1,0:T(2,128)S(1)} all-gather(f32[4,2,8]{2,1,0:T(2,128)S(1)} %all-gather.1), channel_id=1, replica_groups=mesh['py'=8,'pz'=4,'px'=4,'chan'=4] {'pz'}, dimensions={0}, use_global_device_ids=true | all-gather | bytes 1280 | tf_op jit(solution)/shard_map/all_gather | solution.py:57
  41.8 22.1 %all_gather.20 = f32[128,2,8]{2,1,0:T(2,128)S(1)} all-gather(f32[16,2,8]{2,1,0:T(2,128)S(1)} %all_gather.19), channel_id=1, replica_groups=mesh['py'=8,'pz'=4,'px'=4,'chan'=4] {'py'}, dimensions={0}, use_global_device_ids=true | all-gather | bytes 9216 | tf_op jit(solution)/shard_map/all_gather | solution.py:57
  64.0 0.2 slice_reduce_fusion.1
  64.2 0.1 mul.85
  64.3 0.1 mul.86
  64.4 0.1 sub.79
  65.2 0.1 divide_multiply_fusion
  65.3 1.2 convolution_reduce_fusion
  66.5 0.8 fusion.16
  67.4 26.2 %all-gather.2 = bf16[4,320,64]{1,2,0:T(8,128)(2,1)S(1)} all-gather(bf16[1,320,64]{1,2,0:T(8,128)(2,1)S(1)} %fusion.16), channel_id=1, replica_groups=mesh['py'=8,'pz'=4,'px'=4,'chan'=4] {'chan'}, dimensions={0}, use_global_device_ids=true | all-gather | bytes 204800 | tf_op jit(solution)/shard_map/all_gather | solution.py:68
  93.5 0.2 copy.75
  93.7 0.2 reshape.195
  93.9 0.2 convolution_convert_fusion.1
  94.1 0.6 copy-done.4
  94.7 0.1 stack.31
  94.8 1.3 convolution_convert_fusion
  96.2 0.6 copy-done.5
  96.8 0.1 stack.32
  96.9 0.2 convolution_convert_fusion.2
  97.2 0.1 stack.30
  97.4 0.9 reshape.201
  98.2 3.3 %all-to-all-start = ((bf16[4,2,6144]{2,1,0:T(2,128)(2,1)}), bf16[4,2,6144]{2,1,0:T(2,128)(2,1)S(1)}, u32[]{:S(2)}, u32[]{:S(2)}) async-start(bf16[4,2,6144]{2,1,0:T(2,128)(2,1)} %reshape.201), calls=%async_computation | async-start | bytes 196608 | tf_op jit(solution)/shard_map/all_to_all | solution.py:91
  101.6 0.1 iota_compare_fusion
  101.7 0.7 copy.84
  102.4 1.1 copy.92
  103.5 3.0 %all-to-all-done = bf16[4,2,6144]{2,1,0:T(2,128)(2,1)S(1)} async-done(((bf16[4,2,6144]{2,1,0:T(2,128)(2,1)}), bf16[4,2,6144]{2,1,0:T(2,128)(2,1)S(1)}, u32[]{:S(2)}, u32[]{:S(2)}) %all-to-all-start) | async-done | bytes 98336 | tf_op jit(solution)/shard_map/all_to_all | solution.py:91
  106.5 5.9 %all-to-all-start.2 = ((bf16[256,4,320]{0,2,1:T(8,128)(2,1)}), bf16[256,4,320]{0,2,1:T(8,128)(2,1)S(1)}, u32[]{:S(2)}, u32[]{:S(2)}) async-start(bf16[256,4,320]{0,2,1:T(8,128)(2,1)} %bitcast.23), calls=%async_computation.2 | async-start | bytes 1310720 | tf_op jit(solution)/shard_map/all_to_all | solution.py:132
  112.5 0.2 reshape.202
  112.7 0.2 fusion.23
  112.9 0.1 broadcast_in_dim.59
  113.0 0.1 broadcast_in_dim.64
  113.1 0.2 fusion.14
  113.3 0.7 copy.86
  114.0 59.3 %all-gather.5.cloned.1.call-done = bf16[2,8192,64]{2,1,0:T(8,128)(2,1)} async-done(((bf16[2,256,64]{2,1,0:T(8,128)(2,1)}), bf16[2,8192,64]{2,1,0:T(8,128)(2,1)}) %all-gather.5.cloned.1.call-update) | async-done | bytes 2097168 | tf_op jit(solution)/shard_map/all_gather | solution.py:83
  173.4 2.5 %fusion.22 = (bf16[1,8192,64]{2,1,0:T(8,128)(2,1)S(1)}, bf16[1,8192,64]{2,1,0:T(8,128)(2,1)S(1)}) fusion(bf16[2,8192,64]{2,1,0:T(8,128)(2,1)} %all-gather.5.cloned.1.call-done), kind=kLoop, calls=%fused_computation.61 | loop fusion | bytes 4194304 | tf_op jit(solution)/shard_map/slice | solution.py:86
  175.9 2.2 multiply_reduce_fusion
  178.1 3.7 %convert_reduce_fusion = (f32[256,128]{1,0:T(8,128)}, bf16[256,128,64]{1,0,2:T(8,128)(2,1)}) fusion(f32[256,128]{1,0:T(8,128)S(1)} %get-tuple-element.16, f32[256,128,64]{1,0,2:T(8,128)S(1)} %get-tuple-element.17), kind=kLoop, calls=%fused_computation.3 | loop fusion | flops 10452992 | bytes 12845056 | tf_op jit(solution)/shard_map/reduce_sum | solution.py:101
  181.8 6.8 %copy.89 = bf16[256,128,64]{0,2,1:T(8,128)(2,1)} copy(bf16[256,128,64]{1,0,2:T(8,128)(2,1)} %get-tuple-element.8) | data formatting | bytes 8388608 | tf_op jit(solution)/shard_map/convert_element_type | solution.py:99
  188.6 0.2 fusion.13
  188.8 1.8 multiply_reduce_fusion.1
  190.6 1.0 copy.83
  191.6 4.4 %fusion.1 = f32[256,64]{0,1:T(8,128)} fusion(f32[256,64]{0,1:T(8,128)} %copy.86, f32[256,128]{0,1:T(8,128)S(1)} %copy.83, pred[256,128]{0,1:T(8,128)(4,1)} %copy.84, bf16[128,64,64]{2,1,0:T(8,128)(2,1)S(1)} %bitcast.73, bf16[256,128,64]{0,2,1:T(8,128)(2,1)} %copy.89), kind=kOutput, calls=%fused_computation.2 | convolution fusion | flops 274710528 | bytes 5537792 | tf_op jit(solution)/shard_map/qsk,skd->qsd/dot_general | solution.py:100
  196.0 0.9 reduce_sum.107
  196.9 0.1 div.65
  197.0 0.1 copy.90
  197.2 0.9 reshape.203
  198.1 27.1 %all-to-all-start.1 = ((bf16[16,2,2048]{2,1,0:T(2,128)(2,1)}), bf16[16,2,2048]{2,1,0:T(2,128)(2,1)S(1)}, u32[]{:S(2)}, u32[]{:S(2)}) async-start(bf16[16,2,2048]{2,1,0:T(2,128)(2,1)} %reshape.203), calls=%async_computation.1 | async-start | bytes 262144 | tf_op jit(solution)/shard_map/all_to_all | solution.py:130
  225.3 9.9 %all-to-all-done.1 = bf16[16,2,2048]{2,1,0:T(2,128)(2,1)S(1)} async-done(((bf16[16,2,2048]{2,1,0:T(2,128)(2,1)}), bf16[16,2,2048]{2,1,0:T(2,128)(2,1)S(1)}, u32[]{:S(2)}, u32[]{:S(2)}) %all-to-all-start.1) | async-done | bytes 131104 | tf_op jit(solution)/shard_map/all_to_all | solution.py:130
  235.2 0.2 reshape.204
  235.4 0.2 copy.91
  235.6 0.2 reshape.190
  235.8 1.8 fusion.4
  (33 shorter events, 0.6 us)
Async XLA Ops:
  7.2 86.7 %copy-start = (bf16[1280,256]{1,0:T(8,128)(2,1)S(1)}, bf16[1280,256]{1,0:T(8,128)(2,1)}, u32[]{:S(2)}) copy-start(bf16[1280,256]{1,0:T(8,128)(2,1)} %param.17) | copy-start | bytes 1966084
  7.2 89.7 %copy-start.3 = (bf16[1280,256]{1,0:T(8,128)(2,1)S(1)}, bf16[1280,256]{1,0:T(8,128)(2,1)}, u32[]{:S(2)}) copy-start(bf16[1280,256]{1,0:T(8,128)(2,1)} %param.16) | copy-start | bytes 1966084
  7.2 95.2 %copy-start.2 = (bf16[256,1280]{1,0:T(8,128)(2,1)S(1)}, bf16[256,1280]{1,0:T(8,128)(2,1)}, u32[]{:S(2)}) copy-start(bf16[256,1280]{1,0:T(8,128)(2,1)} %param.19) | copy-start | bytes 1966084
  7.2 166.2 %all-gather.5.cloned.1.call-start = ((), (), s32[]{:S(2)}) async-start(), calls=%async_computation.3 | async-start | bytes 4325376 | tf_op jit(solution)/shard_map/all_gather | solution.py:83
  94.1 0.6 copy-start.4
  96.2 0.6 copy-start.5
  98.2 8.3 %all-to-all-start = ((bf16[4,2,6144]{2,1,0:T(2,128)(2,1)}), bf16[4,2,6144]{2,1,0:T(2,128)(2,1)S(1)}, u32[]{:S(2)}, u32[]{:S(2)}) async-start(bf16[4,2,6144]{2,1,0:T(2,128)(2,1)} %reshape.201), calls=%async_computation | async-start | bytes 196608 | tf_op jit(solution)/shard_map/all_to_all | solution.py:91
  106.5 91.5 %all-to-all-start.2 = ((bf16[256,4,320]{0,2,1:T(8,128)(2,1)}), bf16[256,4,320]{0,2,1:T(8,128)(2,1)S(1)}, u32[]{:S(2)}, u32[]{:S(2)}) async-start(bf16[256,4,320]{0,2,1:T(8,128)(2,1)} %bitcast.23), calls=%async_computation.2 | async-start | bytes 1310720 | tf_op jit(solution)/shard_map/all_to_all | solution.py:132
  112.7 1.3 copy-start.1
  173.4 2.5 %slice-start = ((bf16[3,4,64,1,64]{4,2,1,3,0:T(8,128)(2,1)}), bf16[1,4,64,1,64]{4,2,1,3,0:T(8,128)(2,1)S(1)}, s32[]{:S(2)}) async-start(bf16[3,4,64,1,64]{4,2,1,3,0:T(8,128)(2,1)} %copy-done.1), calls=%async_computation.4 | async-start | bytes 131072 | tf_op jit(solution)/shard_map/slice | solution.py:104
  198.1 37.1 %all-to-all-start.1 = ((bf16[16,2,2048]{2,1,0:T(2,128)(2,1)}), bf16[16,2,2048]{2,1,0:T(2,128)(2,1)S(1)}, u32[]{:S(2)}, u32[]{:S(2)}) async-start(bf16[16,2,2048]{2,1,0:T(2,128)(2,1)} %reshape.203), calls=%async_computation.1 | async-start | bytes 262144 | tf_op jit(solution)/shard_map/all_to_all | solution.py:130
Sparse Core Ops, SparseCore 0:
  19.6 153.7 all-gather.4

commit v5 on v4

--- a/solution.py
+++ b/solution.py
@@ -49,16 +49,16 @@
     local_groups = GROUPS // chan_count
     width = D // GROUPS
     values = latent.astype(jnp.float32).reshape(rows_here, local_groups, width)
-    here = rows_here * width
-    local_mean = jnp.sum(values, axis=(0, 2)) / here
-    local_spread = jnp.sum(jnp.square(values - local_mean[None, :, None]), axis=(0, 2))
-    gathered = jnp.stack([local_mean, local_spread])[None]
+    count = rows_here * width
+    group_mean = jnp.sum(values, axis=(0, 2)) / count
+    spread = jnp.sum(jnp.square(values - group_mean[None, :, None]), axis=(0, 2))
     for name in reversed(PATCH_AXES):
-        gathered = lax.all_gather(gathered, name, axis=0, tiled=True)
-    group_mean = jnp.mean(gathered[:, 0], axis=0)
-    offset = gathered[:, 0] - group_mean[None, :]
-    spread = jnp.sum(gathered[:, 1], axis=0) + here * jnp.sum(offset * offset, axis=0)
-    variance = spread / (here * patch_count)
+        gathered = lax.all_gather(jnp.stack([group_mean, spread]), name)
+        group_mean = jnp.mean(gathered[:, 0], axis=0)
+        offset = gathered[:, 0] - group_mean[None, :]
+        spread = jnp.sum(gathered[:, 1], axis=0) + count * jnp.sum(offset * offset, axis=0)
+        count = count * gathered.shape[0]
+    variance = spread / count
     centered = values - group_mean[None, :, None]
     scaled = (centered * lax.rsqrt(variance + 1e-05)[None, :, None]).reshape(rows_here, chan_width)
     normed = (scaled * norm_gain + norm_bias + timestep_shift(timestep, w_time)).astype(
@@ -80,7 +80,8 @@
 
     stacked = lax.all_gather(jnp.stack([stale_keys, stale_values]), "px", axis=1, tiled=True)
     stacked = lax.dynamic_slice_in_dim(stacked, own_head * HEAD_DIM, HEAD_DIM, axis=2)
-    stacked = lax.all_gather(stacked, PATCH_AXES[:-1], axis=1, tiled=True)
+    for name in reversed(PATCH_AXES[:-1]):
+        stacked = lax.all_gather(stacked, name, axis=1, tiled=True)
     slab_count = stacked.shape[1] // rows_here
     stale_k = stacked[0].reshape(slab_count, rows_here, HEAD_DIM)
     stale_v = stacked[1].reshape(slab_count, rows_here, HEAD_DIM)

time: 245 us -> 168 us (0.69)
  waiting for transfers between devices: 72.3 us -> 12.5 us
  starting transfers between devices: 36.4 us -> 19.3 us
    all_gather x1, waiting for transfers between devices: 59.3 us -> 0.01 us  [local(): stacked = lax.all_gather(stacked, name, axis=1, tiled=True)]
    all_to_all x1, starting transfers between devices: 27.1 us -> 7.83 us  [local(): attended = lax.all_to_all(result, ('chan', 'px'), 0, 0, tiled=True)]
    all_gather x3 -> x4, blocking collectives: 42.3 us -> 47.3 us  [the longest x3 30.6 us: local(): gathered = lax.all_gather(jnp.stack([group_mean, spread]), name)]
    all_gather x1, blocking collectives: 26.2 us -> 22.1 us  [local(): shard_piece = lax.all_gather(normed, 'chan', axis=1, tiled=True)]
  transfers between devices with their start and end apart: 4 -> 4, of which waited for: 3 -> 2; matrix products, arithmetic and copies ran while one was open for 15% -> 21% of each run, Pallas kernels for 0% -> 0%
where the time goes in v5:
time: 168 us; the launch traced here: 167 us
  blocking collectives  80 us (48%)
  local copies, waits for them, and re-layouts  19.4 us (12%)
  starting transfers between devices  19.3 us (11%)
  between operations  15 us (9%)
  waiting for transfers between devices  12.5 us (7%)
  matrix products  10.6 us (6%)
  other arithmetic  9.98 us (6%)
    all_gather x3, blocking collectives, local(): gathered = lax.all_gather(jnp.stack([group_mean, spread]), name)  30.6 us
    all_gather x1, blocking collectives, local(): shard_piece = lax.all_gather(normed, 'chan', axis=1, tiled=True)  22.1 us
    all_gather x1, blocking collectives, local(): stacked = lax.all_gather(stacked, name, axis=1, tiled=True)  16.8 us
    all_gather x1, blocking collectives, local(): lax.all_gather(jnp.stack([stale_keys, stale_values]), 'px', axis=1, tiled...  10.5 us
    all_to_all x1, waiting for transfers between devices, local(): attended = lax.all_to_all(result, ('chan', 'px'), 0, 0, tiled=True)  9.88 us
    all_to_all x1, starting transfers between devices, local(): out_columns = lax.all_to_all(w_out, 'chan', 1, 0, tiled=True)  8.17 us
    all_to_all x1, starting transfers between devices, local(): attended = lax.all_to_all(result, ('chan', 'px'), 0, 0, tiled=True)  7.83 us
    convert_element_type x1, local copies, waits for them, and re-layouts, local(): weight = jnp.exp(score - block_max[..., None]).astype(jnp.bfloat16)  6.8 us
  transfers between devices with their start and end apart: 4, of which 2 were waited for; matrix products, arithmetic and copies ran while one was open for 21% of the time, Pallas kernels for 0%

profile of v5, /device:TPU:1, one launch (start us, length us, event | category | flops | bytes accessed | tf_op | source)
XLA Modules:
  0.0 166.8 jit_solution(10474553059700699442)
XLA Ops:
  7.3 0.9 pad_maximum_fusion.1
  8.2 10.5 %all_gather.37 = bf16[2,256,256]{2,1,0:T(8,128)(2,1)S(1)} all-gather(bf16[2,64,256]{2,1,0:T(8,128)(2,1)S(1)} %pad_maximum_fusion.1), channel_id=1, replica_groups=mesh['py'=8,'pz'=4,'px'=4,'chan'=4] {'px'}, dimensions={1}, use_global_device_ids=true | all-gather | bytes 327680 | tf_op jit(solution)/shard_map/all_gather | solution.py:81
  18.7 0.1 constant_dynamic-slice_fusion
  18.8 16.8 %all_gather.38 = bf16[2,1024,64]{2,1,0:T(8,128)(2,1)} all-gather(bf16[2,256,64]{2,1,0:T(8,128)(2,1)S(1)} %constant_dynamic-slice_fusion), channel_id=1, replica_groups=mesh['py'=8,'pz'=4,'px'=4,'chan'=4] {'pz'}, dimensions={1}, use_global_device_ids=true | all-gather | bytes 327680 | tf_op jit(solution)/shard_map/all_gather | solution.py:84
  35.6 0.8 convert_reduce_fusion.1
  36.4 0.1 reduce_sum.152
  36.5 0.1 reduce_sum.153
  36.7 0.1 sub.90
  36.7 0.1 sub.91
  36.8 0.8 fusion.6
  37.7 0.1 reduce_sum.155
  37.7 0.1 reduce_sum.156
  37.9 6.8 %all-gather.3 = f32[4,2,8]{2,1,0:T(2,128)S(1)} all-gather(f32[1,2,8]{2,1,0:T(2,128)S(1)} %maximum_bitcast_fusion), channel_id=2, replica_groups=mesh['py'=8,'pz'=4,'px'=4,'chan'=4] {'px'}, dimensions={0}, use_global_device_ids=true | all-gather | bytes 320 | tf_op jit(solution)/shard_map/all_gather | solution.py:56
  44.7 9.6 %all-gather.4 = f32[4,2,8]{2,1,0:T(2,128)S(1)} all-gather(f32[1,2,8]{2,1,0:T(2,128)S(1)} %maximum_bitcast_fusion.1), channel_id=3, replica_groups=mesh['py'=8,'pz'=4,'px'=4,'chan'=4] {'pz'}, dimensions={0}, use_global_device_ids=true | all-gather | bytes 320 | tf_op jit(solution)/shard_map/all_gather | solution.py:56
  54.4 14.1 %all-gather.5 = f32[8,2,8]{2,1,0:T(2,128)S(1)} all-gather(f32[1,2,8]{2,1,0:T(2,128)S(1)} %maximum_bitcast_fusion.2), channel_id=4, replica_groups=mesh['py'=8,'pz'=4,'px'=4,'chan'=4] {'py'}, dimensions={0}, use_global_device_ids=true | all-gather | bytes 576 | tf_op jit(solution)/shard_map/all_gather | solution.py:56
  68.7 0.1 mul.117
  68.7 0.1 mul.118
  68.9 0.1 sub.99
  69.7 0.1 divide_multiply_fusion
  69.8 1.2 convolution_reduce_fusion
  71.0 0.8 fusion.16
  71.8 22.1 %all-gather.6 = bf16[4,320,64]{1,2,0:T(8,128)(2,1)S(1)} all-gather(bf16[1,320,64]{1,2,0:T(8,128)(2,1)S(1)} %fusion.16), channel_id=1, replica_groups=mesh['py'=8,'pz'=4,'px'=4,'chan'=4] {'chan'}, dimensions={0}, use_global_device_ids=true | all-gather | bytes 204800 | tf_op jit(solution)/shard_map/all_gather | solution.py:68
  93.9 0.2 copy.77
  94.1 0.2 reshape.253
  94.3 0.2 convolution_convert_fusion.2
  94.5 0.1 stack.42
  94.7 0.2 convolution_convert_fusion.1
  94.9 0.6 copy-done.5
  95.5 0.1 stack.43
  95.7 0.2 convolution_convert_fusion
  95.9 0.1 stack.44
  96.0 0.5 copy-done.6
  96.6 0.8 reshape.261
  97.4 3.3 %all-to-all-start = ((bf16[4,2,6144]{2,1,0:T(2,128)(2,1)}), bf16[4,2,6144]{2,1,0:T(2,128)(2,1)S(1)}, u32[]{:S(2)}, u32[]{:S(2)}) async-start(bf16[4,2,6144]{2,1,0:T(2,128)(2,1)} %reshape.261), calls=%async_computation | async-start | bytes 196608 | tf_op jit(solution)/shard_map/all_to_all | solution.py:92
  100.8 0.1 iota_compare_fusion
  100.9 0.7 copy.86
  101.6 1.1 copy.94
  102.8 2.6 %all-to-all-done = bf16[4,2,6144]{2,1,0:T(2,128)(2,1)S(1)} async-done(((bf16[4,2,6144]{2,1,0:T(2,128)(2,1)}), bf16[4,2,6144]{2,1,0:T(2,128)(2,1)S(1)}, u32[]{:S(2)}, u32[]{:S(2)}) %all-to-all-start) | async-done | bytes 98336 | tf_op jit(solution)/shard_map/all_to_all | solution.py:92
  105.4 8.2 %all-to-all-start.2 = ((bf16[256,4,320]{0,2,1:T(8,128)(2,1)}), bf16[256,4,320]{0,2,1:T(8,128)(2,1)S(1)}, u32[]{:S(2)}, u32[]{:S(2)}) async-start(bf16[256,4,320]{0,2,1:T(8,128)(2,1)} %bitcast.31), calls=%async_computation.2 | async-start | bytes 1310720 | tf_op jit(solution)/shard_map/all_to_all | solution.py:133
  113.6 0.2 reshape.262
  113.8 0.2 fusion.26
  114.0 0.1 broadcast_in_dim.37
  114.1 0.1 broadcast_in_dim.62
  114.2 0.2 fusion.14
  114.4 0.7 copy.88
  115.1 2.5 %fusion.24 = (bf16[1,8192,64]{2,1,0:T(8,128)(2,1)S(1)}, bf16[1,8192,64]{2,1,0:T(8,128)(2,1)S(1)}) fusion(bf16[2,8192,64]{2,1,0:T(8,128)(2,1)} %all-gather.9.cloned.1.call-done), kind=kLoop, calls=%fused_computation.74 | loop fusion | bytes 4194304 | tf_op jit(solution)/shard_map/slice | solution.py:87
  117.6 2.2 %multiply_reduce_fusion = (f32[256,128]{1,0:T(8,128)S(1)}, f32[256,128,64]{1,0,2:T(8,128)S(1)}) fusion(bf16[256,64,1]{1,0,2:T(8,128)(2,1)S(1)} %bitcast.90, bf16[128,64,64]{2,1,0:T(8,128)(2,1)S(1)} %bitcast.86), kind=kOutput, calls=%fused_computation.5 | convolution fusion | flops 272596992 | bytes 9601024 | tf_op jit(solution)/shard_map/qd,skd->qsk/dot_general | solution.py:96
  119.8 3.7 %convert_reduce_fusion = (f32[256,128]{1,0:T(8,128)}, bf16[256,128,64]{1,0,2:T(8,128)(2,1)}) fusion(f32[256,128]{1,0:T(8,128)S(1)} %get-tuple-element.25, f32[256,128,64]{1,0,2:T(8,128)S(1)} %get-tuple-element.26), kind=kLoop, calls=%fused_computation.3 | loop fusion | flops 10452992 | bytes 12845056 | tf_op jit(solution)/shard_map/reduce_sum | solution.py:102
  123.5 6.8 %copy.91 = bf16[256,128,64]{0,2,1:T(8,128)(2,1)} copy(bf16[256,128,64]{1,0,2:T(8,128)(2,1)} %get-tuple-element.10) | data formatting | bytes 8388608 | tf_op jit(solution)/shard_map/convert_element_type | solution.py:100
  130.3 0.2 fusion.13
  130.5 1.8 %multiply_reduce_fusion.1 = (f32[256]{0:T(256)S(1)}, f32[256,128]{1,0:T(8,128)}) fusion(f32[256,128]{1,0:T(8,128)} %get-tuple-element.9, f32[256]{0:T(256)S(1)} %broadcast_in_dim.62, s32[256]{0:T(256)S(1)} %fusion.17, f32[256]{0:T(256)S(1)} %fusion.13, f32[256,128]{1,0:T(8,128)S(1)} %get-tuple-element.25, f32[256]{0:T(256)S(1)} %broadcast_in_dim.37), kind=kLoop, calls=%fused_computation.20 | loop fusion | flops 196352 | bytes 398336 | tf_op jit(solution)/shard_map/reduce_sum | solution.py:126
  132.3 1.0 copy.85
  133.3 4.4 %fusion.1 = f32[256,64]{0,1:T(8,128)} fusion(f32[256,64]{0,1:T(8,128)} %copy.88, f32[256,128]{0,1:T(8,128)S(1)} %copy.85, pred[256,128]{0,1:T(8,128)(4,1)} %copy.86, bf16[128,64,64]{2,1,0:T(8,128)(2,1)S(1)} %bitcast.89, bf16[256,128,64]{0,2,1:T(8,128)(2,1)} %copy.91), kind=kOutput, calls=%fused_computation.2 | convolution fusion | flops 274710528 | bytes 5537792 | tf_op jit(solution)/shard_map/qsk,skd->qsd/dot_general | solution.py:101
  137.7 0.9 reduce_sum.167
  138.6 0.1 div.79
  138.8 0.1 copy.92
  138.9 0.9 reshape.263
  139.8 7.8 %all-to-all-start.1 = ((bf16[16,2,2048]{2,1,0:T(2,128)(2,1)}), bf16[16,2,2048]{2,1,0:T(2,128)(2,1)S(1)}, u32[]{:S(2)}, u32[]{:S(2)}) async-start(bf16[16,2,2048]{2,1,0:T(2,128)(2,1)} %reshape.263), calls=%async_computation.1 | async-start | bytes 262144 | tf_op jit(solution)/shard_map/all_to_all | solution.py:131
  147.6 0.1 copy.104
  147.7 9.9 %all-to-all-done.1 = bf16[16,2,2048]{2,1,0:T(2,128)(2,1)S(1)} async-done(((bf16[16,2,2048]{2,1,0:T(2,128)(2,1)}), bf16[16,2,2048]{2,1,0:T(2,128)(2,1)S(1)}, u32[]{:S(2)}, u32[]{:S(2)}) %all-to-all-start.1) | async-done | bytes 131104 | tf_op jit(solution)/shard_map/all_to_all | solution.py:131
  157.6 0.2 reshape.264
  157.8 0.2 copy.93
  158.0 0.2 reshape.242
  158.2 1.8 %fusion.4 = bf16[64,320]{1,0:T(8,128)(2,1)} fusion(bf16[64,1024]{1,0:T(8,128)(2,1)S(1)} %reshape.242, bf16[1024,320]{0,1:T(8,128)(2,1)S(1)} %bitcast.88, bf16[64,320]{1,0:T(8,128)(2,1)} %param.11), kind=kOutput, calls=%fused_computation.10 | convolution fusion | flops 42004480 | bytes 868352 | tf_op jit(solution)/shard_map/dot_general | solution.py:134
  (47 shorter events, 0.7 us)
Async XLA Ops:
  7.2 87.1 %copy-start = (bf16[1280,256]{1,0:T(8,128)(2,1)S(1)}, bf16[1280,256]{1,0:T(8,128)(2,1)}, u32[]{:S(2)}) copy-start(bf16[1280,256]{1,0:T(8,128)(2,1)} %param.16) | copy-start | bytes 1966084
  7.2 87.5 %copy-start.3 = (bf16[1280,256]{1,0:T(8,128)(2,1)S(1)}, bf16[1280,256]{1,0:T(8,128)(2,1)}, u32[]{:S(2)}) copy-start(bf16[1280,256]{1,0:T(8,128)(2,1)} %param.17) | copy-start | bytes 1966084
  7.2 88.5 %copy-start.4 = (bf16[1280,256]{1,0:T(8,128)(2,1)S(1)}, bf16[1280,256]{1,0:T(8,128)(2,1)}, u32[]{:S(2)}) copy-start(bf16[1280,256]{1,0:T(8,128)(2,1)} %param.18) | copy-start | bytes 1966084
  7.2 94.4 %copy-start.2 = (bf16[256,1280]{1,0:T(8,128)(2,1)S(1)}, bf16[256,1280]{1,0:T(8,128)(2,1)}, u32[]{:S(2)}) copy-start(bf16[256,1280]{1,0:T(8,128)(2,1)} %param.19) | copy-start | bytes 1966084
  7.2 107.9 %all-gather.9.cloned.1.call-start = ((), (), s32[]{:S(2)}) async-start(), calls=%async_computation.3 | async-start | bytes 4718592 | tf_op jit(solution)/shard_map/all_gather | solution.py:84
  94.9 0.6 copy-start.5
  95.9 0.6 copy-start.6
  97.4 7.9 %all-to-all-start = ((bf16[4,2,6144]{2,1,0:T(2,128)(2,1)}), bf16[4,2,6144]{2,1,0:T(2,128)(2,1)S(1)}, u32[]{:S(2)}, u32[]{:S(2)}) async-start(bf16[4,2,6144]{2,1,0:T(2,128)(2,1)} %reshape.261), calls=%async_computation | async-start | bytes 196608 | tf_op jit(solution)/shard_map/all_to_all | solution.py:92
  105.4 34.4 %all-to-all-start.2 = ((bf16[256,4,320]{0,2,1:T(8,128)(2,1)}), bf16[256,4,320]{0,2,1:T(8,128)(2,1)S(1)}, u32[]{:S(2)}, u32[]{:S(2)}) async-start(bf16[256,4,320]{0,2,1:T(8,128)(2,1)} %bitcast.31), calls=%async_computation.2 | async-start | bytes 1310720 | tf_op jit(solution)/shard_map/all_to_all | solution.py:133
  113.8 1.3 copy-start.1
  115.1 2.5 %slice-start = ((bf16[3,4,64,1,64]{4,2,1,3,0:T(8,128)(2,1)}), bf16[1,4,64,1,64]{4,2,1,3,0:T(8,128)(2,1)S(1)}, s32[]{:S(2)}) async-start(bf16[3,4,64,1,64]{4,2,1,3,0:T(8,128)(2,1)} %copy-done.1), calls=%async_computation.4 | async-start | bytes 131072 | tf_op jit(solution)/shard_map/slice | solution.py:105
  139.8 17.8 %all-to-all-start.1 = ((bf16[16,2,2048]{2,1,0:T(2,128)(2,1)}), bf16[16,2,2048]{2,1,0:T(2,128)(2,1)S(1)}, u32[]{:S(2)}, u32[]{:S(2)}) async-start(bf16[16,2,2048]{2,1,0:T(2,128)(2,1)} %reshape.263), calls=%async_computation.1 | async-start | bytes 262144 | tf_op jit(solution)/shard_map/all_to_all | solution.py:131
Sparse Core Ops, SparseCore 0:
  35.7 63.9 all-gather.8

commit v6 on v5

--- a/solution.py
+++ b/solution.py
@@ -78,8 +78,8 @@
     split = lax.axis_size("px")
     own_head = lax.axis_index("px")
 
-    stacked = lax.all_gather(jnp.stack([stale_keys, stale_values]), "px", axis=1, tiled=True)
-    stacked = lax.dynamic_slice_in_dim(stacked, own_head * HEAD_DIM, HEAD_DIM, axis=2)
+    stacked = jnp.stack([stale_keys, stale_values]).reshape(2, rows_here, heads_here, HEAD_DIM)
+    stacked = lax.all_to_all(stacked, "px", 2, 1, tiled=True).reshape(2, split * rows_here, HEAD_DIM)
     for name in reversed(PATCH_AXES[:-1]):
         stacked = lax.all_gather(stacked, name, axis=1, tiled=True)
     slab_count = stacked.shape[1] // rows_here
@@ -93,12 +93,12 @@
     query_rows = fresh[0].reshape(split * rows_here, HEAD_DIM)
 
     score = (
-        jnp.einsum("qd,skd->qsk", query_rows, stale_k, preferred_element_type=jnp.float32)
+        jnp.einsum("qd,skd->sqk", query_rows, stale_k, preferred_element_type=jnp.float32)
         * score_scale
     )
     block_max = jnp.max(score, axis=-1)
     weight = jnp.exp(score - block_max[..., None]).astype(jnp.bfloat16)
-    block_num = jnp.einsum("qsk,skd->qsd", weight, stale_v, preferred_element_type=jnp.float32)
+    block_num = jnp.einsum("sqk,skd->sqd", weight, stale_v, preferred_element_type=jnp.float32)
     block_den = jnp.sum(weight.astype(jnp.float32), axis=-1)
 
     home_score = (
@@ -109,29 +109,30 @@
     home_weight = jnp.exp(home_score - home_max[..., None]).astype(jnp.bfloat16)
     home_num = jnp.einsum("gqk,gkd->gqd", home_weight, fresh[2], preferred_element_type=jnp.float32)
     home_den = jnp.sum(home_weight.astype(jnp.float32), axis=-1)
-    home_max = home_max.reshape(split * rows_here, 1)
-    home_num = home_num.reshape(split * rows_here, 1, HEAD_DIM)
-    home_den = home_den.reshape(split * rows_here, 1)
+    home_max = home_max.reshape(1, split * rows_here)
+    home_num = home_num.reshape(1, split * rows_here, HEAD_DIM)
+    home_den = home_den.reshape(1, split * rows_here)
 
     first_slab = (device // split) * split
     query_slab = first_slab + jnp.arange(split * rows_here, dtype=jnp.int32) // rows_here
-    is_home = query_slab[:, None] == jnp.arange(slab_count, dtype=jnp.int32)[None, :]
+    is_home = jnp.arange(slab_count, dtype=jnp.int32)[:, None] == query_slab[None, :]
     block_max = jnp.where(is_home, home_max, block_max)
     block_den = jnp.where(is_home, home_den, block_den)
     block_num = jnp.where(is_home[..., None], home_num, block_num)
 
-    top = jnp.max(block_max, axis=-1)
-    factor = jnp.exp(block_max - top[:, None])
-    numer = jnp.sum(factor[..., None] * block_num, axis=1)
-    denom = jnp.sum(factor * block_den, axis=1)
+    top = jnp.max(block_max, axis=0)
+    factor = jnp.exp(block_max - top[None, :])
+    numer = jnp.sum(factor[..., None] * block_num, axis=0)
+    denom = jnp.sum(factor * block_den, axis=0)
     result = (numer / denom[:, None]).astype(jnp.bfloat16)
     result = result.reshape(1, split, rows_here, HEAD_DIM)
     result = jnp.broadcast_to(result, (chan_count, split, rows_here, HEAD_DIM))
     result = result.reshape(chan_count * split, rows_here, HEAD_DIM)
     attended = lax.all_to_all(result, ("chan", "px"), 0, 0, tiled=True)
     attended = jnp.transpose(attended, (1, 0, 2)).reshape(rows_here, chan_count * inner)
-    out_columns = lax.all_to_all(w_out, "chan", 1, 0, tiled=True)
-    projected = jnp.dot(attended, out_columns, preferred_element_type=jnp.float32)
+    out_rows = lax.all_gather(w_out, "chan", axis=0, tiled=True)
+    projected = jnp.dot(attended, out_rows, preferred_element_type=jnp.float32)
+    projected = lax.dynamic_slice_in_dim(projected, lax.axis_index("chan") * chan_width, chan_width, axis=1)
     mixed = (latent.astype(jnp.float32) + projected).astype(jnp.bfloat16)
     return (mixed, fresh_keys, fresh_values)
 

time: 168 us -> 161 us (0.958)
  blocking collectives: 80 us -> 66.4 us
  waiting for transfers between devices: 12.5 us -> 19.7 us
  matrix products: 10.6 us -> 16.5 us
  other arithmetic: 9.98 us -> 5.73 us
  starting transfers between devices: 19.3 us -> 17.1 us
    all_gather x1 -> x0, blocking collectives: 10.5 us -> none  [local(): lax.all_gather(jnp.stack([stale_keys, stale_values]), 'px', axis=1, tiled...]
    another operation x0 -> x3, local copies, waits for them, and re-layouts: none -> 8.95 us  [the longest x2 5.65 us: local(): stale_k = stacked[0].reshape(slab_count, rows_here, HEAD_DIM)]
    convert_element_type x1 -> x0, local copies, waits for them, and re-layouts: 6.8 us -> none  [local(): weight = jnp.exp(score - block_max[..., None]).astype(jnp.bfloat16)]
    dot_general x3, matrix products: 8.33 us -> 14.2 us  [the longest x1 9.27 us: local(): jnp.einsum('sqk,skd->sqd', weight, stale_v, preferred_element_type=jnp.fl...]
    all_to_all x1, waiting for transfers between devices: 9.88 us -> 15.3 us  [local(): attended = lax.all_to_all(result, ('chan', 'px'), 0, 0, tiled=True)]
    all_to_all x1, starting transfers between devices: 8.17 us -> 4.83 us  [local(): lax.all_to_all(stacked, 'px', 2, 1, tiled=True)]
    all_gather x1, blocking collectives: 16.8 us -> 14 us  [local(): stacked = lax.all_gather(stacked, name, axis=1, tiled=True)]
    reduce_sum x1, other arithmetic: 3.72 us -> 1.59 us  [local(): block_den = jnp.sum(weight.astype(jnp.float32), axis=-1)]
  transfers between devices with their start and end apart: 4 -> 5, of which waited for: 2 -> 2; matrix products, arithmetic and copies ran while one was open for 21% -> 22% of each run, Pallas kernels for 0% -> 0%
where the time goes in v6:
time: 161 us; the launch traced here: 160 us
  blocking collectives  66.4 us (41%)
  waiting for transfers between devices  19.7 us (12%)
  local copies, waits for them, and re-layouts  19.6 us (12%)
  starting transfers between devices  17.1 us (11%)
  matrix products  16.5 us (10%)
  between operations  15.1 us (9%)
  other arithmetic  5.73 us (4%)
    all_gather x3, blocking collectives, local(): gathered = lax.all_gather(jnp.stack([group_mean, spread]), name)  30.9 us
    all_gather x1, blocking collectives, local(): shard_piece = lax.all_gather(normed, 'chan', axis=1, tiled=True)  21.5 us
    all_to_all x1, waiting for transfers between devices, local(): attended = lax.all_to_all(result, ('chan', 'px'), 0, 0, tiled=True)  15.3 us
    all_gather x1, blocking collectives, local(): stacked = lax.all_gather(stacked, name, axis=1, tiled=True)  14 us
    dot_general x1, matrix products, local(): jnp.einsum('sqk,skd->sqd', weight, stale_v, preferred_element_type=jnp.fl...  9.27 us
    all_to_all x1, starting transfers between devices, local(): attended = lax.all_to_all(result, ('chan', 'px'), 0, 0, tiled=True)  8.77 us
    another operation x2, local copies, waits for them, and re-layouts, local(): stale_k = stacked[0].reshape(slab_count, rows_here, HEAD_DIM)  5.65 us
    unnamed x21, local copies, waits for them, and re-layouts  5.13 us
  transfers between devices with their start and end apart: 5, of which 2 were waited for; matrix products, arithmetic and copies ran while one was open for 22% of the time, Pallas kernels for 0%

profile of v6, /device:TPU:1, one launch (start us, length us, event | category | flops | bytes accessed | tf_op | source)
XLA Modules:
  0.0 160.0 jit_solution(3801575283384904783)
XLA Ops:
  7.2 1.0 copy.69
  8.2 0.9 copy.70
  9.1 0.8 reshape.260
  9.9 4.8 %all-to-all-start.1 = ((bf16[4,2,4096]{2,1,0:T(2,128)(2,1)}), bf16[4,2,4096]{2,1,0:T(2,128)(2,1)S(1)}, u32[]{:S(2)}, u32[]{:S(2)}) async-start(bf16[4,2,4096]{2,1,0:T(2,128)(2,1)} %reshape.260), calls=%async_computation.1 | async-start | bytes 131072 | tf_op jit(solution)/shard_map/all_to_all | solution.py:82
  14.7 0.8 convert_reduce_fusion.1
  15.6 0.1 reduce_sum.152
  15.7 0.1 reduce_sum.153
  15.8 0.1 sub.90
  15.9 0.1 sub.91
  15.9 0.8 fusion.8
  16.8 0.1 reduce_sum.155
  16.9 0.1 reduce_sum.156
  17.0 8.2 %all-gather.3 = f32[4,2,8]{2,1,0:T(2,128)S(1)} all-gather(f32[1,2,8]{2,1,0:T(2,128)S(1)} %maximum_bitcast_fusion), channel_id=2, replica_groups=mesh['py'=8,'pz'=4,'px'=4,'chan'=4] {'px'}, dimensions={0}, use_global_device_ids=true | all-gather | bytes 320 | tf_op jit(solution)/shard_map/all_gather | solution.py:56
  25.3 0.1 reshape.261
  25.4 0.1 copy.71
  25.5 0.1 reshape.237
  25.7 14.0 %all_gather.37 = bf16[2,1024,64]{1,2,0:T(8,128)(2,1)} all-gather(bf16[2,256,64]{1,2,0:T(8,128)(2,1)S(1)} %reshape.237), channel_id=1, replica_groups=mesh['py'=8,'pz'=4,'px'=4,'chan'=4] {'pz'}, dimensions={1}, use_global_device_ids=true | all-gather | bytes 327680 | tf_op jit(solution)/shard_map/all_gather | solution.py:84
  39.8 9.4 %all-gather.4 = f32[4,2,8]{2,1,0:T(2,128)S(1)} all-gather(f32[1,2,8]{2,1,0:T(2,128)S(1)} %maximum_bitcast_fusion.1), channel_id=3, replica_groups=mesh['py'=8,'pz'=4,'px'=4,'chan'=4] {'pz'}, dimensions={0}, use_global_device_ids=true | all-gather | bytes 320 | tf_op jit(solution)/shard_map/all_gather | solution.py:56
  49.2 13.3 %all-gather.5 = f32[8,2,8]{2,1,0:T(2,128)S(1)} all-gather(f32[1,2,8]{2,1,0:T(2,128)S(1)} %maximum_bitcast_fusion.2), channel_id=4, replica_groups=mesh['py'=8,'pz'=4,'px'=4,'chan'=4] {'py'}, dimensions={0}, use_global_device_ids=true | all-gather | bytes 576 | tf_op jit(solution)/shard_map/all_gather | solution.py:56
  62.6 0.1 mul.120
  62.6 0.1 mul.121
  62.7 0.1 sub.98
  62.8 0.1 sub.99
  63.6 0.1 divide_multiply_fusion
  63.7 1.2 convolution_reduce_fusion
  64.9 0.8 fusion.19
  65.7 21.5 %all-gather.6 = bf16[4,320,64]{1,2,0:T(8,128)(2,1)S(1)} all-gather(bf16[1,320,64]{1,2,0:T(8,128)(2,1)S(1)} %fusion.19), channel_id=1, replica_groups=mesh['py'=8,'pz'=4,'px'=4,'chan'=4] {'chan'}, dimensions={0}, use_global_device_ids=true | all-gather | bytes 204800 | tf_op jit(solution)/shard_map/all_gather | solution.py:68
  87.2 0.2 copy.64
  87.4 0.2 reshape.250
  87.6 0.2 convolution_convert_fusion.2
  87.8 0.1 stack.42
  88.0 0.2 convolution_convert_fusion.1
  88.2 0.1 stack.43
  88.3 0.2 convolution_convert_fusion
  88.6 0.1 stack.44
  88.8 0.8 reshape.258
  89.6 3.3 %all-to-all-start = ((bf16[4,2,6144]{2,1,0:T(2,128)(2,1)}), bf16[4,2,6144]{2,1,0:T(2,128)(2,1)S(1)}, u32[]{:S(2)}, u32[]{:S(2)}) async-start(bf16[4,2,6144]{2,1,0:T(2,128)(2,1)} %reshape.258), calls=%async_computation | async-start | bytes 196608 | tf_op jit(solution)/shard_map/all_to_all | solution.py:92
  92.9 0.2 all-gather.12.cloned.1.call-start
  93.2 0.5 all-gather.12.cloned.1.call-update
  93.7 3.8 %all-to-all-done = bf16[4,2,6144]{2,1,0:T(2,128)(2,1)S(1)} async-done(((bf16[4,2,6144]{2,1,0:T(2,128)(2,1)}), bf16[4,2,6144]{2,1,0:T(2,128)(2,1)S(1)}, u32[]{:S(2)}, u32[]{:S(2)}) %all-to-all-start) | async-done | bytes 98336 | tf_op jit(solution)/shard_map/all_to_all | solution.py:92
  97.6 0.2 reshape.259
  97.8 0.2 fusion.30
  98.0 0.1 broadcast_in_dim.37
  98.1 0.2 fusion.17
  98.3 0.1 broadcast_in_dim.62
  98.4 0.1 copy.75
  98.5 3.1 %fusion.28 = (bf16[1,8192,64]{1,2,0:T(8,128)(2,1)}, bf16[1,8192,64]{1,2,0:T(8,128)(2,1)}) fusion(bf16[2,8192,64]{1,2,0:T(8,128)(2,1)} %all-gather.10.cloned.1.call-done), kind=kLoop, calls=%fused_computation.74 | loop fusion | bytes 4194304 | tf_op jit(solution)/shard_map/slice | solution.py:87
  101.6 3.3 %reshape_squeeze.9 = bf16[128,64,64]{1,0,2:T(8,128)(2,1)S(1)} reshape(bf16[1,8192,64]{1,2,0:T(8,128)(2,1)} %get-tuple-element.12) | data formatting | bytes 2097152 | tf_op jit(solution)/shard_map/reshape;squeeze | solution.py:86
  104.9 2.4 %copy.72 = bf16[128,64,64]{0,2,1:T(8,128)(2,1)} copy(bf16[128,64,64]{1,0,2:T(8,128)(2,1)S(1)} %reshape_squeeze.9) | data formatting | bytes 2097152 | tf_op jit(solution)/shard_map/reshape;squeeze | solution.py:86
  107.3 3.3 %reshape_squeeze.11 = bf16[128,64,64]{1,0,2:T(8,128)(2,1)S(1)} reshape(bf16[1,8192,64]{1,2,0:T(8,128)(2,1)} %get-tuple-element.11) | data formatting | bytes 2097152 | tf_op jit(solution)/shard_map/reshape;squeeze | solution.py:87
  110.6 2.6 %bitcast_reduce_fusion = (f32[128,256]{1,0:T(8,128)S(1)}, f32[128,64,256]{2,0,1:T(8,128)S(1)}) fusion(bf16[128,64,64]{0,2,1:T(8,128)(2,1)} %copy.72, bf16[256,64,1]{1,0,2:T(8,128)(2,1)S(1)} %bitcast.98), kind=kOutput, calls=%fused_computation.1 | convolution fusion | flops 272596992 | bytes 9601024 | tf_op jit(solution)/shard_map/qd,skd->sqk/dot_general | solution.py:96
  113.2 1.6 convert_reduce_fusion
  114.9 9.3 %multiply_reduce_fusion = f32[256,64]{0,1:T(8,128)S(1)} fusion(f32[256,64]{0,1:T(8,128)S(1)} %copy.75, f32[128,256]{1,0:T(8,128)S(1)} %get-tuple-element.8, pred[128,256]{1,0:T(8,128)(4,1)S(1)} %iota_compare_fusion, bf16[128,256,64]{1,0,2:T(8,128)(2,1)S(1)} %get-tuple-element.10, bf16[128,64,64]{1,0,2:T(8,128)(2,1)S(1)} %reshape_squeeze.11), kind=kOutput, calls=%fused_computation.5 | convolution fusion | flops 274710528 | bytes 5537792 | tf_op jit(solution)/shard_map/sqk,skd->sqd/dot_general | solution.py:101
  124.2 0.1 reduce_sum.167
  124.3 0.1 div.79
  124.4 0.1 copy.78
  124.6 0.9 reshape.262
  125.5 8.8 %all-to-all-start.2 = ((bf16[16,2,2048]{2,1,0:T(2,128)(2,1)}), bf16[16,2,2048]{2,1,0:T(2,128)(2,1)S(1)}, u32[]{:S(2)}, u32[]{:S(2)}) async-start(bf16[16,2,2048]{2,1,0:T(2,128)(2,1)} %reshape.262), calls=%async_computation.2 | async-start | bytes 262144 | tf_op jit(solution)/shard_map/all_to_all | solution.py:131
  134.3 15.3 %all-to-all-done.2 = bf16[16,2,2048]{2,1,0:T(2,128)(2,1)S(1)} async-done(((bf16[16,2,2048]{2,1,0:T(2,128)(2,1)}), bf16[16,2,2048]{2,1,0:T(2,128)(2,1)S(1)}, u32[]{:S(2)}, u32[]{:S(2)}) %all-to-all-start.2) | async-done | bytes 131104 | tf_op jit(solution)/shard_map/all_to_all | solution.py:131
  149.5 0.2 reshape.263
  149.8 0.2 copy.79
  149.9 0.2 reshape.239
  150.2 2.3 %fusion.33 = f32[64,1280]{1,0:T(8,128)S(1)} fusion(bf16[64,1024]{1,0:T(8,128)(2,1)S(1)} %reshape.239, bf16[1024,1280]{1,0:T(8,128)(2,1)} %all-gather.12.cloned.1.call-done), kind=kOutput, calls=%fused_computation.80 | convolution fusion | flops 167772160 | bytes 3080192 | tf_op jit(solution)/shard_map/dot_general | solution.py:134
  152.5 0.7 fusion.14
  (51 shorter events, 0.8 us)
Async XLA Ops:
  7.2 80.4 %copy-start = (bf16[1280,256]{1,0:T(8,128)(2,1)S(1)}, bf16[1280,256]{1,0:T(8,128)(2,1)}, u32[]{:S(2)}) copy-start(bf16[1280,256]{1,0:T(8,128)(2,1)} %param.16) | copy-start | bytes 1966084
  7.2 80.8 %copy-start.2 = (bf16[1280,256]{1,0:T(8,128)(2,1)S(1)}, bf16[1280,256]{1,0:T(8,128)(2,1)}, u32[]{:S(2)}) copy-start(bf16[1280,256]{1,0:T(8,128)(2,1)} %param.17) | copy-start | bytes 1966084
  7.2 81.1 %copy-start.3 = (bf16[1280,256]{1,0:T(8,128)(2,1)S(1)}, bf16[1280,256]{1,0:T(8,128)(2,1)}, u32[]{:S(2)}) copy-start(bf16[1280,256]{1,0:T(8,128)(2,1)} %param.18) | copy-start | bytes 1966084
  9.9 15.4 %all-to-all-start.1 = ((bf16[4,2,4096]{2,1,0:T(2,128)(2,1)}), bf16[4,2,4096]{2,1,0:T(2,128)(2,1)S(1)}, u32[]{:S(2)}, u32[]{:S(2)}) async-start(bf16[4,2,4096]{2,1,0:T(2,128)(2,1)} %reshape.260), calls=%async_computation.1 | async-start | bytes 131072 | tf_op jit(solution)/shard_map/all_to_all | solution.py:82
  14.7 83.8 %all-gather.10.cloned.1.call-start = ((), (), s32[]{:S(2)}) async-start(), calls=%async_computation.3 | async-start | bytes 2359296 | tf_op jit(solution)/shard_map/all_gather | solution.py:84
  88.2 13.4 %copy-start.4 = (bf16[64,256]{1,0:T(8,128)(2,1)}, bf16[64,256]{1,0:T(8,128)(2,1)S(1)}, u32[]{:S(2)}) copy-start(bf16[64,256]{1,0:T(8,128)(2,1)S(1)} %convolution_convert_fusion.1) | copy-start | bytes 98308
  88.6 16.3 %copy-start.5 = (bf16[64,256]{1,0:T(8,128)(2,1)}, bf16[64,256]{1,0:T(8,128)(2,1)S(1)}, u32[]{:S(2)}) copy-start(bf16[64,256]{1,0:T(8,128)(2,1)S(1)} %convolution_convert_fusion) | copy-start | bytes 98308
  89.6 7.9 %all-to-all-start = ((bf16[4,2,6144]{2,1,0:T(2,128)(2,1)}), bf16[4,2,6144]{2,1,0:T(2,128)(2,1)S(1)}, u32[]{:S(2)}, u32[]{:S(2)}) async-start(bf16[4,2,6144]{2,1,0:T(2,128)(2,1)} %reshape.258), calls=%async_computation | async-start | bytes 196608 | tf_op jit(solution)/shard_map/all_to_all | solution.py:92
  92.9 57.2 %all-gather.12.cloned.1.call-start = ((), (), s32[]{:S(2)}) async-start(), calls=%async_computation.4 | async-start | bytes 3276800 | tf_op jit(solution)/shard_map/all_gather | solution.py:133
  124.2 28.3 %copy-start.1 = (bf16[64,320]{1,0:T(8,128)(2,1)S(1)}, bf16[64,320]{1,0:T(8,128)(2,1)}, u32[]{:S(2)}) copy-start(bf16[64,320]{1,0:T(8,128)(2,1)} %param.11) | copy-start | bytes 122884
  125.5 24.0 %all-to-all-start.2 = ((bf16[16,2,2048]{2,1,0:T(2,128)(2,1)}), bf16[16,2,2048]{2,1,0:T(2,128)(2,1)S(1)}, u32[]{:S(2)}, u32[]{:S(2)}) async-start(bf16[16,2,2048]{2,1,0:T(2,128)(2,1)} %reshape.262), calls=%async_computation.2 | async-start | bytes 262144 | tf_op jit(solution)/shard_map/all_to_all | solution.py:131
Sparse Core Ops, SparseCore 0:
  39.8 45.2 all-gather.9
  95.9 53.2 all-gather.11

commit v7 on v5

--- a/solution.py
+++ b/solution.py
@@ -27,6 +27,20 @@
     for name in reversed(PATCH_AXES):
         partial = lax.optimization_barrier(lax.psum(partial, name))
     return partial
+
+
+def permute_gather(piece, name):
+    size = lax.axis_size(name)
+    here = lax.axis_index(name)
+    received = [piece]
+    for shift in range(1, size):
+        pairs = [(source, (source + shift) % size) for source in range(size)]
+        received.append(lax.ppermute(piece, name, pairs))
+    received = jnp.stack(received)
+    order = (here - jnp.arange(size, dtype=jnp.int32)) % size
+    blocks = jnp.take(received, order, axis=0)
+    blocks = jnp.moveaxis(blocks, 0, 1)
+    return blocks.reshape(piece.shape[0], size * piece.shape[1], *piece.shape[2:])
 
 
 def local(
@@ -78,10 +92,10 @@
     split = lax.axis_size("px")
     own_head = lax.axis_index("px")
 
-    stacked = lax.all_gather(jnp.stack([stale_keys, stale_values]), "px", axis=1, tiled=True)
-    stacked = lax.dynamic_slice_in_dim(stacked, own_head * HEAD_DIM, HEAD_DIM, axis=2)
-    for name in reversed(PATCH_AXES[:-1]):
-        stacked = lax.all_gather(stacked, name, axis=1, tiled=True)
+    stacked = jnp.stack([stale_keys, stale_values]).reshape(2, rows_here, heads_here, HEAD_DIM)
+    stacked = lax.all_to_all(stacked, "px", 2, 1, tiled=True).reshape(2, split * rows_here, HEAD_DIM)
+    stacked = permute_gather(stacked, "pz")
+    stacked = lax.all_gather(stacked, "py", axis=1, tiled=True)
     slab_count = stacked.shape[1] // rows_here
     stale_k = stacked[0].reshape(slab_count, rows_here, HEAD_DIM)
     stale_v = stacked[1].reshape(slab_count, rows_here, HEAD_DIM)
@@ -130,8 +144,9 @@
     result = result.reshape(chan_count * split, rows_here, HEAD_DIM)
     attended = lax.all_to_all(result, ("chan", "px"), 0, 0, tiled=True)
     attended = jnp.transpose(attended, (1, 0, 2)).reshape(rows_here, chan_count * inner)
-    out_columns = lax.all_to_all(w_out, "chan", 1, 0, tiled=True)
-    projected = jnp.dot(attended, out_columns, preferred_element_type=jnp.float32)
+    out_rows = lax.all_gather(w_out, "chan", axis=0, tiled=True)
+    projected = jnp.dot(attended, out_rows, preferred_element_type=jnp.float32)
+    projected = lax.dynamic_slice_in_dim(projected, lax.axis_index("chan") * chan_width, chan_width, axis=1)
     mixed = (latent.astype(jnp.float32) + projected).astype(jnp.bfloat16)
     return (mixed, fresh_keys, fresh_values)
 

time: 168 us -> 160 us (0.952)
  blocking collectives: 80 us -> 49.5 us
  starting transfers between devices: 19.3 us -> 28.8 us
  waiting for transfers between devices: 12.5 us -> 21.3 us
  local copies, waits for them, and re-layouts: 19.4 us -> 27.1 us
  other arithmetic: 9.98 us -> 7.04 us
    all_gather x2 -> x0, blocking collectives: 27.3 us -> none  [the longest x1 16.8 us: local(): stacked = lax.all_gather(stacked, name, axis=1, tiled=True)]
    ppermute x0 -> x3, starting transfers between devices: none -> 11.7 us  [permute_gather(): received.append(lax.ppermute(piece, name, pairs))]
    another operation x0 -> x4, local copies, waits for them, and re-layouts: none -> 9.52 us  [the longest x2 6.07 us: local(): stale_k = stacked[0].reshape(slab_count, rows_here, HEAD_DIM)]
    ppermute x0 -> x3, waiting for transfers between devices: none -> 4.11 us  [permute_gather(): received.append(lax.ppermute(piece, name, pairs))]
    all_to_all x1, starting transfers between devices: 8.17 us -> 4.83 us  [local(): lax.all_to_all(stacked, 'px', 2, 1, tiled=True)]
    all_to_all x1, waiting for transfers between devices: 9.88 us -> 13 us  [local(): attended = lax.all_to_all(result, ('chan', 'px'), 0, 0, tiled=True)]
    all_gather x3, blocking collectives: 30.6 us -> 27.7 us  [local(): gathered = lax.all_gather(jnp.stack([group_mean, spread]), name)]
    unnamed x20 -> x27, local copies, waits for them, and re-layouts: 4.57 us -> 5.15 us
  transfers between devices with their start and end apart: 4 -> 8, of which waited for: 2 -> 3; matrix products, arithmetic and copies ran while one was open for 21% -> 23% of each run, Pallas kernels for 0% -> 0%
where the time goes in v7:
time: 160 us; the launch traced here: 159 us
  blocking collectives  49.5 us (31%)
  starting transfers between devices  28.8 us (18%)
  local copies, waits for them, and re-layouts  27.1 us (17%)
  waiting for transfers between devices  21.3 us (13%)
  between operations  15.2 us (10%)
  matrix products  10.1 us (6%)
  other arithmetic  7.04 us (4%)
    all_gather x3, blocking collectives, local(): gathered = lax.all_gather(jnp.stack([group_mean, spread]), name)  27.7 us
    all_gather x1, blocking collectives, local(): shard_piece = lax.all_gather(normed, 'chan', axis=1, tiled=True)  21.7 us
    all_to_all x1, waiting for transfers between devices, local(): attended = lax.all_to_all(result, ('chan', 'px'), 0, 0, tiled=True)  13 us
    ppermute x3, starting transfers between devices, permute_gather(): received.append(lax.ppermute(piece, name, pairs))  11.7 us
    all_to_all x1, starting transfers between devices, local(): attended = lax.all_to_all(result, ('chan', 'px'), 0, 0, tiled=True)  8.79 us
    convert_element_type x1, local copies, waits for them, and re-layouts, local(): weight = jnp.exp(score - block_max[..., None]).astype(jnp.bfloat16)  6.86 us
    another operation x2, local copies, waits for them, and re-layouts, local(): stale_k = stacked[0].reshape(slab_count, rows_here, HEAD_DIM)  6.07 us
    dot_general x1, matrix products, local(): jnp.einsum('qsk,skd->qsd', weight, stale_v, preferred_element_type=jnp.fl...  5.19 us
  transfers between devices with their start and end apart: 8, of which 3 were waited for; matrix products, arithmetic and copies ran while one was open for 23% of the time, Pallas kernels for 0%

profile of v7, /device:TPU:1, one launch (start us, length us, event | category | flops | bytes accessed | tf_op | source)
XLA Modules:
  0.0 159.1 jit_solution(9288006474996083003)
XLA Ops:
  7.2 1.0 copy.81
  8.2 0.9 copy.82
  9.2 0.8 reshape.337
  10.0 4.8 %all-to-all-start.1 = ((bf16[4,2,4096]{2,1,0:T(2,128)(2,1)}), bf16[4,2,4096]{2,1,0:T(2,128)(2,1)S(1)}, u32[]{:S(2)}, u32[]{:S(2)}) async-start(bf16[4,2,4096]{2,1,0:T(2,128)(2,1)} %reshape.337), calls=%async_computation.1 | async-start | bytes 131072 | tf_op jit(solution)/shard_map/all_to_all | solution.py:96
  14.8 0.8 convert_reduce_fusion.1
  15.7 0.1 reduce_sum.153
  16.0 0.8 fusion.4
  16.9 0.1 reduce_sum.156
  17.0 8.2 %all-gather.3 = f32[4,2,8]{2,1,0:T(2,128)S(1)} all-gather(f32[1,2,8]{2,1,0:T(2,128)S(1)} %maximum_bitcast_fusion), channel_id=2, replica_groups=mesh['py'=8,'pz'=4,'px'=4,'chan'=4] {'px'}, dimensions={0}, use_global_device_ids=true | all-gather | bytes 320 | tf_op jit(solution)/shard_map/all_gather | solution.py:70
  25.3 0.1 reshape.338
  25.5 0.1 copy.83
  25.6 0.1 reshape.305
  25.8 3.7 %collective-permute-start = (bf16[2,256,64]{1,2,0:T(8,128)(2,1)S(1)}, bf16[2,256,64]{1,2,0:T(8,128)(2,1)S(1)}, u32[]{:S(2)}, u32[]{:S(2)}) collective-permute-start(bf16[2,256,64]{1,2,0:T(8,128)(2,1)S(1)} %reshape.305), channel_id=1, source_target_pairs={{0,16},{16,32},{32,48},{48,0},{1,17},{17,33},{33,49},{49,1},{2,18}... | collective-permute-start | bytes 196616 | tf_op jit(solution)/shard_map/ppermute | solution.py:38
  29.4 5.8 %collective-permute-start.1 = (bf16[2,256,64]{1,2,0:T(8,128)(2,1)S(1)}, bf16[2,256,64]{1,2,0:T(8,128)(2,1)S(1)}, u32[]{:S(2)}, u32[]{:S(2)}) collective-permute-start(bf16[2,256,64]{1,2,0:T(8,128)(2,1)S(1)} %reshape.305), channel_id=1, source_target_pairs={{0,32},{16,48},{32,0},{48,16},{1,33},{17,49},{33,1},{49,17},{2,34}... | collective-permute-start | bytes 196616 | tf_op jit(solution)/shard_map/ppermute | solution.py:38
  35.3 2.2 %collective-permute-start.2 = (bf16[2,256,64]{1,2,0:T(8,128)(2,1)S(1)}, bf16[2,256,64]{1,2,0:T(8,128)(2,1)S(1)}, u32[]{:S(2)}, u32[]{:S(2)}) collective-permute-start(bf16[2,256,64]{1,2,0:T(8,128)(2,1)S(1)} %reshape.305), channel_id=1, source_target_pairs={{0,48},{16,0},{32,16},{48,32},{1,49},{17,1},{33,17},{49,33},{2,50}... | collective-permute-start | bytes 196616 | tf_op jit(solution)/shard_map/ppermute | solution.py:38
  37.5 0.1 stack_reshape.3
  37.6 4.1 %collective-permute-done.2 = bf16[2,256,64]{1,2,0:T(8,128)(2,1)S(1)} collective-permute-done((bf16[2,256,64]{1,2,0:T(8,128)(2,1)S(1)}, bf16[2,256,64]{1,2,0:T(8,128)(2,1)S(1)}, u32[]{:S(2)}, u32[]{:S(2)}) %collective-permute-start.2) | collective-permute-done | bytes 65568 | tf_op jit(solution)/shard_map/ppermute | solution.py:38
  41.8 0.6 gather_fusion
  42.4 0.1 select_bitcast_fusion
  42.5 0.8 copy.100
  43.3 6.4 %all-gather.4 = f32[4,2,8]{2,1,0:T(2,128)S(1)} all-gather(f32[1,2,8]{2,1,0:T(2,128)S(1)} %maximum_bitcast_fusion.1), channel_id=3, replica_groups=mesh['py'=8,'pz'=4,'px'=4,'chan'=4] {'pz'}, dimensions={0}, use_global_device_ids=true | all-gather | bytes 320 | tf_op jit(solution)/shard_map/all_gather | solution.py:70
  49.8 13.1 %all-gather.5 = f32[8,2,8]{2,1,0:T(2,128)S(1)} all-gather(f32[1,2,8]{2,1,0:T(2,128)S(1)} %maximum_bitcast_fusion.2), channel_id=4, replica_groups=mesh['py'=8,'pz'=4,'px'=4,'chan'=4] {'py'}, dimensions={0}, use_global_device_ids=true | all-gather | bytes 576 | tf_op jit(solution)/shard_map/all_gather | solution.py:70
  64.1 0.2 convolution_reduce_fusion
  64.4 21.7 %all-gather.6 = bf16[4,320,64]{1,2,0:T(8,128)(2,1)S(1)} all-gather(bf16[1,320,64]{1,2,0:T(8,128)(2,1)S(1)} %fusion.15), channel_id=1, replica_groups=mesh['py'=8,'pz'=4,'px'=4,'chan'=4] {'chan'}, dimensions={0}, use_global_device_ids=true | all-gather | bytes 204800 | tf_op jit(solution)/shard_map/all_gather | solution.py:82
  86.1 0.2 copy.76
  86.3 0.2 reshape.327
  86.4 0.2 convolution_convert_fusion.2
  86.7 0.1 stack.54
  86.8 0.2 convolution_convert_fusion.1
  87.1 0.1 stack.55
  87.2 0.2 convolution_convert_fusion
  87.5 0.1 stack.56
  87.7 0.8 reshape.335
  88.5 3.3 %all-to-all-start = ((bf16[4,2,6144]{2,1,0:T(2,128)(2,1)}), bf16[4,2,6144]{2,1,0:T(2,128)(2,1)S(1)}, u32[]{:S(2)}, u32[]{:S(2)}) async-start(bf16[4,2,6144]{2,1,0:T(2,128)(2,1)} %reshape.335), calls=%async_computation | async-start | bytes 196608 | tf_op jit(solution)/shard_map/all_to_all | solution.py:106
  91.8 0.2 all-gather.12.cloned.1.call-start
  92.0 0.5 all-gather.12.cloned.1.call-update
  92.6 0.1 iota_compare_fusion
  92.7 0.1 copy.89
  92.8 3.6 %all-to-all-done = bf16[4,2,6144]{2,1,0:T(2,128)(2,1)S(1)} async-done(((bf16[4,2,6144]{2,1,0:T(2,128)(2,1)}), bf16[4,2,6144]{2,1,0:T(2,128)(2,1)S(1)}, u32[]{:S(2)}, u32[]{:S(2)}) %all-to-all-start) | async-done | bytes 98336 | tf_op jit(solution)/shard_map/all_to_all | solution.py:106
  96.4 0.2 reshape.336
  96.7 0.2 fusion.28
  97.0 0.2 fusion.13
  97.3 0.1 copy.91
  97.4 1.7 %fusion.26 = (bf16[1,8192,64]{1,2,0:T(8,128)(2,1)S(1)}, bf16[1,8192,64]{1,2,0:T(8,128)(2,1)S(1)}) fusion(bf16[2,8192,64]{1,2,0:T(8,128)(2,1)} %all-gather.10.cloned.1.call-done), kind=kLoop, calls=%fused_computation.88 | loop fusion | bytes 4194304 | tf_op jit(solution)/shard_map/slice | solution.py:101
  99.1 3.3 %reshape_squeeze.10 = bf16[128,64,64]{1,0,2:T(8,128)(2,1)} reshape(bf16[1,8192,64]{1,2,0:T(8,128)(2,1)S(1)} %get-tuple-element.12) | data formatting | bytes 2097152 | tf_op jit(solution)/shard_map/reshape;squeeze | solution.py:100
  102.4 2.8 %copy.87 = bf16[128,64,64]{0,2,1:T(8,128)(2,1)S(1)} copy(bf16[128,64,64]{1,0,2:T(8,128)(2,1)} %reshape_squeeze.10) | data formatting | bytes 2097152 | tf_op jit(solution)/shard_map/reshape;squeeze | solution.py:100
  105.2 1.2 multiply_reduce_fusion
  106.4 3.1 %convert_reduce_fusion = (f32[256,128]{1,0:T(8,128)S(1)}, bf16[256,128,64]{1,0,2:T(8,128)(2,1)}) fusion(f32[256,128]{1,0:T(8,128)S(1)} %get-tuple-element.25, f32[256,128,64]{1,0,2:T(8,128)S(1)} %get-tuple-element.26), kind=kLoop, calls=%fused_computation.4 | loop fusion | flops 10452992 | bytes 12845056 | tf_op jit(solution)/shard_map/reduce_sum | solution.py:116
  109.5 6.9 %copy.93 = bf16[256,128,64]{0,2,1:T(8,128)(2,1)} copy(bf16[256,128,64]{1,0,2:T(8,128)(2,1)} %get-tuple-element.10) | data formatting | bytes 8388608 | tf_op jit(solution)/shard_map/convert_element_type | solution.py:114
  116.4 0.2 fusion.12
  116.6 0.3 multiply_reduce_fusion.1
  116.9 0.1 copy.88
  117.0 3.3 %reshape_squeeze.11 = bf16[128,64,64]{1,0,2:T(8,128)(2,1)} reshape(bf16[1,8192,64]{1,2,0:T(8,128)(2,1)S(1)} %get-tuple-element.11) | data formatting | bytes 2097152 | tf_op jit(solution)/shard_map/reshape;squeeze | solution.py:101
  120.3 5.2 %fusion.1 = f32[256,64]{0,1:T(8,128)S(1)} fusion(f32[256,64]{0,1:T(8,128)S(1)} %copy.91, f32[256,128]{0,1:T(8,128)S(1)} %copy.88, pred[256,128]{0,1:T(8,128)(4,1)S(1)} %copy.89, bf16[256,128,64]{0,2,1:T(8,128)(2,1)} %copy.93, bf16[128,64,64]{1,0,2:T(8,128)(2,1)} %reshape_squeeze.11), kind=kOutput, calls=%fused_computation.3 | convolution fusion | flops 274710528 | bytes 5537792 | tf_op jit(solution)/shard_map/qsk,skd->qsd/dot_general | solution.py:115
  125.5 0.1 reduce_sum.167
  125.7 0.1 copy.94
  125.9 0.9 reshape.339
  126.8 8.8 %all-to-all-start.2 = ((bf16[16,2,2048]{2,1,0:T(2,128)(2,1)}), bf16[16,2,2048]{2,1,0:T(2,128)(2,1)S(1)}, u32[]{:S(2)}, u32[]{:S(2)}) async-start(bf16[16,2,2048]{2,1,0:T(2,128)(2,1)} %reshape.339), calls=%async_computation.2 | async-start | bytes 262144 | tf_op jit(solution)/shard_map/all_to_all | solution.py:145
  135.6 13.0 %all-to-all-done.2 = bf16[16,2,2048]{2,1,0:T(2,128)(2,1)S(1)} async-done(((bf16[16,2,2048]{2,1,0:T(2,128)(2,1)}), bf16[16,2,2048]{2,1,0:T(2,128)(2,1)S(1)}, u32[]{:S(2)}, u32[]{:S(2)}) %all-to-all-start.2) | async-done | bytes 131104 | tf_op jit(solution)/shard_map/all_to_all | solution.py:145
  148.6 0.2 reshape.340
  148.8 0.2 copy.95
  149.0 0.2 reshape.308
  149.2 2.3 %fusion.31 = f32[64,1280]{1,0:T(8,128)S(1)} fusion(bf16[64,1024]{1,0:T(8,128)(2,1)S(1)} %reshape.308, bf16[1024,1280]{1,0:T(8,128)(2,1)} %all-gather.12.cloned.1.call-done), kind=kOutput, calls=%fused_computation.94 | convolution fusion | flops 167772160 | bytes 3080192 | tf_op jit(solution)/shard_map/dot_general | solution.py:148
  151.5 0.7 fusion.10
  (73 shorter events, 1.7 us)
Async XLA Ops:
  7.2 79.3 %copy-start = (bf16[1280,256]{1,0:T(8,128)(2,1)S(1)}, bf16[1280,256]{1,0:T(8,128)(2,1)}, u32[]{:S(2)}) copy-start(bf16[1280,256]{1,0:T(8,128)(2,1)} %param.16) | copy-start | bytes 1966084
  7.2 57.1 %copy-start.1 = (bf16[64,320]{1,0:T(8,128)(2,1)S(1)}, bf16[64,320]{1,0:T(8,128)(2,1)}, u32[]{:S(2)}) copy-start(bf16[64,320]{1,0:T(8,128)(2,1)} %param.11) | copy-start | bytes 122884
  7.2 56.9 %copy-start.4 = (bf16[320,320]{1,0:T(8,128)(2,1)S(1)}, bf16[320,320]{1,0:T(8,128)(2,1)}, u32[]{:S(2)}) copy-start(bf16[320,320]{1,0:T(8,128)(2,1)} %param.15) | copy-start | bytes 614404
  7.2 57.1 %copy-start.8 = (f32[320]{0:T(512)S(1)}, f32[320]{0:T(512)}, u32[]{:S(2)}) copy-start(f32[320]{0:T(512)} %param.13) | copy-start | bytes 3844
  7.2 57.1 %copy-start.7 = (f32[320]{0:T(512)S(1)}, f32[320]{0:T(512)}, u32[]{:S(2)}) copy-start(f32[320]{0:T(512)} %param.14) | copy-start | bytes 3844
  7.2 79.6 %copy-start.2 = (bf16[1280,256]{1,0:T(8,128)(2,1)S(1)}, bf16[1280,256]{1,0:T(8,128)(2,1)}, u32[]{:S(2)}) copy-start(bf16[1280,256]{1,0:T(8,128)(2,1)} %param.17) | copy-start | bytes 1966084
  9.1 78.1 %copy-start.3 = (bf16[1280,256]{1,0:T(8,128)(2,1)S(1)}, bf16[1280,256]{1,0:T(8,128)(2,1)}, u32[]{:S(2)}) copy-start(bf16[1280,256]{1,0:T(8,128)(2,1)} %param.18) | copy-start | bytes 1966084
  10.0 15.4 %all-to-all-start.1 = ((bf16[4,2,4096]{2,1,0:T(2,128)(2,1)}), bf16[4,2,4096]{2,1,0:T(2,128)(2,1)S(1)}, u32[]{:S(2)}, u32[]{:S(2)}) async-start(bf16[4,2,4096]{2,1,0:T(2,128)(2,1)} %reshape.337), calls=%async_computation.1 | async-start | bytes 131072 | tf_op jit(solution)/shard_map/all_to_all | solution.py:96
  14.8 82.6 %all-gather.10.cloned.1.call-start = ((), (), s32[]{:S(2)}) async-start(), calls=%async_computation.3 | async-start | bytes 2359296 | tf_op jit(solution)/shard_map/all_gather | solution.py:98
  25.8 11.8 %collective-permute-start = (bf16[2,256,64]{1,2,0:T(8,128)(2,1)S(1)}, bf16[2,256,64]{1,2,0:T(8,128)(2,1)S(1)}, u32[]{:S(2)}, u32[]{:S(2)}) collective-permute-start(bf16[2,256,64]{1,2,0:T(8,128)(2,1)S(1)} %reshape.305), channel_id=1, source_target_pairs={{0,16},{16,32},{32,48},{48,0},{1,17},{17,33},{33,49},{49,1},{2,18}... | collective-permute-start | bytes 196616 | tf_op jit(solution)/shard_map/ppermute | solution.py:38
  29.4 8.2 %collective-permute-start.1 = (bf16[2,256,64]{1,2,0:T(8,128)(2,1)S(1)}, bf16[2,256,64]{1,2,0:T(8,128)(2,1)S(1)}, u32[]{:S(2)}, u32[]{:S(2)}) collective-permute-start(bf16[2,256,64]{1,2,0:T(8,128)(2,1)S(1)} %reshape.305), channel_id=1, source_target_pairs={{0,32},{16,48},{32,0},{48,16},{1,33},{17,49},{33,1},{49,17},{2,34}... | collective-permute-start | bytes 196616 | tf_op jit(solution)/shard_map/ppermute | solution.py:38
  35.3 6.5 %collective-permute-start.2 = (bf16[2,256,64]{1,2,0:T(8,128)(2,1)S(1)}, bf16[2,256,64]{1,2,0:T(8,128)(2,1)S(1)}, u32[]{:S(2)}, u32[]{:S(2)}) collective-permute-start(bf16[2,256,64]{1,2,0:T(8,128)(2,1)S(1)} %reshape.305), channel_id=1, source_target_pairs={{0,48},{16,0},{32,16},{48,32},{1,49},{17,1},{33,17},{49,33},{2,50}... | collective-permute-start | bytes 196616 | tf_op jit(solution)/shard_map/ppermute | solution.py:38
  87.1 12.0 %copy-start.5 = (bf16[64,256]{1,0:T(8,128)(2,1)}, bf16[64,256]{1,0:T(8,128)(2,1)S(1)}, u32[]{:S(2)}) copy-start(bf16[64,256]{1,0:T(8,128)(2,1)S(1)} %convolution_convert_fusion.1) | copy-start | bytes 98308
  87.5 15.0 %copy-start.6 = (bf16[64,256]{1,0:T(8,128)(2,1)}, bf16[64,256]{1,0:T(8,128)(2,1)S(1)}, u32[]{:S(2)}) copy-start(bf16[64,256]{1,0:T(8,128)(2,1)S(1)} %convolution_convert_fusion) | copy-start | bytes 98308
  88.5 7.9 %all-to-all-start = ((bf16[4,2,6144]{2,1,0:T(2,128)(2,1)}), bf16[4,2,6144]{2,1,0:T(2,128)(2,1)S(1)}, u32[]{:S(2)}, u32[]{:S(2)}) async-start(bf16[4,2,6144]{2,1,0:T(2,128)(2,1)} %reshape.335), calls=%async_computation | async-start | bytes 196608 | tf_op jit(solution)/shard_map/all_to_all | solution.py:106
  91.8 57.4 %all-gather.12.cloned.1.call-start = ((), (), s32[]{:S(2)}) async-start(), calls=%async_computation.4 | async-start | bytes 3276800 | tf_op jit(solution)/shard_map/all_gather | solution.py:147
  126.8 21.8 %all-to-all-start.2 = ((bf16[16,2,2048]{2,1,0:T(2,128)(2,1)}), bf16[16,2,2048]{2,1,0:T(2,128)(2,1)S(1)}, u32[]{:S(2)}, u32[]{:S(2)}) async-start(bf16[16,2,2048]{2,1,0:T(2,128)(2,1)} %reshape.339), calls=%async_computation.2 | async-start | bytes 262144 | tf_op jit(solution)/shard_map/all_to_all | solution.py:145
Sparse Core Ops, SparseCore 0:
  43.3 41.7 all-gather.9
  94.7 53.4 all-gather.11

commit v8 on v7

--- a/solution.py
+++ b/solution.py
@@ -97,8 +97,6 @@
     stacked = permute_gather(stacked, "pz")
     stacked = lax.all_gather(stacked, "py", axis=1, tiled=True)
     slab_count = stacked.shape[1] // rows_here
-    stale_k = stacked[0].reshape(slab_count, rows_here, HEAD_DIM)
-    stale_v = stacked[1].reshape(slab_count, rows_here, HEAD_DIM)
 
     fresh = jnp.stack([queries, fresh_keys, fresh_values]).reshape(
         3, rows_here, heads_here, HEAD_DIM
@@ -106,14 +104,14 @@
     fresh = lax.all_to_all(fresh, "px", 2, 1, tiled=True).reshape(3, split, rows_here, HEAD_DIM)
     query_rows = fresh[0].reshape(split * rows_here, HEAD_DIM)
 
+    key_rows = stacked[0]
+    value_rows = stacked[1]
     score = (
-        jnp.einsum("qd,skd->qsk", query_rows, stale_k, preferred_element_type=jnp.float32)
+        jnp.einsum("kd,qd->kq", key_rows, query_rows, preferred_element_type=jnp.float32)
         * score_scale
-    )
-    block_max = jnp.max(score, axis=-1)
-    weight = jnp.exp(score - block_max[..., None]).astype(jnp.bfloat16)
-    block_num = jnp.einsum("qsk,skd->qsd", weight, stale_v, preferred_element_type=jnp.float32)
-    block_den = jnp.sum(weight.astype(jnp.float32), axis=-1)
+    ).reshape(slab_count, rows_here, split * rows_here)
+    block_max = jnp.max(score, axis=1)
+    weight = jnp.exp(score - block_max[:, None, :]).astype(jnp.bfloat16).astype(jnp.float32)
 
     home_score = (
         jnp.einsum("gqd,gkd->gqk", fresh[0], fresh[1], preferred_element_type=jnp.float32)
@@ -123,21 +121,25 @@
     home_weight = jnp.exp(home_score - home_max[..., None]).astype(jnp.bfloat16)
     home_num = jnp.einsum("gqk,gkd->gqd", home_weight, fresh[2], preferred_element_type=jnp.float32)
     home_den = jnp.sum(home_weight.astype(jnp.float32), axis=-1)
-    home_max = home_max.reshape(split * rows_here, 1)
-    home_num = home_num.reshape(split * rows_here, 1, HEAD_DIM)
-    home_den = home_den.reshape(split * rows_here, 1)
+    home_max = home_max.reshape(split * rows_here)
+    home_num = home_num.reshape(split * rows_here, HEAD_DIM)
+    home_den = home_den.reshape(split * rows_here)
 
     first_slab = (device // split) * split
     query_slab = first_slab + jnp.arange(split * rows_here, dtype=jnp.int32) // rows_here
-    is_home = query_slab[:, None] == jnp.arange(slab_count, dtype=jnp.int32)[None, :]
-    block_max = jnp.where(is_home, home_max, block_max)
-    block_den = jnp.where(is_home, home_den, block_den)
-    block_num = jnp.where(is_home[..., None], home_num, block_num)
-
-    top = jnp.max(block_max, axis=-1)
-    factor = jnp.exp(block_max - top[:, None])
-    numer = jnp.sum(factor[..., None] * block_num, axis=1)
-    denom = jnp.sum(factor * block_den, axis=1)
+    is_home = jnp.arange(slab_count, dtype=jnp.int32)[:, None] == query_slab[None, :]
+    block_max = jnp.where(is_home, home_max[None, :], block_max)
+    top = jnp.max(block_max, axis=0)
+    factor = jnp.exp(block_max - top[None, :])
+    stale_factor = jnp.where(is_home, 0.0, factor)
+    scaled_weight = (weight * stale_factor[:, None, :]).reshape(slab_count * rows_here, split * rows_here)
+    stale_den = jnp.sum(scaled_weight, axis=0)
+    stale_num = jnp.einsum(
+        "kd,kq->qd", value_rows, scaled_weight.astype(jnp.bfloat16), preferred_element_type=jnp.float32
+    )
+    home_factor = jnp.exp(home_max - top)
+    numer = stale_num + home_factor[:, None] * home_num
+    denom = stale_den + home_factor * home_den
     result = (numer / denom[:, None]).astype(jnp.bfloat16)
     result = result.reshape(1, split, rows_here, HEAD_DIM)
     result = jnp.broadcast_to(result, (chan_count, split, rows_here, HEAD_DIM))

time: 160 us -> 150 us (0.938)
  local copies, waits for them, and re-layouts: 27.1 us -> 8.76 us
  waiting for transfers between devices: 21.3 us -> 36.2 us
  matrix products: 10.1 us -> 7.1 us
  other arithmetic: 7.04 us -> 4.05 us
    all_gather x1, waiting for transfers between devices: 0.02 us -> 11.2 us  [local(): out_rows = lax.all_gather(w_out, 'chan', axis=0, tiled=True)]
    another operation x3 -> x0, local copies, waits for them, and re-layouts: 9.37 us -> none  [the longest x2 6.07 us: local(): stale_k = stacked[0].reshape(slab_count, rows_here, HEAD_DIM)]
    convert_element_type x2 -> x0, local copies, waits for them, and re-layouts: 6.97 us -> none  [the longest x1 6.86 us: local(): weight = jnp.exp(score - block_max[..., None]).astype(jnp.bfloat16)]
    all_to_all x1, waiting for transfers between devices: 0.01 us -> 4.44 us  [local(): lax.all_to_all(stacked, 'px', 2, 1, tiled=True)]
    dot_general x2, matrix products: 6.43 us -> 3.46 us  [the longest x1 2.66 us: local(): jnp.einsum('kd,qd->kq', key_rows, query_rows, preferred_element_type=jnp....]
    slice x2 -> x1, local copies, waits for them, and re-layouts: 1.68 us -> 0.01 us  [local(): query_rows = fresh[0].reshape(split * rows_here, HEAD_DIM)]
    reduce_sum x2 -> x1, other arithmetic: 3.38 us -> 2.23 us  [local(): stale_den = jnp.sum(scaled_weight, axis=0)]
    unnamed x27 -> x29, local copies, waits for them, and re-layouts: 5.15 us -> 5.12 us
  transfers between devices with their start and end apart: 8 -> 8, of which waited for: 3 -> 5; matrix products, arithmetic and copies ran while one was open for 23% -> 8% of each run, Pallas kernels for 0% -> 0%
where the time goes in v8:
time: 150 us; the launch traced here: 149 us
  blocking collectives  48.9 us (33%)
  waiting for transfers between devices  36.2 us (24%)
  starting transfers between devices  28.9 us (19%)
  between operations  15.2 us (10%)
  local copies, waits for them, and re-layouts  8.76 us (6%)
  matrix products  7.1 us (5%)
  other arithmetic  4.05 us (3%)
    all_gather x3, blocking collectives, local(): gathered = lax.all_gather(jnp.stack([group_mean, spread]), name)  27.6 us
    all_gather x1, blocking collectives, local(): shard_piece = lax.all_gather(normed, 'chan', axis=1, tiled=True)  21.3 us
    ppermute x3, starting transfers between devices, permute_gather(): received.append(lax.ppermute(piece, name, pairs))  12 us
    all_to_all x1, waiting for transfers between devices, local(): attended = lax.all_to_all(result, ('chan', 'px'), 0, 0, tiled=True)  11.9 us
    all_gather x1, waiting for transfers between devices, local(): out_rows = lax.all_gather(w_out, 'chan', axis=0, tiled=True)  11.2 us
    all_to_all x1, starting transfers between devices, local(): attended = lax.all_to_all(result, ('chan', 'px'), 0, 0, tiled=True)  8.75 us
    unnamed x29, local copies, waits for them, and re-layouts  5.12 us
    all_to_all x1, starting transfers between devices, local(): lax.all_to_all(stacked, 'px', 2, 1, tiled=True)  4.83 us
  transfers between devices with their start and end apart: 8, of which 5 were waited for; matrix products, arithmetic and copies ran while one was open for 8% of the time, Pallas kernels for 0%

profile of v8, /device:TPU:1, one launch (start us, length us, event | category | flops | bytes accessed | tf_op | source)
XLA Modules:
  0.0 149.1 jit_solution(7936458992009665535)
XLA Ops:
  7.2 1.0 copy.45
  8.2 0.9 copy.46
  9.1 0.8 reshape.327
  9.9 4.8 %all-to-all-start = ((bf16[4,2,4096]{2,1,0:T(2,128)(2,1)}), bf16[4,2,4096]{2,1,0:T(2,128)(2,1)S(1)}, u32[]{:S(2)}, u32[]{:S(2)}) async-start(bf16[4,2,4096]{2,1,0:T(2,128)(2,1)} %reshape.327), calls=%async_computation | async-start | bytes 131072 | tf_op jit(solution)/shard_map/all_to_all | solution.py:96
  14.8 4.4 %all-to-all-done = bf16[4,2,4096]{2,1,0:T(2,128)(2,1)S(1)} async-done(((bf16[4,2,4096]{2,1,0:T(2,128)(2,1)}), bf16[4,2,4096]{2,1,0:T(2,128)(2,1)S(1)}, u32[]{:S(2)}, u32[]{:S(2)}) %all-to-all-start) | async-done | bytes 65568 | tf_op jit(solution)/shard_map/all_to_all | solution.py:96
  19.2 0.1 reshape.328
  19.4 0.1 copy.47
  19.5 0.1 reshape.293
  19.7 4.0 %collective-permute-start = (bf16[2,256,64]{1,2,0:T(8,128)(2,1)S(1)}, bf16[2,256,64]{1,2,0:T(8,128)(2,1)S(1)}, u32[]{:S(2)}, u32[]{:S(2)}) collective-permute-start(bf16[2,256,64]{1,2,0:T(8,128)(2,1)S(1)} %reshape.293), channel_id=1, source_target_pairs={{0,16},{16,32},{32,48},{48,0},{1,17},{17,33},{33,49},{49,1},{2,18}... | collective-permute-start | bytes 196616 | tf_op jit(solution)/shard_map/ppermute | solution.py:38
  23.7 5.8 %collective-permute-start.1 = (bf16[2,256,64]{1,2,0:T(8,128)(2,1)S(1)}, bf16[2,256,64]{1,2,0:T(8,128)(2,1)S(1)}, u32[]{:S(2)}, u32[]{:S(2)}) collective-permute-start(bf16[2,256,64]{1,2,0:T(8,128)(2,1)S(1)} %reshape.293), channel_id=1, source_target_pairs={{0,32},{16,48},{32,0},{48,16},{1,33},{17,49},{33,1},{49,17},{2,34}... | collective-permute-start | bytes 196616 | tf_op jit(solution)/shard_map/ppermute | solution.py:38
  29.5 2.2 %collective-permute-start.2 = (bf16[2,256,64]{1,2,0:T(8,128)(2,1)S(1)}, bf16[2,256,64]{1,2,0:T(8,128)(2,1)S(1)}, u32[]{:S(2)}, u32[]{:S(2)}) collective-permute-start(bf16[2,256,64]{1,2,0:T(8,128)(2,1)S(1)} %reshape.293), channel_id=1, source_target_pairs={{0,48},{16,0},{32,16},{48,32},{1,49},{17,1},{33,17},{49,33},{2,50}... | collective-permute-start | bytes 196616 | tf_op jit(solution)/shard_map/ppermute | solution.py:38
  31.7 0.1 stack_reshape.3
  31.9 3.4 %collective-permute-done.2 = bf16[2,256,64]{1,2,0:T(8,128)(2,1)S(1)} collective-permute-done((bf16[2,256,64]{1,2,0:T(8,128)(2,1)S(1)}, bf16[2,256,64]{1,2,0:T(8,128)(2,1)S(1)}, u32[]{:S(2)}, u32[]{:S(2)}) %collective-permute-start.2) | collective-permute-done | bytes 65568 | tf_op jit(solution)/shard_map/ppermute | solution.py:38
  35.3 0.6 gather_fusion
  35.8 0.1 select_bitcast_fusion
  35.9 0.7 copy.64
  36.7 0.0 all-gather.12.cloned.1.call-start
  36.7 0.7 all-gather.12.cloned.1.call-update
  37.5 0.1 reduce_sum.132
  37.6 0.1 reduce_sum.133
  37.7 0.1 sub.124
  37.8 0.1 sub.125
  37.9 0.1 reduce_sum.135
  38.0 0.1 reduce_sum.136
  38.1 6.1 %all-gather.3 = f32[4,2,8]{2,1,0:T(2,128)S(1)} all-gather(f32[1,2,8]{2,1,0:T(2,128)S(1)} %maximum_bitcast_fusion), channel_id=2, replica_groups=mesh['py'=8,'pz'=4,'px'=4,'chan'=4] {'px'}, dimensions={0}, use_global_device_ids=true | all-gather | bytes 320 | tf_op jit(solution)/shard_map/all_gather | solution.py:70
  44.3 7.2 %all-gather.4 = f32[4,2,8]{2,1,0:T(2,128)S(1)} all-gather(f32[1,2,8]{2,1,0:T(2,128)S(1)} %maximum_bitcast_fusion.1), channel_id=3, replica_groups=mesh['py'=8,'pz'=4,'px'=4,'chan'=4] {'pz'}, dimensions={0}, use_global_device_ids=true | all-gather | bytes 320 | tf_op jit(solution)/shard_map/all_gather | solution.py:70
  51.6 14.2 %all-gather.5 = f32[8,2,8]{2,1,0:T(2,128)S(1)} all-gather(f32[1,2,8]{2,1,0:T(2,128)S(1)} %maximum_bitcast_fusion.2), channel_id=4, replica_groups=mesh['py'=8,'pz'=4,'px'=4,'chan'=4] {'py'}, dimensions={0}, use_global_device_ids=true | all-gather | bytes 576 | tf_op jit(solution)/shard_map/all_gather | solution.py:70
  65.9 0.1 mul.129
  66.0 0.1 mul.130
  66.1 0.1 sub.132
  66.1 0.1 sub.133
  66.9 0.1 divide_multiply_fusion
  67.0 0.2 convolution_reduce_fusion
  67.3 21.3 %all-gather.6 = bf16[4,320,64]{1,2,0:T(8,128)(2,1)S(1)} all-gather(bf16[1,320,64]{1,2,0:T(8,128)(2,1)S(1)} %fusion.18), channel_id=1, replica_groups=mesh['py'=8,'pz'=4,'px'=4,'chan'=4] {'chan'}, dimensions={0}, use_global_device_ids=true | all-gather | bytes 204800 | tf_op jit(solution)/shard_map/all_gather | solution.py:82
  88.6 0.2 copy.51
  88.8 0.2 reshape.318
  89.0 0.2 convolution_convert_fusion.2
  89.2 0.1 stack.61
  89.4 0.2 convolution_convert_fusion.1
  89.6 0.1 stack.62
  89.7 0.2 convolution_convert_fusion
  90.0 0.1 stack.63
  90.2 0.8 reshape.325
  91.0 3.3 %all-to-all-start.1 = ((bf16[4,2,6144]{2,1,0:T(2,128)(2,1)}), bf16[4,2,6144]{2,1,0:T(2,128)(2,1)S(1)}, u32[]{:S(2)}, u32[]{:S(2)}) async-start(bf16[4,2,6144]{2,1,0:T(2,128)(2,1)} %reshape.325), calls=%async_computation.1 | async-start | bytes 196608 | tf_op jit(solution)/shard_map/all_to_all | solution.py:104
  94.4 4.6 %all-to-all-done.1 = bf16[4,2,6144]{2,1,0:T(2,128)(2,1)S(1)} async-done(((bf16[4,2,6144]{2,1,0:T(2,128)(2,1)}), bf16[4,2,6144]{2,1,0:T(2,128)(2,1)S(1)}, u32[]{:S(2)}, u32[]{:S(2)}) %all-to-all-start.1) | async-done | bytes 98336 | tf_op jit(solution)/shard_map/all_to_all | solution.py:104
  99.0 0.2 reshape.326
  99.2 0.2 fusion.30
  99.4 0.1 broadcast_in_dim.31
  99.5 0.1 reshape.297
  99.6 0.2 fusion.16
  99.8 0.1 copy.61
  99.9 2.7 %bitcast_reduce_fusion = (f32[128,256]{1,0:T(8,128)S(1)}, f32[8192,256]{1,0:T(8,128)S(1)}) fusion(bf16[256,64]{1,0:T(8,128)(2,1)S(1)} %bitcast.121, bf16[2,8192,64]{1,2,0:T(8,128)(2,1)} %all-gather.10.cloned.1.call-done), kind=kOutput, calls=%fused_computation.6 | convolution fusion | flops 272596992 | bytes 9601024 | tf_op jit(solution)/shard_map/kd,qd->kq/dot_general | solution.py:110
  102.7 2.2 %fusion.2 = (f32[256]{0:T(256)S(1)}, bf16[8192,256]{1,0:T(8,128)(2,1)S(1)}) fusion(f32[128,256]{1,0:T(8,128)S(1)} %exponential_select_fusion, f32[8192,256]{1,0:T(8,128)S(1)} %get-tuple-element.22, f32[128,256]{1,0:T(8,128)S(1)} %get-tuple-element.21), kind=kLoop, calls=%fused_computation.7 | loop fusion | flops 12582656 | bytes 12846080 | tf_op jit(solution)/shard_map/reduce_sum | solution.py:136
  105.0 0.8 fusion.5
  105.8 0.1 copy.62
  106.0 0.9 reshape.329
  106.8 8.8 %all-to-all-start.2 = ((bf16[16,2,2048]{2,1,0:T(2,128)(2,1)}), bf16[16,2,2048]{2,1,0:T(2,128)(2,1)S(1)}, u32[]{:S(2)}, u32[]{:S(2)}) async-start(bf16[16,2,2048]{2,1,0:T(2,128)(2,1)} %reshape.329), calls=%async_computation.2 | async-start | bytes 262144 | tf_op jit(solution)/shard_map/all_to_all | solution.py:147
  115.6 11.9 %all-to-all-done.2 = bf16[16,2,2048]{2,1,0:T(2,128)(2,1)S(1)} async-done(((bf16[16,2,2048]{2,1,0:T(2,128)(2,1)}), bf16[16,2,2048]{2,1,0:T(2,128)(2,1)S(1)}, u32[]{:S(2)}, u32[]{:S(2)}) %all-to-all-start.2) | async-done | bytes 131104 | tf_op jit(solution)/shard_map/all_to_all | solution.py:147
  127.5 0.2 reshape.330
  127.7 0.2 copy.59
  127.9 0.2 reshape.299
  128.1 11.2 %all-gather.12.cloned.1.call-done = bf16[1024,1280]{1,0:T(8,128)(2,1)} async-done(((bf16[256,1280]{1,0:T(8,128)(2,1)}), bf16[1024,1280]{1,0:T(8,128)(2,1)}) %all-gather.12.cloned.1.call-update) | async-done | bytes 2621456 | tf_op jit(solution)/shard_map/all_gather | solution.py:149
  139.3 2.3 %fusion.33 = f32[64,1280]{1,0:T(8,128)S(1)} fusion(bf16[64,1024]{1,0:T(8,128)(2,1)S(1)} %reshape.299, bf16[1024,1280]{1,0:T(8,128)(2,1)} %all-gather.12.cloned.1.call-done), kind=kOutput, calls=%fused_computation.99 | convolution fusion | flops 167772160 | bytes 3080192 | tf_op jit(solution)/shard_map/dot_general | solution.py:150
  141.6 0.7 fusion.15
  (65 shorter events, 0.9 us)
Async XLA Ops:
  7.2 81.8 %copy-start = (bf16[1280,256]{1,0:T(8,128)(2,1)S(1)}, bf16[1280,256]{1,0:T(8,128)(2,1)}, u32[]{:S(2)}) copy-start(bf16[1280,256]{1,0:T(8,128)(2,1)} %param.16) | copy-start | bytes 1966084
  7.2 30.3 %copy-start.2 = (bf16[64,320]{1,0:T(8,128)(2,1)S(1)}, bf16[64,320]{1,0:T(8,128)(2,1)}, u32[]{:S(2)}) copy-start(bf16[64,320]{1,0:T(8,128)(2,1)} %param.11) | copy-start | bytes 122884
  7.2 59.8 %copy-start.5 = (bf16[320,320]{1,0:T(8,128)(2,1)S(1)}, bf16[320,320]{1,0:T(8,128)(2,1)}, u32[]{:S(2)}) copy-start(bf16[320,320]{1,0:T(8,128)(2,1)} %param.15) | copy-start | bytes 614404
  7.2 60.1 %copy-start.9 = (f32[320]{0:T(512)S(1)}, f32[320]{0:T(512)}, u32[]{:S(2)}) copy-start(f32[320]{0:T(512)} %param.13) | copy-start | bytes 3844
  7.2 60.1 %copy-start.8 = (f32[320]{0:T(512)S(1)}, f32[320]{0:T(512)}, u32[]{:S(2)}) copy-start(f32[320]{0:T(512)} %param.14) | copy-start | bytes 3844
  7.2 82.1 %copy-start.3 = (bf16[1280,256]{1,0:T(8,128)(2,1)S(1)}, bf16[1280,256]{1,0:T(8,128)(2,1)}, u32[]{:S(2)}) copy-start(bf16[1280,256]{1,0:T(8,128)(2,1)} %param.17) | copy-start | bytes 1966084
  9.9 9.3 %all-to-all-start = ((bf16[4,2,4096]{2,1,0:T(2,128)(2,1)}), bf16[4,2,4096]{2,1,0:T(2,128)(2,1)S(1)}, u32[]{:S(2)}, u32[]{:S(2)}) async-start(bf16[4,2,4096]{2,1,0:T(2,128)(2,1)} %reshape.327), calls=%async_computation | async-start | bytes 131072 | tf_op jit(solution)/shard_map/all_to_all | solution.py:96
  14.7 85.2 %all-gather.10.cloned.1.call-start = ((), (), s32[]{:S(2)}) async-start(), calls=%async_computation.3 | async-start | bytes 2359296 | tf_op jit(solution)/shard_map/all_gather | solution.py:98
  14.8 75.0 %copy-start.4 = (bf16[1280,256]{1,0:T(8,128)(2,1)S(1)}, bf16[1280,256]{1,0:T(8,128)(2,1)}, u32[]{:S(2)}) copy-start(bf16[1280,256]{1,0:T(8,128)(2,1)} %param.18) | copy-start | bytes 1966084
  19.7 12.2 %collective-permute-start = (bf16[2,256,64]{1,2,0:T(8,128)(2,1)S(1)}, bf16[2,256,64]{1,2,0:T(8,128)(2,1)S(1)}, u32[]{:S(2)}, u32[]{:S(2)}) collective-permute-start(bf16[2,256,64]{1,2,0:T(8,128)(2,1)S(1)} %reshape.293), channel_id=1, source_target_pairs={{0,16},{16,32},{32,48},{48,0},{1,17},{17,33},{33,49},{49,1},{2,18}... | collective-permute-start | bytes 196616 | tf_op jit(solution)/shard_map/ppermute | solution.py:38
  23.7 8.2 %collective-permute-start.1 = (bf16[2,256,64]{1,2,0:T(8,128)(2,1)S(1)}, bf16[2,256,64]{1,2,0:T(8,128)(2,1)S(1)}, u32[]{:S(2)}, u32[]{:S(2)}) collective-permute-start(bf16[2,256,64]{1,2,0:T(8,128)(2,1)S(1)} %reshape.293), channel_id=1, source_target_pairs={{0,32},{16,48},{32,0},{48,16},{1,33},{17,49},{33,1},{49,17},{2,34}... | collective-permute-start | bytes 196616 | tf_op jit(solution)/shard_map/ppermute | solution.py:38
  29.5 5.7 %collective-permute-start.2 = (bf16[2,256,64]{1,2,0:T(8,128)(2,1)S(1)}, bf16[2,256,64]{1,2,0:T(8,128)(2,1)S(1)}, u32[]{:S(2)}, u32[]{:S(2)}) collective-permute-start(bf16[2,256,64]{1,2,0:T(8,128)(2,1)S(1)} %reshape.293), channel_id=1, source_target_pairs={{0,48},{16,0},{32,16},{48,32},{1,49},{17,1},{33,17},{49,33},{2,50}... | collective-permute-start | bytes 196616 | tf_op jit(solution)/shard_map/ppermute | solution.py:38
  36.7 102.6 %all-gather.12.cloned.1.call-start = ((), (), s32[]{:S(2)}) async-start(), calls=%async_computation.4 | async-start | bytes 3276800 | tf_op jit(solution)/shard_map/all_gather | solution.py:149
  89.6 13.0 %copy-start.6 = (bf16[64,256]{1,0:T(8,128)(2,1)}, bf16[64,256]{1,0:T(8,128)(2,1)S(1)}, u32[]{:S(2)}) copy-start(bf16[64,256]{1,0:T(8,128)(2,1)S(1)} %convolution_convert_fusion.1) | copy-start | bytes 98308
  90.0 12.6 %copy-start.7 = (bf16[64,256]{1,0:T(8,128)(2,1)}, bf16[64,256]{1,0:T(8,128)(2,1)S(1)}, u32[]{:S(2)}) copy-start(bf16[64,256]{1,0:T(8,128)(2,1)S(1)} %convolution_convert_fusion) | copy-start | bytes 98308
  91.0 7.9 %all-to-all-start.1 = ((bf16[4,2,6144]{2,1,0:T(2,128)(2,1)}), bf16[4,2,6144]{2,1,0:T(2,128)(2,1)S(1)}, u32[]{:S(2)}, u32[]{:S(2)}) async-start(bf16[4,2,6144]{2,1,0:T(2,128)(2,1)} %reshape.325), calls=%async_computation.1 | async-start | bytes 196608 | tf_op jit(solution)/shard_map/all_to_all | solution.py:104
  102.7 2.3 %copy-start.1 = (bf16[2,8192,64]{1,2,0:T(8,128)(2,1)S(1)}, bf16[2,8192,64]{1,2,0:T(8,128)(2,1)}, u32[]{:S(2)}) copy-start(bf16[2,8192,64]{1,2,0:T(8,128)(2,1)} %all-gather.10.cloned.1.call-done) | copy-start | bytes 6291460
  106.8 20.6 %all-to-all-start.2 = ((bf16[16,2,2048]{2,1,0:T(2,128)(2,1)}), bf16[16,2,2048]{2,1,0:T(2,128)(2,1)S(1)}, u32[]{:S(2)}, u32[]{:S(2)}) async-start(bf16[16,2,2048]{2,1,0:T(2,128)(2,1)} %reshape.329), calls=%async_computation.2 | async-start | bytes 262144 | tf_op jit(solution)/shard_map/all_to_all | solution.py:147
Sparse Core Ops, SparseCore 0:
  36.8 41.9 all-gather.9
  80.9 58.2 all-gather.11

commit v9 on v8

--- a/solution.py
+++ b/solution.py
@@ -27,6 +27,14 @@
     for name in reversed(PATCH_AXES):
         partial = lax.optimization_barrier(lax.psum(partial, name))
     return partial
+
+
+def replicated_gather(piece, name):
+    size = lax.axis_size(name)
+    if size <= 4:
+        return lax.all_gather(piece, name)
+    copies = jnp.broadcast_to(piece[None], (size,) + piece.shape)
+    return lax.all_to_all(copies, name, 0, 0, tiled=True)
 
 
 def permute_gather(piece, name):
@@ -67,7 +75,7 @@
     group_mean = jnp.sum(values, axis=(0, 2)) / count
     spread = jnp.sum(jnp.square(values - group_mean[None, :, None]), axis=(0, 2))
     for name in reversed(PATCH_AXES):
-        gathered = lax.all_gather(jnp.stack([group_mean, spread]), name)
+        gathered = replicated_gather(jnp.stack([group_mean, spread]), name)
         group_mean = jnp.mean(gathered[:, 0], axis=0)
         offset = gathered[:, 0] - group_mean[None, :]
         spread = jnp.sum(gathered[:, 1], axis=0) + count * jnp.sum(offset * offset, axis=0)
@@ -133,9 +141,10 @@
     factor = jnp.exp(block_max - top[None, :])
     stale_factor = jnp.where(is_home, 0.0, factor)
     scaled_weight = (weight * stale_factor[:, None, :]).reshape(slab_count * rows_here, split * rows_here)
-    stale_den = jnp.sum(scaled_weight, axis=0)
+    scaled_weight = scaled_weight.astype(jnp.bfloat16)
+    stale_den = jnp.sum(scaled_weight.astype(jnp.float32), axis=0)
     stale_num = jnp.einsum(
-        "kd,kq->qd", value_rows, scaled_weight.astype(jnp.bfloat16), preferred_element_type=jnp.float32
+        "kd,kq->qd", value_rows, scaled_weight, preferred_element_type=jnp.float32
     )
     home_factor = jnp.exp(home_max - top)
     numer = stale_num + home_factor[:, None] * home_num
@@ -146,9 +155,8 @@
     result = result.reshape(chan_count * split, rows_here, HEAD_DIM)
     attended = lax.all_to_all(result, ("chan", "px"), 0, 0, tiled=True)
     attended = jnp.transpose(attended, (1, 0, 2)).reshape(rows_here, chan_count * inner)
-    out_rows = lax.all_gather(w_out, "chan", axis=0, tiled=True)
-    projected = jnp.dot(attended, out_rows, preferred_element_type=jnp.float32)
-    projected = lax.dynamic_slice_in_dim(projected, lax.axis_index("chan") * chan_width, chan_width, axis=1)
+    out_columns = lax.all_to_all(w_out, "chan", 1, 0, tiled=True)
+    projected = jnp.dot(attended, out_columns, preferred_element_type=jnp.float32)
     mixed = (latent.astype(jnp.float32) + projected).astype(jnp.bfloat16)
     return (mixed, fresh_keys, fresh_values)
 

time: 150 us -> 144 us (0.960)
  the two profiles are of different devices: /device:TPU:1 before, /device:TPU:65 now
where the time goes in v9:
time: 144 us; the launch traced here: 143 us
  starting transfers between devices  37.7 us (26%)
  blocking collectives  33.3 us (23%)
  waiting for transfers between devices  33.1 us (23%)
  between operations  15.2 us (11%)
  local copies, waits for them, and re-layouts  11.6 us (8%)
  matrix products  6.59 us (5%)
  other arithmetic  5.74 us (4%)
    all_gather x1, blocking collectives, local(): shard_piece = lax.all_gather(normed, 'chan', axis=1, tiled=True)  17.8 us
    all_gather x2, blocking collectives, replicated_gather(): return lax.all_gather(piece, name)  15.6 us
    all_to_all x1, waiting for transfers between devices, local(): out_columns = lax.all_to_all(w_out, 'chan', 1, 0, tiled=True)  12.4 us
    ppermute x3, starting transfers between devices, permute_gather(): received.append(lax.ppermute(piece, name, pairs))  11.1 us
    all_to_all x1, waiting for transfers between devices, local(): attended = lax.all_to_all(result, ('chan', 'px'), 0, 0, tiled=True)  9.95 us
    all_to_all x1, starting transfers between devices, local(): out_columns = lax.all_to_all(w_out, 'chan', 1, 0, tiled=True)  8.17 us
    unnamed x24, local copies, waits for them, and re-layouts  7.31 us
    all_to_all x1, starting transfers between devices, replicated_gather(): return lax.all_to_all(copies, name, 0, 0, tiled=True)  6.82 us
  transfers between devices with their start and end apart: 9, of which 5 were waited for; matrix products, arithmetic and copies ran while one was open for 12% of the time, Pallas kernels for 0%

profile of v9, /device:TPU:65, one launch (start us, length us, event | category | flops | bytes accessed | tf_op | source)
XLA Modules:
  0.0 143.2 jit_solution(2049784710728429758)
XLA Ops:
  7.2 1.0 copy.49
  8.2 0.9 copy.50
  9.1 0.8 reshape.327
  9.9 4.0 %all-to-all-start = ((bf16[4,2,4096]{2,1,0:T(2,128)(2,1)}), bf16[4,2,4096]{2,1,0:T(2,128)(2,1)S(1)}, u32[]{:S(2)}, u32[]{:S(2)}) async-start(bf16[4,2,4096]{2,1,0:T(2,128)(2,1)} %reshape.327), calls=%async_computation | async-start | bytes 131072 | tf_op jit(solution)/shard_map/all_to_all | solution.py:104
  13.9 0.8 convert_reduce_fusion.1
  14.8 0.1 reduce_sum.132
  14.8 0.1 reduce_sum.133
  15.0 0.1 sub.125
  15.1 0.8 fusion.9
  16.0 0.1 reduce_sum.135
  16.0 0.1 reduce_sum.136
  16.2 7.9 %all-gather.2 = f32[4,2,8]{2,1,0:T(2,128)S(1)} all-gather(f32[1,2,8]{2,1,0:T(2,128)S(1)} %maximum_bitcast_fusion), channel_id=2, replica_groups=mesh['py'=8,'pz'=4,'px'=4,'chan'=4] {'px'}, dimensions={0}, use_global_device_ids=true | all-gather | bytes 320 | tf_op jit(solution)/shard_map/all_gather | solution.py:35
  24.2 7.7 %all-gather.3 = f32[4,2,8]{2,1,0:T(2,128)S(1)} all-gather(f32[1,2,8]{2,1,0:T(2,128)S(1)} %maximum_bitcast_fusion.1), channel_id=3, replica_groups=mesh['py'=8,'pz'=4,'px'=4,'chan'=4] {'pz'}, dimensions={0}, use_global_device_ids=true | all-gather | bytes 320 | tf_op jit(solution)/shard_map/all_gather | solution.py:35
  31.9 0.1 reshape.328
  32.0 0.1 copy.51
  32.2 0.1 reshape.297
  32.3 3.4 %collective-permute-start = (bf16[2,256,64]{1,2,0:T(8,128)(2,1)S(1)}, bf16[2,256,64]{1,2,0:T(8,128)(2,1)S(1)}, u32[]{:S(2)}, u32[]{:S(2)}) collective-permute-start(bf16[2,256,64]{1,2,0:T(8,128)(2,1)S(1)} %reshape.297), channel_id=1, source_target_pairs={{0,16},{16,32},{32,48},{48,0},{1,17},{17,33},{33,49},{49,1},{2,18}... | collective-permute-start | bytes 196616 | tf_op jit(solution)/shard_map/ppermute | solution.py:46
  35.7 5.8 %collective-permute-start.1 = (bf16[2,256,64]{1,2,0:T(8,128)(2,1)S(1)}, bf16[2,256,64]{1,2,0:T(8,128)(2,1)S(1)}, u32[]{:S(2)}, u32[]{:S(2)}) collective-permute-start(bf16[2,256,64]{1,2,0:T(8,128)(2,1)S(1)} %reshape.297), channel_id=1, source_target_pairs={{0,32},{16,48},{32,0},{48,16},{1,33},{17,49},{33,1},{49,17},{2,34}... | collective-permute-start | bytes 196616 | tf_op jit(solution)/shard_map/ppermute | solution.py:46
  41.5 1.9 %collective-permute-start.2 = (bf16[2,256,64]{1,2,0:T(8,128)(2,1)S(1)}, bf16[2,256,64]{1,2,0:T(8,128)(2,1)S(1)}, u32[]{:S(2)}, u32[]{:S(2)}) collective-permute-start(bf16[2,256,64]{1,2,0:T(8,128)(2,1)S(1)} %reshape.297), channel_id=1, source_target_pairs={{0,48},{16,0},{32,16},{48,32},{1,49},{17,1},{33,17},{49,33},{2,50}... | collective-permute-start | bytes 196616 | tf_op jit(solution)/shard_map/ppermute | solution.py:46
  43.4 0.1 stack_reshape.3
  43.6 3.6 %collective-permute-done.2 = bf16[2,256,64]{1,2,0:T(8,128)(2,1)S(1)} collective-permute-done((bf16[2,256,64]{1,2,0:T(8,128)(2,1)S(1)}, bf16[2,256,64]{1,2,0:T(8,128)(2,1)S(1)}, u32[]{:S(2)}, u32[]{:S(2)}) %collective-permute-start.2) | collective-permute-done | bytes 65568 | tf_op jit(solution)/shard_map/ppermute | solution.py:46
  47.2 0.6 gather_fusion
  47.8 0.1 select_bitcast_fusion
  47.9 0.7 copy.70
  48.7 0.6 broadcast_in_dim.32
  49.3 6.8 %all-to-all-start.1 = ((f32[8,2,8]{2,1,0:T(2,128)}), f32[8,2,8]{2,1,0:T(2,128)S(1)}, u32[]{:S(2)}, u32[]{:S(2)}) async-start(f32[8,2,8]{2,1,0:T(2,128)} %broadcast_in_dim.32), calls=%async_computation.1 | async-start | bytes 16384 | tf_op jit(solution)/shard_map/all_to_all | solution.py:37
  56.8 0.1 divide_multiply_fusion
  56.9 1.2 convolution_reduce_fusion
  58.1 2.2 %copy.64 = bf16[256,1280]{0,1:T(8,128)(2,1)} copy(bf16[256,1280]{1,0:T(8,128)(2,1)} %param.19) | data formatting | bytes 1310720 | tf_op args[8]
  60.3 2.4 %all-to-all-done.1 = f32[8,2,8]{2,1,0:T(2,128)S(1)} async-done(((f32[8,2,8]{2,1,0:T(2,128)}), f32[8,2,8]{2,1,0:T(2,128)S(1)}, u32[]{:S(2)}, u32[]{:S(2)}) %all-to-all-start.1) | async-done | bytes 544 | tf_op jit(solution)/shard_map/all_to_all | solution.py:37
  62.9 0.1 mul.127
  63.0 0.1 sub.133
  63.1 0.9 fusion.17
  64.0 17.8 %all-gather.4 = bf16[4,320,64]{1,2,0:T(8,128)(2,1)S(1)} all-gather(bf16[1,320,64]{1,2,0:T(8,128)(2,1)S(1)} %fusion.17), channel_id=1, replica_groups=mesh['py'=8,'pz'=4,'px'=4,'chan'=4] {'chan'}, dimensions={0}, use_global_device_ids=true | all-gather | bytes 204800 | tf_op jit(solution)/shard_map/all_gather | solution.py:90
  81.7 0.2 copy.55
  81.9 0.2 reshape.319
  82.1 0.2 convolution_convert_fusion.2
  82.3 0.1 stack.61
  82.4 0.2 convolution_convert_fusion.1
  82.7 0.1 stack.62
  82.8 0.2 convolution_convert_fusion
  83.1 0.1 stack.63
  83.3 0.8 reshape.325
  84.1 3.3 %all-to-all-start.2 = ((bf16[4,2,6144]{2,1,0:T(2,128)(2,1)}), bf16[4,2,6144]{2,1,0:T(2,128)(2,1)S(1)}, u32[]{:S(2)}, u32[]{:S(2)}) async-start(bf16[4,2,6144]{2,1,0:T(2,128)(2,1)} %reshape.325), calls=%async_computation.2 | async-start | bytes 196608 | tf_op jit(solution)/shard_map/all_to_all | solution.py:112
  87.4 4.6 %all-to-all-done.2 = bf16[4,2,6144]{2,1,0:T(2,128)(2,1)S(1)} async-done(((bf16[4,2,6144]{2,1,0:T(2,128)(2,1)}), bf16[4,2,6144]{2,1,0:T(2,128)(2,1)S(1)}, u32[]{:S(2)}, u32[]{:S(2)}) %all-to-all-start.2) | async-done | bytes 98336 | tf_op jit(solution)/shard_map/all_to_all | solution.py:112
  92.1 8.2 %all-to-all-start.4 = ((bf16[256,4,320]{0,2,1:T(8,128)(2,1)}), bf16[256,4,320]{0,2,1:T(8,128)(2,1)S(1)}, u32[]{:S(2)}, u32[]{:S(2)}) async-start(bf16[256,4,320]{0,2,1:T(8,128)(2,1)} %bitcast.40), calls=%async_computation.4 | async-start | bytes 1310720 | tf_op jit(solution)/shard_map/all_to_all | solution.py:158
  100.2 0.2 reshape.326
  100.5 0.2 fusion.30
  100.6 0.1 broadcast_in_dim.34
  100.8 0.1 reshape.301
  100.9 0.2 fusion.15
  101.1 0.1 copy.67
  101.2 2.5 %bitcast_reduce_fusion = (f32[128,256]{1,0:T(8,128)S(1)}, f32[8192,256]{1,0:T(8,128)S(1)}) fusion(bf16[256,64]{1,0:T(8,128)(2,1)S(1)} %bitcast.123, bf16[2,8192,64]{1,2,0:T(8,128)(2,1)} %all-gather.7.cloned.1.call-done), kind=kOutput, calls=%fused_computation.7 | convolution fusion | flops 272596992 | bytes 9601024 | tf_op jit(solution)/shard_map/kd,qd->kq/dot_general | solution.py:118
  103.9 2.2 %convert_reduce_fusion = (f32[256]{0:T(256)S(1)}, bf16[8192,256]{1,0:T(8,128)(2,1)S(1)}) fusion(f32[128,256]{1,0:T(8,128)S(1)} %exponential_select_fusion, f32[8192,256]{1,0:T(8,128)S(1)} %get-tuple-element.22, f32[128,256]{1,0:T(8,128)S(1)} %get-tuple-element.21), kind=kLoop, calls=%fused_computation.8 | loop fusion | flops 14679808 | bytes 12846080 | tf_op jit(solution)/shard_map/reduce_sum | solution.py:145
  106.1 0.8 fusion.5
  106.9 0.1 copy.68
  107.1 0.9 reshape.329
  108.0 12.4 %all-to-all-done.4 = bf16[256,4,320]{0,2,1:T(8,128)(2,1)S(1)} async-done(((bf16[256,4,320]{0,2,1:T(8,128)(2,1)}), bf16[256,4,320]{0,2,1:T(8,128)(2,1)S(1)}, u32[]{:S(2)}, u32[]{:S(2)}) %all-to-all-start.4) | async-done | bytes 655392 | tf_op jit(solution)/shard_map/all_to_all | solution.py:158
  120.4 4.3 %all-to-all-start.3 = ((bf16[16,2,2048]{2,1,0:T(2,128)(2,1)}), bf16[16,2,2048]{2,1,0:T(2,128)(2,1)S(1)}, u32[]{:S(2)}, u32[]{:S(2)}) async-start(bf16[16,2,2048]{2,1,0:T(2,128)(2,1)} %reshape.329), calls=%async_computation.3 | async-start | bytes 262144 | tf_op jit(solution)/shard_map/all_to_all | solution.py:156
  124.8 10.0 %all-to-all-done.3 = bf16[16,2,2048]{2,1,0:T(2,128)(2,1)S(1)} async-done(((bf16[16,2,2048]{2,1,0:T(2,128)(2,1)}), bf16[16,2,2048]{2,1,0:T(2,128)(2,1)S(1)}, u32[]{:S(2)}, u32[]{:S(2)}) %all-to-all-start.3) | async-done | bytes 131104 | tf_op jit(solution)/shard_map/all_to_all | solution.py:156
  134.7 0.2 reshape.330
  134.9 0.2 copy.63
  135.1 0.2 reshape.303
  135.3 1.0 fusion.3
  (61 shorter events, 1.1 us)
Async XLA Ops:
  7.2 74.9 %copy-start = (bf16[1280,256]{1,0:T(8,128)(2,1)S(1)}, bf16[1280,256]{1,0:T(8,128)(2,1)}, u32[]{:S(2)}) copy-start(bf16[1280,256]{1,0:T(8,128)(2,1)} %param.16) | copy-start | bytes 1966084
  7.2 75.3 %copy-start.3 = (bf16[1280,256]{1,0:T(8,128)(2,1)S(1)}, bf16[1280,256]{1,0:T(8,128)(2,1)}, u32[]{:S(2)}) copy-start(bf16[1280,256]{1,0:T(8,128)(2,1)} %param.17) | copy-start | bytes 1966084
  7.2 75.6 %copy-start.4 = (bf16[1280,256]{1,0:T(8,128)(2,1)S(1)}, bf16[1280,256]{1,0:T(8,128)(2,1)}, u32[]{:S(2)}) copy-start(bf16[1280,256]{1,0:T(8,128)(2,1)} %param.18) | copy-start | bytes 1966084
  9.9 22.0 %all-to-all-start = ((bf16[4,2,4096]{2,1,0:T(2,128)(2,1)}), bf16[4,2,4096]{2,1,0:T(2,128)(2,1)S(1)}, u32[]{:S(2)}, u32[]{:S(2)}) async-start(bf16[4,2,4096]{2,1,0:T(2,128)(2,1)} %reshape.327), calls=%async_computation | async-start | bytes 131072 | tf_op jit(solution)/shard_map/all_to_all | solution.py:104
  13.9 87.3 %all-gather.7.cloned.1.call-start = ((), (), s32[]{:S(2)}) async-start(), calls=%async_computation.5 | async-start | bytes 2359296 | tf_op jit(solution)/shard_map/all_gather | solution.py:106
  32.3 11.3 %collective-permute-start = (bf16[2,256,64]{1,2,0:T(8,128)(2,1)S(1)}, bf16[2,256,64]{1,2,0:T(8,128)(2,1)S(1)}, u32[]{:S(2)}, u32[]{:S(2)}) collective-permute-start(bf16[2,256,64]{1,2,0:T(8,128)(2,1)S(1)} %reshape.297), channel_id=1, source_target_pairs={{0,16},{16,32},{32,48},{48,0},{1,17},{17,33},{33,49},{49,1},{2,18}... | collective-permute-start | bytes 196616 | tf_op jit(solution)/shard_map/ppermute | solution.py:46
  35.7 7.9 %collective-permute-start.1 = (bf16[2,256,64]{1,2,0:T(8,128)(2,1)S(1)}, bf16[2,256,64]{1,2,0:T(8,128)(2,1)S(1)}, u32[]{:S(2)}, u32[]{:S(2)}) collective-permute-start(bf16[2,256,64]{1,2,0:T(8,128)(2,1)S(1)} %reshape.297), channel_id=1, source_target_pairs={{0,32},{16,48},{32,0},{48,16},{1,33},{17,49},{33,1},{49,17},{2,34}... | collective-permute-start | bytes 196616 | tf_op jit(solution)/shard_map/ppermute | solution.py:46
  41.5 5.7 %collective-permute-start.2 = (bf16[2,256,64]{1,2,0:T(8,128)(2,1)S(1)}, bf16[2,256,64]{1,2,0:T(8,128)(2,1)S(1)}, u32[]{:S(2)}, u32[]{:S(2)}) collective-permute-start(bf16[2,256,64]{1,2,0:T(8,128)(2,1)S(1)} %reshape.297), channel_id=1, source_target_pairs={{0,48},{16,0},{32,16},{48,32},{1,49},{17,1},{33,17},{49,33},{2,50}... | collective-permute-start | bytes 196616 | tf_op jit(solution)/shard_map/ppermute | solution.py:46
  49.3 13.4 %all-to-all-start.1 = ((f32[8,2,8]{2,1,0:T(2,128)}), f32[8,2,8]{2,1,0:T(2,128)S(1)}, u32[]{:S(2)}, u32[]{:S(2)}) async-start(f32[8,2,8]{2,1,0:T(2,128)} %broadcast_in_dim.32), calls=%async_computation.1 | async-start | bytes 16384 | tf_op jit(solution)/shard_map/all_to_all | solution.py:37
  82.7 21.0 %copy-start.5 = (bf16[64,256]{1,0:T(8,128)(2,1)}, bf16[64,256]{1,0:T(8,128)(2,1)S(1)}, u32[]{:S(2)}) copy-start(bf16[64,256]{1,0:T(8,128)(2,1)S(1)} %convolution_convert_fusion.1) | copy-start | bytes 98308
  83.1 20.7 %copy-start.6 = (bf16[64,256]{1,0:T(8,128)(2,1)}, bf16[64,256]{1,0:T(8,128)(2,1)S(1)}, u32[]{:S(2)}) copy-start(bf16[64,256]{1,0:T(8,128)(2,1)S(1)} %convolution_convert_fusion) | copy-start | bytes 98308
  84.1 7.9 %all-to-all-start.2 = ((bf16[4,2,6144]{2,1,0:T(2,128)(2,1)}), bf16[4,2,6144]{2,1,0:T(2,128)(2,1)S(1)}, u32[]{:S(2)}, u32[]{:S(2)}) async-start(bf16[4,2,6144]{2,1,0:T(2,128)(2,1)} %reshape.325), calls=%async_computation.2 | async-start | bytes 196608 | tf_op jit(solution)/shard_map/all_to_all | solution.py:112
  92.1 28.4 %all-to-all-start.4 = ((bf16[256,4,320]{0,2,1:T(8,128)(2,1)}), bf16[256,4,320]{0,2,1:T(8,128)(2,1)S(1)}, u32[]{:S(2)}, u32[]{:S(2)}) async-start(bf16[256,4,320]{0,2,1:T(8,128)(2,1)} %bitcast.40), calls=%async_computation.4 | async-start | bytes 1310720 | tf_op jit(solution)/shard_map/all_to_all | solution.py:158
  103.8 2.4 %copy-start.1 = (bf16[2,8192,64]{1,2,0:T(8,128)(2,1)S(1)}, bf16[2,8192,64]{1,2,0:T(8,128)(2,1)}, u32[]{:S(2)}) copy-start(bf16[2,8192,64]{1,2,0:T(8,128)(2,1)} %all-gather.7.cloned.1.call-done) | copy-start | bytes 6291460
  103.8 31.5 %copy-start.2 = (bf16[64,320]{1,0:T(8,128)(2,1)S(1)}, bf16[64,320]{1,0:T(8,128)(2,1)}, u32[]{:S(2)}) copy-start(bf16[64,320]{1,0:T(8,128)(2,1)} %param.11) | copy-start | bytes 122884
  120.4 14.3 %all-to-all-start.3 = ((bf16[16,2,2048]{2,1,0:T(2,128)(2,1)}), bf16[16,2,2048]{2,1,0:T(2,128)(2,1)S(1)}, u32[]{:S(2)}, u32[]{:S(2)}) async-start(bf16[16,2,2048]{2,1,0:T(2,128)(2,1)} %reshape.329), calls=%async_computation.3 | async-start | bytes 262144 | tf_op jit(solution)/shard_map/all_to_all | solution.py:156
Sparse Core Ops, SparseCore 0:
  48.8 44.6 all-gather.6

commit v10 on v9

--- a/solution.py
+++ b/solution.py
@@ -31,8 +31,6 @@
 
 def replicated_gather(piece, name):
     size = lax.axis_size(name)
-    if size <= 4:
-        return lax.all_gather(piece, name)
     copies = jnp.broadcast_to(piece[None], (size,) + piece.shape)
     return lax.all_to_all(copies, name, 0, 0, tiled=True)
 
@@ -74,7 +72,7 @@
     count = rows_here * width
     group_mean = jnp.sum(values, axis=(0, 2)) / count
     spread = jnp.sum(jnp.square(values - group_mean[None, :, None]), axis=(0, 2))
-    for name in reversed(PATCH_AXES):
+    for name in (PATCH_AXES[1:], PATCH_AXES[0]):
         gathered = replicated_gather(jnp.stack([group_mean, spread]), name)
         group_mean = jnp.mean(gathered[:, 0], axis=0)
         offset = gathered[:, 0] - group_mean[None, :]
@@ -102,7 +100,7 @@
 
     stacked = jnp.stack([stale_keys, stale_values]).reshape(2, rows_here, heads_here, HEAD_DIM)
     stacked = lax.all_to_all(stacked, "px", 2, 1, tiled=True).reshape(2, split * rows_here, HEAD_DIM)
-    stacked = permute_gather(stacked, "pz")
+    stacked = jnp.moveaxis(replicated_gather(stacked, "pz"), 0, 1).reshape(2, -1, HEAD_DIM)
     stacked = lax.all_gather(stacked, "py", axis=1, tiled=True)
     slab_count = stacked.shape[1] // rows_here
 

time: 144 us -> 138 us (0.958)
  the two profiles are of different devices: /device:TPU:65 before, /device:TPU:1 now
where the time goes in v10:
time: 138 us; the launch traced here: 136 us
  waiting for transfers between devices  40.6 us (29%)
  starting transfers between devices  40.2 us (29%)
  between operations  15.1 us (11%)
  blocking collectives  14.8 us (11%)
  local copies, waits for them, and re-layouts  12.2 us (9%)
  matrix products  7.67 us (6%)
  other arithmetic  5.68 us (4%)
    all_to_all x3, starting transfers between devices, replicated_gather(): return lax.all_to_all(copies, name, 0, 0, tiled=True)  19.5 us
    all_gather x1, blocking collectives, local(): shard_piece = lax.all_gather(normed, 'chan', axis=1, tiled=True)  14.8 us
    all_to_all x3, waiting for transfers between devices, replicated_gather(): return lax.all_to_all(copies, name, 0, 0, tiled=True)  13.1 us
    all_to_all x1, waiting for transfers between devices, local(): attended = lax.all_to_all(result, ('chan', 'px'), 0, 0, tiled=True)  9.99 us
    all_to_all x1, waiting for transfers between devices, local(): out_columns = lax.all_to_all(w_out, 'chan', 1, 0, tiled=True)  9.59 us
    all_to_all x1, starting transfers between devices, local(): out_columns = lax.all_to_all(w_out, 'chan', 1, 0, tiled=True)  8.17 us
    unnamed x23, local copies, waits for them, and re-layouts  7.33 us
    all_to_all x1, starting transfers between devices, local(): lax.all_to_all(stacked, 'px', 2, 1, tiled=True)  4.83 us
  transfers between devices with their start and end apart: 8, of which 7 were waited for; matrix products, arithmetic and copies ran while one was open for 14% of the time, Pallas kernels for 0%

profile of v10, /device:TPU:1, one launch (start us, length us, event | category | flops | bytes accessed | tf_op | source)
XLA Modules:
  0.0 136.3 jit_solution(7807051679854844824)
XLA Ops:
  7.2 1.0 copy.48
  8.2 0.9 copy.49
  9.1 0.8 reshape.228
  9.9 4.8 %all-to-all-start = ((bf16[4,2,4096]{2,1,0:T(2,128)(2,1)}), bf16[4,2,4096]{2,1,0:T(2,128)(2,1)S(1)}, u32[]{:S(2)}, u32[]{:S(2)}) async-start(bf16[4,2,4096]{2,1,0:T(2,128)(2,1)} %reshape.228), calls=%async_computation | async-start | bytes 131072 | tf_op jit(solution)/shard_map/all_to_all | solution.py:102
  14.7 0.8 convert_reduce_fusion.1
  15.5 0.1 reduce_sum.105
  15.6 0.1 reduce_sum.106
  15.8 0.1 sub.94
  15.9 3.3 %all-to-all-done = bf16[4,2,4096]{2,1,0:T(2,128)(2,1)S(1)} async-done(((bf16[4,2,4096]{2,1,0:T(2,128)(2,1)}), bf16[4,2,4096]{2,1,0:T(2,128)(2,1)S(1)}, u32[]{:S(2)}, u32[]{:S(2)}) %all-to-all-start) | async-done | bytes 65568 | tf_op jit(solution)/shard_map/all_to_all | solution.py:102
  19.2 0.1 reshape.229
  19.3 0.1 copy.50
  19.5 0.1 broadcast_in_dim.22
  19.6 0.7 broadcast_in_dim.23
  20.3 7.0 %all-to-all-start.1 = ((bf16[4,2,256,64]{2,3,1,0:T(8,128)(2,1)}), bf16[4,2,256,64]{2,3,1,0:T(8,128)(2,1)S(1)}, u32[]{:S(2)}, u32[]{:S(2)}) async-start(bf16[4,2,256,64]{2,3,1,0:T(8,128)(2,1)} %broadcast_in_dim.23), calls=%async_computation.1 | async-start | bytes 524288 | tf_op jit(solution)/shard_map/all_to_all | solution.py:35
  27.3 0.8 fusion.9
  28.1 0.1 reduce_sum.108
  28.2 0.1 reduce_sum.109
  29.0 0.1 divide_multiply_fusion
  29.1 3.8 %all-to-all-done.1 = bf16[4,2,256,64]{2,3,1,0:T(8,128)(2,1)S(1)} async-done(((bf16[4,2,256,64]{2,3,1,0:T(8,128)(2,1)}), bf16[4,2,256,64]{2,3,1,0:T(8,128)(2,1)S(1)}, u32[]{:S(2)}, u32[]{:S(2)}) %all-to-all-start.1) | async-done | bytes 262176 | tf_op jit(solution)/shard_map/all_to_all | solution.py:35
  32.9 0.6 broadcast_in_dim.24
  33.5 4.0 %all-to-all-start.2 = ((f32[16,2,8]{2,1,0:T(2,128)}), f32[16,2,8]{2,1,0:T(2,128)S(1)}, u32[]{:S(2)}, u32[]{:S(2)}) async-start(f32[16,2,8]{2,1,0:T(2,128)} %broadcast_in_dim.24), calls=%async_computation.2 | async-start | bytes 32768 | tf_op jit(solution)/shard_map/all_to_all | solution.py:35
  37.6 1.2 convolution_reduce_fusion
  38.8 0.7 copy.71
  39.5 4.9 %all-to-all-done.2 = f32[16,2,8]{2,1,0:T(2,128)S(1)} async-done(((f32[16,2,8]{2,1,0:T(2,128)}), f32[16,2,8]{2,1,0:T(2,128)S(1)}, u32[]{:S(2)}, u32[]{:S(2)}) %all-to-all-start.2) | async-done | bytes 1056 | tf_op jit(solution)/shard_map/all_to_all | solution.py:35
  44.5 0.2 fusion.19
  44.7 0.6 broadcast_in_dim.25
  45.3 8.5 %all-to-all-start.3 = ((f32[8,2,8]{2,1,0:T(2,128)}), f32[8,2,8]{2,1,0:T(2,128)S(1)}, u32[]{:S(2)}, u32[]{:S(2)}) async-start(f32[8,2,8]{2,1,0:T(2,128)} %broadcast_in_dim.25), calls=%async_computation.3 | async-start | bytes 16384 | tf_op jit(solution)/shard_map/all_to_all | solution.py:35
  53.8 2.2 %copy.63 = bf16[256,1280]{0,1:T(8,128)(2,1)} copy(bf16[256,1280]{1,0:T(8,128)(2,1)} %param.19) | data formatting | bytes 1310720 | tf_op args[8]
  56.0 4.4 %all-to-all-done.3 = f32[8,2,8]{2,1,0:T(2,128)S(1)} async-done(((f32[8,2,8]{2,1,0:T(2,128)}), f32[8,2,8]{2,1,0:T(2,128)S(1)}, u32[]{:S(2)}, u32[]{:S(2)}) %all-to-all-start.3) | async-done | bytes 544 | tf_op jit(solution)/shard_map/all_to_all | solution.py:35
  60.5 0.1 mul.110
  60.5 0.1 mul.111
  60.7 0.1 sub.100
  60.8 0.9 fusion.17
  61.6 14.8 %all-gather = bf16[4,320,64]{1,2,0:T(8,128)(2,1)S(1)} all-gather(bf16[1,320,64]{1,2,0:T(8,128)(2,1)S(1)} %fusion.17), channel_id=1, replica_groups=mesh['py'=8,'pz'=4,'px'=4,'chan'=4] {'chan'}, dimensions={0}, use_global_device_ids=true | all-gather | bytes 204800 | tf_op jit(solution)/shard_map/all_gather | solution.py:88
  76.4 0.2 copy.54
  76.6 0.2 reshape.222
  76.8 0.2 convolution_convert_fusion.1
  77.0 0.1 stack.40
  77.1 1.3 convolution_convert_fusion
  78.5 0.1 stack.41
  78.6 0.2 convolution_convert_fusion.2
  78.9 0.1 stack.39
  79.1 0.8 reshape.226
  79.9 3.3 %all-to-all-start.4 = ((bf16[4,2,6144]{2,1,0:T(2,128)(2,1)}), bf16[4,2,6144]{2,1,0:T(2,128)(2,1)S(1)}, u32[]{:S(2)}, u32[]{:S(2)}) async-start(bf16[4,2,6144]{2,1,0:T(2,128)(2,1)} %reshape.226), calls=%async_computation.4 | async-start | bytes 196608 | tf_op jit(solution)/shard_map/all_to_all | solution.py:110
  83.2 4.6 %all-to-all-done.4 = bf16[4,2,6144]{2,1,0:T(2,128)(2,1)S(1)} async-done(((bf16[4,2,6144]{2,1,0:T(2,128)(2,1)}), bf16[4,2,6144]{2,1,0:T(2,128)(2,1)S(1)}, u32[]{:S(2)}, u32[]{:S(2)}) %all-to-all-start.4) | async-done | bytes 98336 | tf_op jit(solution)/shard_map/all_to_all | solution.py:110
  87.9 8.2 %all-to-all-start.6 = ((bf16[256,4,320]{0,2,1:T(8,128)(2,1)}), bf16[256,4,320]{0,2,1:T(8,128)(2,1)S(1)}, u32[]{:S(2)}, u32[]{:S(2)}) async-start(bf16[256,4,320]{0,2,1:T(8,128)(2,1)} %bitcast.30), calls=%async_computation.6 | async-start | bytes 1310720 | tf_op jit(solution)/shard_map/all_to_all | solution.py:156
  96.0 0.2 reshape.227
  96.3 0.2 fusion.28
  96.4 0.1 broadcast_in_dim.30
  96.6 0.1 reshape.218
  96.7 0.2 fusion.15
  96.9 0.1 copy.66
  97.0 2.5 %bitcast_reduce_fusion = (f32[128,256]{1,0:T(8,128)S(1)}, f32[8192,256]{1,0:T(8,128)S(1)}) fusion(bf16[256,64]{1,0:T(8,128)(2,1)S(1)} %bitcast.112, bf16[2,8192,64]{1,2,0:T(8,128)(2,1)} %all-gather.3.cloned.1.call-done), kind=kOutput, calls=%fused_computation.6 | convolution fusion | flops 272596992 | bytes 9601024 | tf_op jit(solution)/shard_map/kd,qd->kq/dot_general | solution.py:116
  99.7 2.2 %convert_reduce_fusion = (f32[256]{0:T(256)S(1)}, bf16[8192,256]{1,0:T(8,128)(2,1)S(1)}) fusion(f32[128,256]{1,0:T(8,128)S(1)} %exponential_select_fusion, f32[8192,256]{1,0:T(8,128)S(1)} %get-tuple-element.17, f32[128,256]{1,0:T(8,128)S(1)} %get-tuple-element.16), kind=kLoop, calls=%fused_computation.7 | loop fusion | flops 14679808 | bytes 12846080 | tf_op jit(solution)/shard_map/reduce_sum | solution.py:143
  101.9 0.8 fusion.5
  102.7 0.1 copy.67
  102.9 0.9 reshape.230
  103.8 9.6 %all-to-all-done.6 = bf16[256,4,320]{0,2,1:T(8,128)(2,1)S(1)} async-done(((bf16[256,4,320]{0,2,1:T(8,128)(2,1)}), bf16[256,4,320]{0,2,1:T(8,128)(2,1)S(1)}, u32[]{:S(2)}, u32[]{:S(2)}) %all-to-all-start.6) | async-done | bytes 655392 | tf_op jit(solution)/shard_map/all_to_all | solution.py:156
  113.4 4.4 %all-to-all-start.5 = ((bf16[16,2,2048]{2,1,0:T(2,128)(2,1)}), bf16[16,2,2048]{2,1,0:T(2,128)(2,1)S(1)}, u32[]{:S(2)}, u32[]{:S(2)}) async-start(bf16[16,2,2048]{2,1,0:T(2,128)(2,1)} %reshape.230), calls=%async_computation.5 | async-start | bytes 262144 | tf_op jit(solution)/shard_map/all_to_all | solution.py:154
  117.9 10.0 %all-to-all-done.5 = bf16[16,2,2048]{2,1,0:T(2,128)(2,1)S(1)} async-done(((bf16[16,2,2048]{2,1,0:T(2,128)(2,1)}), bf16[16,2,2048]{2,1,0:T(2,128)(2,1)S(1)}, u32[]{:S(2)}, u32[]{:S(2)}) %all-to-all-start.5) | async-done | bytes 131104 | tf_op jit(solution)/shard_map/all_to_all | solution.py:154
  127.9 0.2 reshape.231
  128.1 0.2 copy.62
  128.3 0.2 reshape.220
  128.5 1.0 fusion.3
  (46 shorter events, 1.0 us)
Async XLA Ops:
  7.2 69.6 %copy-start = (bf16[1280,256]{1,0:T(8,128)(2,1)S(1)}, bf16[1280,256]{1,0:T(8,128)(2,1)}, u32[]{:S(2)}) copy-start(bf16[1280,256]{1,0:T(8,128)(2,1)} %param.17) | copy-start | bytes 1966084
  7.2 71.5 %copy-start.3 = (bf16[1280,256]{1,0:T(8,128)(2,1)S(1)}, bf16[1280,256]{1,0:T(8,128)(2,1)}, u32[]{:S(2)}) copy-start(bf16[1280,256]{1,0:T(8,128)(2,1)} %param.16) | copy-start | bytes 1966084
  9.9 9.3 %all-to-all-start = ((bf16[4,2,4096]{2,1,0:T(2,128)(2,1)}), bf16[4,2,4096]{2,1,0:T(2,128)(2,1)S(1)}, u32[]{:S(2)}, u32[]{:S(2)}) async-start(bf16[4,2,4096]{2,1,0:T(2,128)(2,1)} %reshape.228), calls=%async_computation | async-start | bytes 131072 | tf_op jit(solution)/shard_map/all_to_all | solution.py:102
  20.3 12.6 %all-to-all-start.1 = ((bf16[4,2,256,64]{2,3,1,0:T(8,128)(2,1)}), bf16[4,2,256,64]{2,3,1,0:T(8,128)(2,1)S(1)}, u32[]{:S(2)}, u32[]{:S(2)}) async-start(bf16[4,2,256,64]{2,3,1,0:T(8,128)(2,1)} %broadcast_in_dim.23), calls=%async_computation.1 | async-start | bytes 524288 | tf_op jit(solution)/shard_map/all_to_all | solution.py:35
  33.5 10.9 %all-to-all-start.2 = ((f32[16,2,8]{2,1,0:T(2,128)}), f32[16,2,8]{2,1,0:T(2,128)S(1)}, u32[]{:S(2)}, u32[]{:S(2)}) async-start(f32[16,2,8]{2,1,0:T(2,128)} %broadcast_in_dim.24), calls=%async_computation.2 | async-start | bytes 32768 | tf_op jit(solution)/shard_map/all_to_all | solution.py:35
  37.5 59.5 %all-gather.3.cloned.1.call-start = ((), (), s32[]{:S(2)}) async-start(), calls=%async_computation.7 | async-start | bytes 2359296 | tf_op jit(solution)/shard_map/all_gather | solution.py:104
  45.3 15.1 %all-to-all-start.3 = ((f32[8,2,8]{2,1,0:T(2,128)}), f32[8,2,8]{2,1,0:T(2,128)S(1)}, u32[]{:S(2)}, u32[]{:S(2)}) async-start(f32[8,2,8]{2,1,0:T(2,128)} %broadcast_in_dim.25), calls=%async_computation.3 | async-start | bytes 16384 | tf_op jit(solution)/shard_map/all_to_all | solution.py:35
  77.0 22.5 %copy-start.4 = (bf16[64,256]{1,0:T(8,128)(2,1)}, bf16[64,256]{1,0:T(8,128)(2,1)S(1)}, u32[]{:S(2)}) copy-start(bf16[64,256]{1,0:T(8,128)(2,1)S(1)} %convolution_convert_fusion.1) | copy-start | bytes 98308
  78.5 21.0 %copy-start.5 = (bf16[64,256]{1,0:T(8,128)(2,1)}, bf16[64,256]{1,0:T(8,128)(2,1)S(1)}, u32[]{:S(2)}) copy-start(bf16[64,256]{1,0:T(8,128)(2,1)S(1)} %convolution_convert_fusion) | copy-start | bytes 98308
  79.9 7.9 %all-to-all-start.4 = ((bf16[4,2,6144]{2,1,0:T(2,128)(2,1)}), bf16[4,2,6144]{2,1,0:T(2,128)(2,1)S(1)}, u32[]{:S(2)}, u32[]{:S(2)}) async-start(bf16[4,2,6144]{2,1,0:T(2,128)(2,1)} %reshape.226), calls=%async_computation.4 | async-start | bytes 196608 | tf_op jit(solution)/shard_map/all_to_all | solution.py:110
  87.9 25.5 %all-to-all-start.6 = ((bf16[256,4,320]{0,2,1:T(8,128)(2,1)}), bf16[256,4,320]{0,2,1:T(8,128)(2,1)S(1)}, u32[]{:S(2)}, u32[]{:S(2)}) async-start(bf16[256,4,320]{0,2,1:T(8,128)(2,1)} %bitcast.30), calls=%async_computation.6 | async-start | bytes 1310720 | tf_op jit(solution)/shard_map/all_to_all | solution.py:156
  99.5 2.4 %copy-start.1 = (bf16[2,8192,64]{1,2,0:T(8,128)(2,1)S(1)}, bf16[2,8192,64]{1,2,0:T(8,128)(2,1)}, u32[]{:S(2)}) copy-start(bf16[2,8192,64]{1,2,0:T(8,128)(2,1)} %all-gather.3.cloned.1.call-done) | copy-start | bytes 6291460
  99.6 28.8 %copy-start.2 = (bf16[64,320]{1,0:T(8,128)(2,1)S(1)}, bf16[64,320]{1,0:T(8,128)(2,1)}, u32[]{:S(2)}) copy-start(bf16[64,320]{1,0:T(8,128)(2,1)} %param.11) | copy-start | bytes 122884
  113.4 14.5 %all-to-all-start.5 = ((bf16[16,2,2048]{2,1,0:T(2,128)(2,1)}), bf16[16,2,2048]{2,1,0:T(2,128)(2,1)S(1)}, u32[]{:S(2)}, u32[]{:S(2)}) async-start(bf16[16,2,2048]{2,1,0:T(2,128)(2,1)} %reshape.230), calls=%async_computation.5 | async-start | bytes 262144 | tf_op jit(solution)/shard_map/all_to_all | solution.py:154
Sparse Core Ops, SparseCore 0:
  40.4 44.5 all-gather.2

commit v11 on v10

--- a/solution.py
+++ b/solution.py
@@ -23,30 +23,23 @@
     )[0]
 
 
-def patch_sum(partial):
-    for name in reversed(PATCH_AXES):
-        partial = lax.optimization_barrier(lax.psum(partial, name))
-    return partial
-
-
 def replicated_gather(piece, name):
     size = lax.axis_size(name)
     copies = jnp.broadcast_to(piece[None], (size,) + piece.shape)
     return lax.all_to_all(copies, name, 0, 0, tiled=True)
 
 
-def permute_gather(piece, name):
+def permute_columns(rows, name, width):
     size = lax.axis_size(name)
     here = lax.axis_index(name)
-    received = [piece]
+    received = [lax.dynamic_slice_in_dim(rows, here * width, width, axis=1)]
     for shift in range(1, size):
         pairs = [(source, (source + shift) % size) for source in range(size)]
-        received.append(lax.ppermute(piece, name, pairs))
+        chunk = lax.dynamic_slice_in_dim(rows, ((here + shift) % size) * width, width, axis=1)
+        received.append(lax.ppermute(chunk, name, pairs))
     received = jnp.stack(received)
     order = (here - jnp.arange(size, dtype=jnp.int32)) % size
-    blocks = jnp.take(received, order, axis=0)
-    blocks = jnp.moveaxis(blocks, 0, 1)
-    return blocks.reshape(piece.shape[0], size * piece.shape[1], *piece.shape[2:])
+    return jnp.take(received, order, axis=0).reshape(size * rows.shape[0], width)
 
 
 def local(
@@ -63,7 +56,6 @@
     stale_values,
 ):
     rows_here, chan_width = latent.shape
-    patch_count = math.prod(lax.axis_size(name) for name in PATCH_AXES)
     chan_count = lax.axis_size("chan")
     device = lax.axis_index(PATCH_AXES)
     local_groups = GROUPS // chan_count
@@ -87,7 +79,7 @@
     inner = w_query.shape[1]
     shard_piece = lax.all_gather(normed, "chan", axis=1, tiled=True)
     outputs = []
-    for index, weight_matrix in enumerate((w_query, w_key, w_value)):
+    for weight_matrix in (w_query, w_key, w_value):
         outputs.append(jnp.dot(shard_piece, weight_matrix, preferred_element_type=jnp.float32))
     summed = tuple(outputs)
     queries = summed[0].astype(jnp.bfloat16)
@@ -96,7 +88,6 @@
     heads_here = inner // HEAD_DIM
     score_scale = HEAD_DIM ** (-0.5)
     split = lax.axis_size("px")
-    own_head = lax.axis_index("px")
 
     stacked = jnp.stack([stale_keys, stale_values]).reshape(2, rows_here, heads_here, HEAD_DIM)
     stacked = lax.all_to_all(stacked, "px", 2, 1, tiled=True).reshape(2, split * rows_here, HEAD_DIM)
@@ -153,7 +144,7 @@
     result = result.reshape(chan_count * split, rows_here, HEAD_DIM)
     attended = lax.all_to_all(result, ("chan", "px"), 0, 0, tiled=True)
     attended = jnp.transpose(attended, (1, 0, 2)).reshape(rows_here, chan_count * inner)
-    out_columns = lax.all_to_all(w_out, "chan", 1, 0, tiled=True)
+    out_columns = permute_columns(w_out, "chan", chan_width)
     projected = jnp.dot(attended, out_columns, preferred_element_type=jnp.float32)
     mixed = (latent.astype(jnp.float32) + projected).astype(jnp.bfloat16)
     return (mixed, fresh_keys, fresh_values)
@@ -177,6 +168,7 @@
         P(rows, "chan"),
     )
     out_specs = (P(rows, "chan"), P(rows, "chan"), P(rows, "chan"))
+
     return jax.shard_map(
         local, mesh=split_mesh, in_specs=in_specs, out_specs=out_specs, check_vma=False
     )

time: 138 us -> 144 us (1.043)
  starting transfers between devices: 40.2 us -> 51.1 us
  waiting for transfers between devices: 40.6 us -> 31.7 us
  blocking collectives: 14.8 us -> 18.8 us
    ppermute x0 -> x3, starting transfers between devices: none -> 16.4 us  [permute_columns(): received.append(lax.ppermute(chunk, name, pairs))]
    all_to_all x1 -> x0, waiting for transfers between devices: 9.59 us -> none  [local(): out_columns = lax.all_to_all(w_out, 'chan', 1, 0, tiled=True)]
    all_to_all x1 -> x0, starting transfers between devices: 8.17 us -> none  [local(): out_columns = lax.all_to_all(w_out, 'chan', 1, 0, tiled=True)]
    all_to_all x1, starting transfers between devices: 4.44 us -> 9.63 us  [local(): attended = lax.all_to_all(result, ('chan', 'px'), 0, 0, tiled=True)]
    all_to_all x3, waiting for transfers between devices: 13.1 us -> 17.2 us  [replicated_gather(): return lax.all_to_all(copies, name, 0, 0, tiled=True)]
    all_gather x1, blocking collectives: 14.8 us -> 18.8 us  [local(): shard_piece = lax.all_gather(normed, 'chan', axis=1, tiled=True)]
    all_to_all x1, waiting for transfers between devices: 3.29 us -> 0.01 us  [local(): lax.all_to_all(stacked, 'px', 2, 1, tiled=True)]
    all_to_all x3, starting transfers between devices: 19.5 us -> 17 us  [replicated_gather(): return lax.all_to_all(copies, name, 0, 0, tiled=True)]
  transfers between devices with their start and end apart: 8 -> 10, of which waited for: 7 -> 5; matrix products, arithmetic and copies ran while one was open for 14% -> 11% of each run, Pallas kernels for 0% -> 0%
where the time goes in v11:
time: 144 us; the launch traced here: 143 us
  starting transfers between devices  51.1 us (35%)
  waiting for transfers between devices  31.7 us (22%)
  blocking collectives  18.8 us (13%)
  between operations  15.2 us (11%)
  local copies, waits for them, and re-layouts  12.3 us (9%)
  matrix products  7.58 us (5%)
  other arithmetic  6.06 us (4%)
    all_gather x1, blocking collectives, local(): shard_piece = lax.all_gather(normed, 'chan', axis=1, tiled=True)  18.8 us
    all_to_all x3, waiting for transfers between devices, replicated_gather(): return lax.all_to_all(copies, name, 0, 0, tiled=True)  17.2 us
    all_to_all x3, starting transfers between devices, replicated_gather(): return lax.all_to_all(copies, name, 0, 0, tiled=True)  17 us
    ppermute x3, starting transfers between devices, permute_columns(): received.append(lax.ppermute(chunk, name, pairs))  16.4 us
    all_to_all x1, waiting for transfers between devices, local(): attended = lax.all_to_all(result, ('chan', 'px'), 0, 0, tiled=True)  9.8 us
    all_to_all x1, starting transfers between devices, local(): attended = lax.all_to_all(result, ('chan', 'px'), 0, 0, tiled=True)  9.63 us
    unnamed x22, local copies, waits for them, and re-layouts  5.17 us
    all_to_all x1, starting transfers between devices, local(): lax.all_to_all(stacked, 'px', 2, 1, tiled=True)  4.83 us
  transfers between devices with their start and end apart: 10, of which 5 were waited for; matrix products, arithmetic and copies ran while one was open for 11% of the time, Pallas kernels for 0%

profile of v11, /device:TPU:1, one launch (start us, length us, event | category | flops | bytes accessed | tf_op | source)
XLA Modules:
  0.0 142.6 jit_solution(12530011272068831920)
XLA Ops:
  7.2 1.0 copy.44
  8.2 0.9 copy.45
  9.1 0.8 reshape.320
  9.9 4.8 %all-to-all-start = ((bf16[4,2,4096]{2,1,0:T(2,128)(2,1)}), bf16[4,2,4096]{2,1,0:T(2,128)(2,1)S(1)}, u32[]{:S(2)}, u32[]{:S(2)}) async-start(bf16[4,2,4096]{2,1,0:T(2,128)(2,1)} %reshape.320), calls=%async_computation | async-start | bytes 131072 | tf_op jit(solution)/shard_map/all_to_all | solution.py:93
  14.7 1.5 %dynamic-slice_bitcast_fusion = (bf16[1,256,320]{2,1,0:T(8,128)(2,1)S(1)}, bf16[256,320]{1,0:T(8,128)(2,1)S(1)}, bf16[256,320]{1,0:T(8,128)(2,1)S(1)}, bf16[256,320]{1,0:T(8,128)(2,1)S(1)}) fusion(bf16[256,1280]{1,0:T(8,128)(2,1)} %param.19, s32[]{:T(128)S(6)} %select_n.109, s32[]{:T(128)S(6)} %select_n.111, s32[]{:T(128)S(6)} %select_n.115, s32[]{:T(128)S(6)} %select_n.113), kind=kLoop, calls=%fused_computation.25 | loop fusion | bytes 1310736 | tf_op jit(solution)/shard_map/stack | solution.py:40
  16.2 11.5 %collective-permute-start = (bf16[256,320]{1,0:T(8,128)(2,1)S(1)}, bf16[256,320]{1,0:T(8,128)(2,1)S(1)}, u32[]{:S(2)}, u32[]{:S(2)}) collective-permute-start(bf16[256,320]{1,0:T(8,128)(2,1)S(1)} %get-tuple-element.10), channel_id=1, source_target_pairs={{0,1},{1,2},{2,3},{3,0},{4,5},{5,6},{6,7},{7,4},{8,9},{9,10},{10,1... | collective-permute-start | bytes 491528 | tf_op jit(solution)/shard_map/ppermute | solution.py:39
  27.7 2.9 %collective-permute-start.1 = (bf16[256,320]{1,0:T(8,128)(2,1)S(1)}, bf16[256,320]{1,0:T(8,128)(2,1)S(1)}, u32[]{:S(2)}, u32[]{:S(2)}) collective-permute-start(bf16[256,320]{1,0:T(8,128)(2,1)S(1)} %get-tuple-element.12), channel_id=1, source_target_pairs={{0,2},{1,3},{2,0},{3,1},{4,6},{5,7},{6,4},{7,5},{8,10},{9,11},{10,... | collective-permute-start | bytes 491528 | tf_op jit(solution)/shard_map/ppermute | solution.py:39
  30.7 1.9 %collective-permute-start.2 = (bf16[256,320]{1,0:T(8,128)(2,1)S(1)}, bf16[256,320]{1,0:T(8,128)(2,1)S(1)}, u32[]{:S(2)}, u32[]{:S(2)}) collective-permute-start(bf16[256,320]{1,0:T(8,128)(2,1)S(1)} %get-tuple-element.11), channel_id=1, source_target_pairs={{0,3},{1,0},{2,1},{3,2},{4,7},{5,4},{6,5},{7,6},{8,11},{9,8},{10,9... | collective-permute-start | bytes 491528 | tf_op jit(solution)/shard_map/ppermute | solution.py:39
  32.6 0.8 convert_reduce_fusion.1
  33.5 0.1 reduce_sum.106
  33.7 0.1 sub.113
  33.8 0.8 fusion.9
  34.7 0.1 reduce_sum.109
  35.6 0.6 broadcast_in_dim.35
  36.2 6.7 %all-to-all-start.2 = ((f32[16,2,8]{2,1,0:T(2,128)}), f32[16,2,8]{2,1,0:T(2,128)S(1)}, u32[]{:S(2)}, u32[]{:S(2)}) async-start(f32[16,2,8]{2,1,0:T(2,128)} %broadcast_in_dim.35), calls=%async_computation.2 | async-start | bytes 32768 | tf_op jit(solution)/shard_map/all_to_all | solution.py:29
  42.9 0.1 reshape.321
  43.1 0.1 copy.46
  43.2 0.1 broadcast_in_dim.33
  43.4 6.4 %all-to-all-done.2 = f32[16,2,8]{2,1,0:T(2,128)S(1)} async-done(((f32[16,2,8]{2,1,0:T(2,128)}), f32[16,2,8]{2,1,0:T(2,128)S(1)}, u32[]{:S(2)}, u32[]{:S(2)}) %all-to-all-start.2) | async-done | bytes 1056 | tf_op jit(solution)/shard_map/all_to_all | solution.py:29
  49.8 0.7 broadcast_in_dim.34
  50.5 3.4 %all-to-all-start.1 = ((bf16[4,2,256,64]{2,3,1,0:T(8,128)(2,1)}), bf16[4,2,256,64]{2,3,1,0:T(8,128)(2,1)S(1)}, u32[]{:S(2)}, u32[]{:S(2)}) async-start(bf16[4,2,256,64]{2,3,1,0:T(8,128)(2,1)} %broadcast_in_dim.34), calls=%async_computation.1 | async-start | bytes 524288 | tf_op jit(solution)/shard_map/all_to_all | solution.py:29
  54.0 0.1 divide_multiply_fusion
  54.1 1.2 convolution_reduce_fusion
  55.3 4.2 %all-to-all-done.1 = bf16[4,2,256,64]{2,3,1,0:T(8,128)(2,1)S(1)} async-done(((bf16[4,2,256,64]{2,3,1,0:T(8,128)(2,1)}), bf16[4,2,256,64]{2,3,1,0:T(8,128)(2,1)S(1)}, u32[]{:S(2)}, u32[]{:S(2)}) %all-to-all-start.1) | async-done | bytes 262176 | tf_op jit(solution)/shard_map/all_to_all | solution.py:29
  59.5 0.8 copy.65
  60.3 0.2 fusion.19
  60.5 0.6 broadcast_in_dim.36
  61.1 6.8 %all-to-all-start.3 = ((f32[8,2,8]{2,1,0:T(2,128)}), f32[8,2,8]{2,1,0:T(2,128)S(1)}, u32[]{:S(2)}, u32[]{:S(2)}) async-start(f32[8,2,8]{2,1,0:T(2,128)} %broadcast_in_dim.36), calls=%async_computation.3 | async-start | bytes 16384 | tf_op jit(solution)/shard_map/all_to_all | solution.py:29
  67.9 6.6 %all-to-all-done.3 = f32[8,2,8]{2,1,0:T(2,128)S(1)} async-done(((f32[8,2,8]{2,1,0:T(2,128)}), f32[8,2,8]{2,1,0:T(2,128)S(1)}, u32[]{:S(2)}, u32[]{:S(2)}) %all-to-all-start.3) | async-done | bytes 544 | tf_op jit(solution)/shard_map/all_to_all | solution.py:29
  74.7 0.1 mul.123
  74.8 0.1 sub.119
  74.9 0.9 fusion.17
  75.8 18.8 %all-gather = bf16[4,320,64]{1,2,0:T(8,128)(2,1)S(1)} all-gather(bf16[1,320,64]{1,2,0:T(8,128)(2,1)S(1)} %fusion.17), channel_id=1, replica_groups=mesh['py'=8,'pz'=4,'px'=4,'chan'=4] {'chan'}, dimensions={0}, use_global_device_ids=true | all-gather | bytes 204800 | tf_op jit(solution)/shard_map/all_gather | solution.py:80
  94.6 0.2 copy.50
  94.7 0.2 reshape.314
  94.9 0.2 convolution_convert_fusion.1
  95.2 0.1 stack.55
  95.3 1.3 convolution_convert_fusion
  96.6 0.1 stack.56
  96.8 0.2 convolution_convert_fusion.2
  97.0 0.1 stack.54
  97.2 0.8 reshape.318
  98.0 3.3 %all-to-all-start.4 = ((bf16[4,2,6144]{2,1,0:T(2,128)(2,1)}), bf16[4,2,6144]{2,1,0:T(2,128)(2,1)S(1)}, u32[]{:S(2)}, u32[]{:S(2)}) async-start(bf16[4,2,6144]{2,1,0:T(2,128)(2,1)} %reshape.318), calls=%async_computation.4 | async-start | bytes 196608 | tf_op jit(solution)/shard_map/all_to_all | solution.py:101
  101.4 4.7 %all-to-all-done.4 = bf16[4,2,6144]{2,1,0:T(2,128)(2,1)S(1)} async-done(((bf16[4,2,6144]{2,1,0:T(2,128)(2,1)}), bf16[4,2,6144]{2,1,0:T(2,128)(2,1)S(1)}, u32[]{:S(2)}, u32[]{:S(2)}) %all-to-all-start.4) | async-done | bytes 98336 | tf_op jit(solution)/shard_map/all_to_all | solution.py:101
  106.0 0.2 reshape.319
  106.3 0.2 fusion.31
  106.4 0.1 broadcast_in_dim.38
  106.6 0.1 reshape.302
  106.6 0.2 fusion.15
  106.9 0.1 copy.60
  107.0 0.2 pad_maximum_fusion
  107.2 0.7 gather_fusion
  107.9 2.5 %bitcast_reduce_fusion = (f32[128,256]{1,0:T(8,128)S(1)}, f32[8192,256]{1,0:T(8,128)S(1)}) fusion(bf16[256,64]{1,0:T(8,128)(2,1)S(1)} %bitcast.115, bf16[2,8192,64]{1,2,0:T(8,128)(2,1)} %all-gather.3.cloned.1.call-done), kind=kOutput, calls=%fused_computation.7 | convolution fusion | flops 272596992 | bytes 9601024 | tf_op jit(solution)/shard_map/kd,qd->kq/dot_general | solution.py:107
  110.6 2.2 %convert_reduce_fusion = (f32[256]{0:T(256)S(1)}, bf16[8192,256]{1,0:T(8,128)(2,1)S(1)}) fusion(f32[128,256]{1,0:T(8,128)S(1)} %exponential_select_fusion, f32[8192,256]{1,0:T(8,128)S(1)} %get-tuple-element.21, f32[128,256]{1,0:T(8,128)S(1)} %get-tuple-element.20), kind=kLoop, calls=%fused_computation.8 | loop fusion | flops 14679808 | bytes 12846080 | tf_op jit(solution)/shard_map/reduce_sum | solution.py:134
  112.9 0.8 fusion.5
  113.7 0.1 copy.61
  113.8 0.9 reshape.322
  114.7 9.6 %all-to-all-start.5 = ((bf16[16,2,2048]{2,1,0:T(2,128)(2,1)}), bf16[16,2,2048]{2,1,0:T(2,128)(2,1)S(1)}, u32[]{:S(2)}, u32[]{:S(2)}) async-start(bf16[16,2,2048]{2,1,0:T(2,128)(2,1)} %reshape.322), calls=%async_computation.5 | async-start | bytes 262144 | tf_op jit(solution)/shard_map/all_to_all | solution.py:145
  124.4 0.2 broadcast_select_fusion
  124.5 9.8 %all-to-all-done.5 = bf16[16,2,2048]{2,1,0:T(2,128)(2,1)S(1)} async-done(((bf16[16,2,2048]{2,1,0:T(2,128)(2,1)}), bf16[16,2,2048]{2,1,0:T(2,128)(2,1)S(1)}, u32[]{:S(2)}, u32[]{:S(2)}) %all-to-all-start.5) | async-done | bytes 131104 | tf_op jit(solution)/shard_map/all_to_all | solution.py:145
  134.3 0.2 reshape.323
  134.5 0.2 copy.58
  134.7 0.2 reshape.304
  134.9 0.9 fusion.3
  (55 shorter events, 1.2 us)
Async XLA Ops:
  7.2 87.7 %copy-start = (bf16[1280,256]{1,0:T(8,128)(2,1)S(1)}, bf16[1280,256]{1,0:T(8,128)(2,1)}, u32[]{:S(2)}) copy-start(bf16[1280,256]{1,0:T(8,128)(2,1)} %param.17) | copy-start | bytes 1966084
  7.2 89.6 %copy-start.3 = (bf16[1280,256]{1,0:T(8,128)(2,1)S(1)}, bf16[1280,256]{1,0:T(8,128)(2,1)}, u32[]{:S(2)}) copy-start(bf16[1280,256]{1,0:T(8,128)(2,1)} %param.16) | copy-start | bytes 1966084
  9.9 25.7 %all-to-all-start = ((bf16[4,2,4096]{2,1,0:T(2,128)(2,1)}), bf16[4,2,4096]{2,1,0:T(2,128)(2,1)S(1)}, u32[]{:S(2)}, u32[]{:S(2)}) async-start(bf16[4,2,4096]{2,1,0:T(2,128)(2,1)} %reshape.320), calls=%async_computation | async-start | bytes 131072 | tf_op jit(solution)/shard_map/all_to_all | solution.py:93
  16.2 90.8 %collective-permute-start = (bf16[256,320]{1,0:T(8,128)(2,1)S(1)}, bf16[256,320]{1,0:T(8,128)(2,1)S(1)}, u32[]{:S(2)}, u32[]{:S(2)}) collective-permute-start(bf16[256,320]{1,0:T(8,128)(2,1)S(1)} %get-tuple-element.10), channel_id=1, source_target_pairs={{0,1},{1,2},{2,3},{3,0},{4,5},{5,6},{6,7},{7,4},{8,9},{9,10},{10,1... | collective-permute-start | bytes 491528 | tf_op jit(solution)/shard_map/ppermute | solution.py:39
  27.7 79.2 %collective-permute-start.1 = (bf16[256,320]{1,0:T(8,128)(2,1)S(1)}, bf16[256,320]{1,0:T(8,128)(2,1)S(1)}, u32[]{:S(2)}, u32[]{:S(2)}) collective-permute-start(bf16[256,320]{1,0:T(8,128)(2,1)S(1)} %get-tuple-element.12), channel_id=1, source_target_pairs={{0,2},{1,3},{2,0},{3,1},{4,6},{5,7},{6,4},{7,5},{8,10},{9,11},{10,... | collective-permute-start | bytes 491528 | tf_op jit(solution)/shard_map/ppermute | solution.py:39
  30.7 76.3 %collective-permute-start.2 = (bf16[256,320]{1,0:T(8,128)(2,1)S(1)}, bf16[256,320]{1,0:T(8,128)(2,1)S(1)}, u32[]{:S(2)}, u32[]{:S(2)}) collective-permute-start(bf16[256,320]{1,0:T(8,128)(2,1)S(1)} %get-tuple-element.11), channel_id=1, source_target_pairs={{0,3},{1,0},{2,1},{3,2},{4,7},{5,4},{6,5},{7,6},{8,11},{9,8},{10,9... | collective-permute-start | bytes 491528 | tf_op jit(solution)/shard_map/ppermute | solution.py:39
  36.2 13.6 %all-to-all-start.2 = ((f32[16,2,8]{2,1,0:T(2,128)}), f32[16,2,8]{2,1,0:T(2,128)S(1)}, u32[]{:S(2)}, u32[]{:S(2)}) async-start(f32[16,2,8]{2,1,0:T(2,128)} %broadcast_in_dim.35), calls=%async_computation.2 | async-start | bytes 32768 | tf_op jit(solution)/shard_map/all_to_all | solution.py:29
  50.5 9.0 %all-to-all-start.1 = ((bf16[4,2,256,64]{2,3,1,0:T(8,128)(2,1)}), bf16[4,2,256,64]{2,3,1,0:T(8,128)(2,1)S(1)}, u32[]{:S(2)}, u32[]{:S(2)}) async-start(bf16[4,2,256,64]{2,3,1,0:T(8,128)(2,1)} %broadcast_in_dim.34), calls=%async_computation.1 | async-start | bytes 524288 | tf_op jit(solution)/shard_map/all_to_all | solution.py:29
  53.9 54.0 %all-gather.3.cloned.1.call-start = ((), (), s32[]{:S(2)}) async-start(), calls=%async_computation.6 | async-start | bytes 2359296 | tf_op jit(solution)/shard_map/all_gather | solution.py:95
  61.1 13.4 %all-to-all-start.3 = ((f32[8,2,8]{2,1,0:T(2,128)}), f32[8,2,8]{2,1,0:T(2,128)S(1)}, u32[]{:S(2)}, u32[]{:S(2)}) async-start(f32[8,2,8]{2,1,0:T(2,128)} %broadcast_in_dim.36), calls=%async_computation.3 | async-start | bytes 16384 | tf_op jit(solution)/shard_map/all_to_all | solution.py:29
  95.1 15.3 %copy-start.4 = (bf16[64,256]{1,0:T(8,128)(2,1)}, bf16[64,256]{1,0:T(8,128)(2,1)S(1)}, u32[]{:S(2)}) copy-start(bf16[64,256]{1,0:T(8,128)(2,1)S(1)} %convolution_convert_fusion.1) | copy-start | bytes 98308
  96.6 13.9 %copy-start.5 = (bf16[64,256]{1,0:T(8,128)(2,1)}, bf16[64,256]{1,0:T(8,128)(2,1)S(1)}, u32[]{:S(2)}) copy-start(bf16[64,256]{1,0:T(8,128)(2,1)S(1)} %convolution_convert_fusion) | copy-start | bytes 98308
  98.0 8.0 %all-to-all-start.4 = ((bf16[4,2,6144]{2,1,0:T(2,128)(2,1)}), bf16[4,2,6144]{2,1,0:T(2,128)(2,1)S(1)}, u32[]{:S(2)}, u32[]{:S(2)}) async-start(bf16[4,2,6144]{2,1,0:T(2,128)(2,1)} %reshape.318), calls=%async_computation.4 | async-start | bytes 196608 | tf_op jit(solution)/shard_map/all_to_all | solution.py:101
  110.5 2.4 %copy-start.1 = (bf16[2,8192,64]{1,2,0:T(8,128)(2,1)S(1)}, bf16[2,8192,64]{1,2,0:T(8,128)(2,1)}, u32[]{:S(2)}) copy-start(bf16[2,8192,64]{1,2,0:T(8,128)(2,1)} %all-gather.3.cloned.1.call-done) | copy-start | bytes 6291460
  110.6 24.3 %copy-start.2 = (bf16[64,320]{1,0:T(8,128)(2,1)S(1)}, bf16[64,320]{1,0:T(8,128)(2,1)}, u32[]{:S(2)}) copy-start(bf16[64,320]{1,0:T(8,128)(2,1)} %param.11) | copy-start | bytes 122884
  114.7 19.6 %all-to-all-start.5 = ((bf16[16,2,2048]{2,1,0:T(2,128)(2,1)}), bf16[16,2,2048]{2,1,0:T(2,128)(2,1)S(1)}, u32[]{:S(2)}, u32[]{:S(2)}) async-start(bf16[16,2,2048]{2,1,0:T(2,128)(2,1)} %reshape.322), calls=%async_computation.5 | async-start | bytes 262144 | tf_op jit(solution)/shard_map/all_to_all | solution.py:145
Sparse Core Ops, SparseCore 0:
  60.4 42.3 all-gather.2

commit v12 on v10

--- a/solution.py
+++ b/solution.py
@@ -72,7 +72,7 @@
     count = rows_here * width
     group_mean = jnp.sum(values, axis=(0, 2)) / count
     spread = jnp.sum(jnp.square(values - group_mean[None, :, None]), axis=(0, 2))
-    for name in (PATCH_AXES[1:], PATCH_AXES[0]):
+    for name in (PATCH_AXES,):
         gathered = replicated_gather(jnp.stack([group_mean, spread]), name)
         group_mean = jnp.mean(gathered[:, 0], axis=0)
         offset = gathered[:, 0] - group_mean[None, :]
@@ -85,7 +85,8 @@
         jnp.bfloat16
     )
     inner = w_query.shape[1]
-    shard_piece = lax.all_gather(normed, "chan", axis=1, tiled=True)
+    shard_piece = replicated_gather(normed, "chan")
+    shard_piece = jnp.moveaxis(shard_piece, 0, 1).reshape(rows_here, chan_count * chan_width)
     outputs = []
     for index, weight_matrix in enumerate((w_query, w_key, w_value)):
         outputs.append(jnp.dot(shard_piece, weight_matrix, preferred_element_type=jnp.float32))

time: 138 us -> 141 us (1.022)
  the two profiles are of different devices: /device:TPU:1 before, /device:TPU:65 now
where the time goes in v12:
time: 141 us; the launch traced here: 140 us
  waiting for transfers between devices  49.5 us (35%)
  starting transfers between devices  43.3 us (31%)
  between operations  15.1 us (11%)
  local copies, waits for them, and re-layouts  11.8 us (8%)
  blocking collectives  8.29 us (6%)
  matrix products  6.59 us (5%)
  other arithmetic  5.72 us (4%)
    all_to_all x3, starting transfers between devices, replicated_gather(): return lax.all_to_all(copies, name, 0, 0, tiled=True)  30.9 us
    all_to_all x3, waiting for transfers between devices, replicated_gather(): return lax.all_to_all(copies, name, 0, 0, tiled=True)  22 us
    all_to_all x1, waiting for transfers between devices, local(): out_columns = lax.all_to_all(w_out, 'chan', 1, 0, tiled=True)  12.8 us
    all_to_all x1, waiting for transfers between devices, local(): attended = lax.all_to_all(result, ('chan', 'px'), 0, 0, tiled=True)  9.95 us
    all_to_all x1, blocking collectives, local(): lax.all_to_all(stacked, 'px', 2, 1, tiled=True)  8.29 us
    unnamed x24, local copies, waits for them, and re-layouts  6.57 us
    all_to_all x1, starting transfers between devices, local(): out_columns = lax.all_to_all(w_out, 'chan', 1, 0, tiled=True)  5.11 us
    all_to_all x1, waiting for transfers between devices, local(): lax.all_to_all(fresh, 'px', 2, 1, tiled=True)  4.6 us
  transfers between devices with their start and end apart: 7, of which 6 were waited for; matrix products, arithmetic and copies ran while one was open for 13% of the time, Pallas kernels for 0%

profile of v12, /device:TPU:65, one launch (start us, length us, event | category | flops | bytes accessed | tf_op | source)
XLA Modules:
  0.0 140.3 jit_solution(13427605626186821293)
XLA Ops:
  7.2 1.0 copy.78
  8.2 0.9 copy.79
  9.1 0.2 reshape.204
  9.3 8.3 %all_to_all.69 = bf16[4,2,4096]{2,1,0:T(2,128)(2,1)S(1)} all-to-all(bf16[4,2,4096]{2,1,0:T(2,128)(2,1)S(1)} %reshape.204), channel_id=1, replica_groups=mesh['py'=8,'pz'=4,'px'=4,'chan'=4] {'px'}, dimensions={0} | all-to-all | bytes 131072 | tf_op jit(solution)/shard_map/all_to_all | solution.py:103
  17.6 0.1 reshape.205
  17.7 0.1 copy.80
  17.9 0.1 broadcast_in_dim.22
  18.0 0.7 broadcast_in_dim.23
  18.7 6.3 %all-to-all-start.1 = ((bf16[4,2,256,64]{2,3,1,0:T(8,128)(2,1)}), bf16[4,2,256,64]{2,3,1,0:T(8,128)(2,1)S(1)}, u32[]{:S(2)}, u32[]{:S(2)}) async-start(bf16[4,2,256,64]{2,3,1,0:T(8,128)(2,1)} %broadcast_in_dim.23), calls=%async_computation.1 | async-start | bytes 524288 | tf_op jit(solution)/shard_map/all_to_all | solution.py:35
  25.1 0.8 convert_reduce_fusion.1
  25.9 0.1 reduce_sum.78
  26.0 0.1 reduce_sum.79
  26.1 4.3 %all-to-all-done.1 = bf16[4,2,256,64]{2,3,1,0:T(8,128)(2,1)S(1)} async-done(((bf16[4,2,256,64]{2,3,1,0:T(8,128)(2,1)}), bf16[4,2,256,64]{2,3,1,0:T(8,128)(2,1)S(1)}, u32[]{:S(2)}, u32[]{:S(2)}) %all-to-all-start.1) | async-done | bytes 262176 | tf_op jit(solution)/shard_map/all_to_all | solution.py:35
  30.4 0.7 copy.101
  31.2 0.1 sub.85
  31.3 0.1 sub.86
  31.4 0.8 fusion.9
  32.2 0.1 reduce_sum.81
  32.3 0.1 reduce_sum.82
  32.4 0.7 broadcast_in_dim.24
  33.1 12.4 %all-to-all-start.2 = ((f32[128,2,8]{2,1,0:T(2,128)}), f32[128,2,8]{2,1,0:T(2,128)S(1)}, u32[]{:S(2)}, u32[]{:S(2)}) async-start(f32[128,2,8]{2,1,0:T(2,128)} %broadcast_in_dim.24), calls=%async_computation.2 | async-start | bytes 262144 | tf_op jit(solution)/shard_map/all_to_all | solution.py:35
  46.2 0.1 divide_multiply_fusion
  46.3 1.2 convolution_reduce_fusion
  47.5 9.3 %all-to-all-done.2 = f32[128,2,8]{2,1,0:T(2,128)S(1)} async-done(((f32[128,2,8]{2,1,0:T(2,128)}), f32[128,2,8]{2,1,0:T(2,128)S(1)}, u32[]{:S(2)}, u32[]{:S(2)}) %all-to-all-start.2) | async-done | bytes 8224 | tf_op jit(solution)/shard_map/all_to_all | solution.py:35
  56.8 0.2 slice_reduce_fusion.1
  57.0 0.2 fusion.18
  57.3 0.1 mul.95
  57.4 0.1 sub.89
  57.4 0.1 sub.90
  57.5 0.9 fusion.14
  58.4 0.7 broadcast_in_dim.28
  59.1 12.1 %all-to-all-start.3 = ((bf16[4,64,320]{2,1,0:T(8,128)(2,1)}), bf16[4,64,320]{2,1,0:T(8,128)(2,1)S(1)}, u32[]{:S(2)}, u32[]{:S(2)}) async-start(bf16[4,64,320]{2,1,0:T(8,128)(2,1)} %broadcast_in_dim.28), calls=%async_computation.3 | async-start | bytes 393216 | tf_op jit(solution)/shard_map/all_to_all | solution.py:35
  71.2 2.2 %copy.93 = bf16[256,1280]{0,1:T(8,128)(2,1)} copy(bf16[256,1280]{1,0:T(8,128)(2,1)} %param.19) | data formatting | bytes 1310720 | tf_op args[8]
  73.4 8.4 %all-to-all-done.3 = bf16[4,64,320]{2,1,0:T(8,128)(2,1)S(1)} async-done(((bf16[4,64,320]{2,1,0:T(8,128)(2,1)}), bf16[4,64,320]{2,1,0:T(8,128)(2,1)S(1)}, u32[]{:S(2)}, u32[]{:S(2)}) %all-to-all-start.3) | async-done | bytes 163872 | tf_op jit(solution)/shard_map/all_to_all | solution.py:35
  81.8 0.2 copy.84
  82.0 0.2 reshape.193
  82.2 0.2 convolution_convert_fusion.1
  82.4 0.1 stack.34
  82.5 0.2 convolution_convert_fusion
  82.8 0.1 stack.35
  82.9 0.2 convolution_convert_fusion.2
  83.2 0.1 stack.33
  83.4 0.8 reshape.202
  84.2 3.3 %all-to-all-start.4 = ((bf16[4,2,6144]{2,1,0:T(2,128)(2,1)}), bf16[4,2,6144]{2,1,0:T(2,128)(2,1)S(1)}, u32[]{:S(2)}, u32[]{:S(2)}) async-start(bf16[4,2,6144]{2,1,0:T(2,128)(2,1)} %reshape.202), calls=%async_computation.4 | async-start | bytes 196608 | tf_op jit(solution)/shard_map/all_to_all | solution.py:111
  87.5 4.6 %all-to-all-done.4 = bf16[4,2,6144]{2,1,0:T(2,128)(2,1)S(1)} async-done(((bf16[4,2,6144]{2,1,0:T(2,128)(2,1)}), bf16[4,2,6144]{2,1,0:T(2,128)(2,1)S(1)}, u32[]{:S(2)}, u32[]{:S(2)}) %all-to-all-start.4) | async-done | bytes 98336 | tf_op jit(solution)/shard_map/all_to_all | solution.py:111
  92.1 5.1 %all-to-all-start.6 = ((bf16[256,4,320]{0,2,1:T(8,128)(2,1)}), bf16[256,4,320]{0,2,1:T(8,128)(2,1)S(1)}, u32[]{:S(2)}, u32[]{:S(2)}) async-start(bf16[256,4,320]{0,2,1:T(8,128)(2,1)} %bitcast.26), calls=%async_computation.6 | async-start | bytes 1310720 | tf_op jit(solution)/shard_map/all_to_all | solution.py:157
  97.2 0.2 reshape.203
  97.5 0.2 fusion.25
  97.6 0.1 broadcast_in_dim.31
  97.8 0.1 reshape.196
  97.9 0.2 fusion.15
  98.1 0.1 copy.96
  98.2 2.5 %bitcast_reduce_fusion = (f32[128,256]{1,0:T(8,128)S(1)}, f32[8192,256]{1,0:T(8,128)S(1)}) fusion(bf16[256,64]{1,0:T(8,128)(2,1)S(1)} %bitcast.101, bf16[2,8192,64]{1,2,0:T(8,128)(2,1)} %all-gather.2.cloned.1.call-done), kind=kOutput, calls=%fused_computation.6 | convolution fusion | flops 272596992 | bytes 9601024 | tf_op jit(solution)/shard_map/kd,qd->kq/dot_general | solution.py:117
  100.9 2.2 %convert_reduce_fusion = (f32[256]{0:T(256)S(1)}, bf16[8192,256]{1,0:T(8,128)(2,1)S(1)}) fusion(f32[128,256]{1,0:T(8,128)S(1)} %exponential_select_fusion, f32[8192,256]{1,0:T(8,128)S(1)} %get-tuple-element.13, f32[128,256]{1,0:T(8,128)S(1)} %get-tuple-element.12), kind=kLoop, calls=%fused_computation.7 | loop fusion | flops 14679808 | bytes 12846080 | tf_op jit(solution)/shard_map/reduce_sum | solution.py:144
  103.1 0.8 fusion.5
  103.9 0.1 copy.97
  104.1 0.9 reshape.206
  105.0 12.8 %all-to-all-done.6 = bf16[256,4,320]{0,2,1:T(8,128)(2,1)S(1)} async-done(((bf16[256,4,320]{0,2,1:T(8,128)(2,1)}), bf16[256,4,320]{0,2,1:T(8,128)(2,1)S(1)}, u32[]{:S(2)}, u32[]{:S(2)}) %all-to-all-start.6) | async-done | bytes 655392 | tf_op jit(solution)/shard_map/all_to_all | solution.py:157
  117.8 4.0 %all-to-all-start.5 = ((bf16[16,2,2048]{2,1,0:T(2,128)(2,1)}), bf16[16,2,2048]{2,1,0:T(2,128)(2,1)S(1)}, u32[]{:S(2)}, u32[]{:S(2)}) async-start(bf16[16,2,2048]{2,1,0:T(2,128)(2,1)} %reshape.206), calls=%async_computation.5 | async-start | bytes 262144 | tf_op jit(solution)/shard_map/all_to_all | solution.py:155
  121.9 10.0 %all-to-all-done.5 = bf16[16,2,2048]{2,1,0:T(2,128)(2,1)S(1)} async-done(((bf16[16,2,2048]{2,1,0:T(2,128)(2,1)}), bf16[16,2,2048]{2,1,0:T(2,128)(2,1)S(1)}, u32[]{:S(2)}, u32[]{:S(2)}) %all-to-all-start.5) | async-done | bytes 131104 | tf_op jit(solution)/shard_map/all_to_all | solution.py:155
  131.8 0.2 reshape.207
  132.1 0.2 copy.92
  132.2 0.2 reshape.198
  132.5 1.0 fusion.3
  (40 shorter events, 0.7 us)
Async XLA Ops:
  7.2 75.0 %copy-start = (bf16[1280,256]{1,0:T(8,128)(2,1)S(1)}, bf16[1280,256]{1,0:T(8,128)(2,1)}, u32[]{:S(2)}) copy-start(bf16[1280,256]{1,0:T(8,128)(2,1)} %param.17) | copy-start | bytes 1966084
  7.2 75.4 %copy-start.3 = (bf16[1280,256]{1,0:T(8,128)(2,1)S(1)}, bf16[1280,256]{1,0:T(8,128)(2,1)}, u32[]{:S(2)}) copy-start(bf16[1280,256]{1,0:T(8,128)(2,1)} %param.18) | copy-start | bytes 1966084
  7.2 75.7 %copy-start.4 = (bf16[1280,256]{1,0:T(8,128)(2,1)S(1)}, bf16[1280,256]{1,0:T(8,128)(2,1)}, u32[]{:S(2)}) copy-start(bf16[1280,256]{1,0:T(8,128)(2,1)} %param.16) | copy-start | bytes 1966084
  18.7 11.7 %all-to-all-start.1 = ((bf16[4,2,256,64]{2,3,1,0:T(8,128)(2,1)}), bf16[4,2,256,64]{2,3,1,0:T(8,128)(2,1)S(1)}, u32[]{:S(2)}, u32[]{:S(2)}) async-start(bf16[4,2,256,64]{2,3,1,0:T(8,128)(2,1)} %broadcast_in_dim.23), calls=%async_computation.1 | async-start | bytes 524288 | tf_op jit(solution)/shard_map/all_to_all | solution.py:35
  25.1 73.1 %all-gather.2.cloned.1.call-start = ((), (), s32[]{:S(2)}) async-start(), calls=%async_computation.7 | async-start | bytes 2359296 | tf_op jit(solution)/shard_map/all_gather | solution.py:105
  33.1 23.7 %all-to-all-start.2 = ((f32[128,2,8]{2,1,0:T(2,128)}), f32[128,2,8]{2,1,0:T(2,128)S(1)}, u32[]{:S(2)}, u32[]{:S(2)}) async-start(f32[128,2,8]{2,1,0:T(2,128)} %broadcast_in_dim.24), calls=%async_computation.2 | async-start | bytes 262144 | tf_op jit(solution)/shard_map/all_to_all | solution.py:35
  59.1 22.7 %all-to-all-start.3 = ((bf16[4,64,320]{2,1,0:T(8,128)(2,1)}), bf16[4,64,320]{2,1,0:T(8,128)(2,1)S(1)}, u32[]{:S(2)}, u32[]{:S(2)}) async-start(bf16[4,64,320]{2,1,0:T(8,128)(2,1)} %broadcast_in_dim.28), calls=%async_computation.3 | async-start | bytes 393216 | tf_op jit(solution)/shard_map/all_to_all | solution.py:35
  82.4 18.4 %copy-start.5 = (bf16[64,256]{1,0:T(8,128)(2,1)}, bf16[64,256]{1,0:T(8,128)(2,1)S(1)}, u32[]{:S(2)}) copy-start(bf16[64,256]{1,0:T(8,128)(2,1)S(1)} %convolution_convert_fusion.1) | copy-start | bytes 98308
  82.8 18.0 %copy-start.6 = (bf16[64,256]{1,0:T(8,128)(2,1)}, bf16[64,256]{1,0:T(8,128)(2,1)S(1)}, u32[]{:S(2)}) copy-start(bf16[64,256]{1,0:T(8,128)(2,1)S(1)} %convolution_convert_fusion) | copy-start | bytes 98308
  84.2 7.9 %all-to-all-start.4 = ((bf16[4,2,6144]{2,1,0:T(2,128)(2,1)}), bf16[4,2,6144]{2,1,0:T(2,128)(2,1)S(1)}, u32[]{:S(2)}, u32[]{:S(2)}) async-start(bf16[4,2,6144]{2,1,0:T(2,128)(2,1)} %reshape.202), calls=%async_computation.4 | async-start | bytes 196608 | tf_op jit(solution)/shard_map/all_to_all | solution.py:111
  92.1 25.7 %all-to-all-start.6 = ((bf16[256,4,320]{0,2,1:T(8,128)(2,1)}), bf16[256,4,320]{0,2,1:T(8,128)(2,1)S(1)}, u32[]{:S(2)}, u32[]{:S(2)}) async-start(bf16[256,4,320]{0,2,1:T(8,128)(2,1)} %bitcast.26), calls=%async_computation.6 | async-start | bytes 1310720 | tf_op jit(solution)/shard_map/all_to_all | solution.py:157
  100.8 2.4 %copy-start.1 = (bf16[2,8192,64]{1,2,0:T(8,128)(2,1)S(1)}, bf16[2,8192,64]{1,2,0:T(8,128)(2,1)}, u32[]{:S(2)}) copy-start(bf16[2,8192,64]{1,2,0:T(8,128)(2,1)} %all-gather.2.cloned.1.call-done) | copy-start | bytes 6291460
  100.9 31.6 %copy-start.2 = (bf16[64,320]{1,0:T(8,128)(2,1)S(1)}, bf16[64,320]{1,0:T(8,128)(2,1)}, u32[]{:S(2)}) copy-start(bf16[64,320]{1,0:T(8,128)(2,1)} %param.11) | copy-start | bytes 122884
  117.8 14.0 %all-to-all-start.5 = ((bf16[16,2,2048]{2,1,0:T(2,128)(2,1)}), bf16[16,2,2048]{2,1,0:T(2,128)(2,1)S(1)}, u32[]{:S(2)}, u32[]{:S(2)}) async-start(bf16[16,2,2048]{2,1,0:T(2,128)(2,1)} %reshape.206), calls=%async_computation.5 | async-start | bytes 262144 | tf_op jit(solution)/shard_map/all_to_all | solution.py:155
Sparse Core Ops, SparseCore 0:
  31.3 43.9 all-gather.1

commit v13 on v11

--- a/solution.py
+++ b/solution.py
@@ -27,19 +27,6 @@
     size = lax.axis_size(name)
     copies = jnp.broadcast_to(piece[None], (size,) + piece.shape)
     return lax.all_to_all(copies, name, 0, 0, tiled=True)
-
-
-def permute_columns(rows, name, width):
-    size = lax.axis_size(name)
-    here = lax.axis_index(name)
-    received = [lax.dynamic_slice_in_dim(rows, here * width, width, axis=1)]
-    for shift in range(1, size):
-        pairs = [(source, (source + shift) % size) for source in range(size)]
-        chunk = lax.dynamic_slice_in_dim(rows, ((here + shift) % size) * width, width, axis=1)
-        received.append(lax.ppermute(chunk, name, pairs))
-    received = jnp.stack(received)
-    order = (here - jnp.arange(size, dtype=jnp.int32)) % size
-    return jnp.take(received, order, axis=0).reshape(size * rows.shape[0], width)
 
 
 def local(
@@ -98,7 +85,8 @@
     fresh = jnp.stack([queries, fresh_keys, fresh_values]).reshape(
         3, rows_here, heads_here, HEAD_DIM
     )
-    fresh = lax.all_to_all(fresh, "px", 2, 1, tiled=True).reshape(3, split, rows_here, HEAD_DIM)
+    fresh = lax.all_to_all(fresh, "px", 2, 1, tiled=True)
+    fresh = fresh.reshape(3, split, rows_here, HEAD_DIM)
     query_rows = fresh[0].reshape(split * rows_here, HEAD_DIM)
 
     key_rows = stacked[0]
@@ -144,7 +132,7 @@
     result = result.reshape(chan_count * split, rows_here, HEAD_DIM)
     attended = lax.all_to_all(result, ("chan", "px"), 0, 0, tiled=True)
     attended = jnp.transpose(attended, (1, 0, 2)).reshape(rows_here, chan_count * inner)
-    out_columns = permute_columns(w_out, "chan", chan_width)
+    out_columns = lax.all_to_all(w_out, "chan", 1, 0, tiled=True)
     projected = jnp.dot(attended, out_columns, preferred_element_type=jnp.float32)
     mixed = (latent.astype(jnp.float32) + projected).astype(jnp.bfloat16)
     return (mixed, fresh_keys, fresh_values)

time: 144 us -> 138 us (0.958)
  starting transfers between devices: 51.1 us -> 40.2 us
  waiting for transfers between devices: 31.7 us -> 40.6 us
  blocking collectives: 18.8 us -> 14.8 us
    ppermute x3 -> x0, starting transfers between devices: 16.4 us -> none  [permute_columns(): received.append(lax.ppermute(chunk, name, pairs))]
    all_to_all x1 -> x2, waiting for transfers between devices: 4.65 us -> 14.2 us  [the longest x1 9.59 us: local(): out_columns = lax.all_to_all(w_out, 'chan', 1, 0, tiled=True)]
    all_to_all x1 -> x2, starting transfers between devices: 3.3 us -> 11.5 us  [the longest x1 8.17 us: local(): out_columns = lax.all_to_all(w_out, 'chan', 1, 0, tiled=True)]
    all_to_all x1, starting transfers between devices: 9.63 us -> 4.44 us  [local(): attended = lax.all_to_all(result, ('chan', 'px'), 0, 0, tiled=True)]
    all_to_all x3, waiting for transfers between devices: 17.2 us -> 13.1 us  [replicated_gather(): return lax.all_to_all(copies, name, 0, 0, tiled=True)]
    all_gather x1, blocking collectives: 18.8 us -> 14.8 us  [local(): shard_piece = lax.all_gather(normed, 'chan', axis=1, tiled=True)]
    all_to_all x1, waiting for transfers between devices: 0.01 us -> 3.29 us  [local(): lax.all_to_all(stacked, 'px', 2, 1, tiled=True)]
    all_to_all x3, starting transfers between devices: 17 us -> 19.5 us  [replicated_gather(): return lax.all_to_all(copies, name, 0, 0, tiled=True)]
  transfers between devices with their start and end apart: 10 -> 8, of which waited for: 5 -> 7; matrix products, arithmetic and copies ran while one was open for 11% -> 14% of each run, Pallas kernels for 0% -> 0%
where the time goes in v13:
time: 138 us; the launch traced here: 136 us
  waiting for transfers between devices  40.6 us (29%)
  starting transfers between devices  40.2 us (29%)
  between operations  15.1 us (11%)
  blocking collectives  14.8 us (11%)
  local copies, waits for them, and re-layouts  12.2 us (9%)
  matrix products  7.67 us (6%)
  other arithmetic  5.68 us (4%)
    all_to_all x3, starting transfers between devices, replicated_gather(): return lax.all_to_all(copies, name, 0, 0, tiled=True)  19.5 us
    all_gather x1, blocking collectives, local(): shard_piece = lax.all_gather(normed, 'chan', axis=1, tiled=True)  14.8 us
    all_to_all x3, waiting for transfers between devices, replicated_gather(): return lax.all_to_all(copies, name, 0, 0, tiled=True)  13.1 us
    all_to_all x1, waiting for transfers between devices, local(): attended = lax.all_to_all(result, ('chan', 'px'), 0, 0, tiled=True)  9.99 us
    all_to_all x1, waiting for transfers between devices, local(): out_columns = lax.all_to_all(w_out, 'chan', 1, 0, tiled=True)  9.59 us
    all_to_all x1, starting transfers between devices, local(): out_columns = lax.all_to_all(w_out, 'chan', 1, 0, tiled=True)  8.17 us
    unnamed x23, local copies, waits for them, and re-layouts  7.33 us
    all_to_all x1, starting transfers between devices, local(): lax.all_to_all(stacked, 'px', 2, 1, tiled=True)  4.83 us
  transfers between devices with their start and end apart: 8, of which 7 were waited for; matrix products, arithmetic and copies ran while one was open for 14% of the time, Pallas kernels for 0%

profile of v13, /device:TPU:1, one launch (start us, length us, event | category | flops | bytes accessed | tf_op | source)
XLA Modules:
  0.0 136.3 jit_solution(7807051679854844824)
XLA Ops:
  7.2 1.0 copy.48
  8.2 0.9 copy.49
  9.1 0.8 reshape.228
  9.9 4.8 %all-to-all-start = ((bf16[4,2,4096]{2,1,0:T(2,128)(2,1)}), bf16[4,2,4096]{2,1,0:T(2,128)(2,1)S(1)}, u32[]{:S(2)}, u32[]{:S(2)}) async-start(bf16[4,2,4096]{2,1,0:T(2,128)(2,1)} %reshape.228), calls=%async_computation | async-start | bytes 131072 | tf_op jit(solution)/shard_map/all_to_all | solution.py:80
  14.7 0.8 convert_reduce_fusion.1
  15.5 0.1 reduce_sum.105
  15.6 0.1 reduce_sum.106
  15.8 0.1 sub.94
  15.9 3.3 %all-to-all-done = bf16[4,2,4096]{2,1,0:T(2,128)(2,1)S(1)} async-done(((bf16[4,2,4096]{2,1,0:T(2,128)(2,1)}), bf16[4,2,4096]{2,1,0:T(2,128)(2,1)S(1)}, u32[]{:S(2)}, u32[]{:S(2)}) %all-to-all-start) | async-done | bytes 65568 | tf_op jit(solution)/shard_map/all_to_all | solution.py:80
  19.2 0.1 reshape.229
  19.3 0.1 copy.50
  19.5 0.1 broadcast_in_dim.22
  19.6 0.7 broadcast_in_dim.23
  20.3 7.0 %all-to-all-start.1 = ((bf16[4,2,256,64]{2,3,1,0:T(8,128)(2,1)}), bf16[4,2,256,64]{2,3,1,0:T(8,128)(2,1)S(1)}, u32[]{:S(2)}, u32[]{:S(2)}) async-start(bf16[4,2,256,64]{2,3,1,0:T(8,128)(2,1)} %broadcast_in_dim.23), calls=%async_computation.1 | async-start | bytes 524288 | tf_op jit(solution)/shard_map/all_to_all | solution.py:29
  27.3 0.8 fusion.9
  28.1 0.1 reduce_sum.108
  28.2 0.1 reduce_sum.109
  29.0 0.1 divide_multiply_fusion
  29.1 3.8 %all-to-all-done.1 = bf16[4,2,256,64]{2,3,1,0:T(8,128)(2,1)S(1)} async-done(((bf16[4,2,256,64]{2,3,1,0:T(8,128)(2,1)}), bf16[4,2,256,64]{2,3,1,0:T(8,128)(2,1)S(1)}, u32[]{:S(2)}, u32[]{:S(2)}) %all-to-all-start.1) | async-done | bytes 262176 | tf_op jit(solution)/shard_map/all_to_all | solution.py:29
  32.9 0.6 broadcast_in_dim.24
  33.5 4.0 %all-to-all-start.2 = ((f32[16,2,8]{2,1,0:T(2,128)}), f32[16,2,8]{2,1,0:T(2,128)S(1)}, u32[]{:S(2)}, u32[]{:S(2)}) async-start(f32[16,2,8]{2,1,0:T(2,128)} %broadcast_in_dim.24), calls=%async_computation.2 | async-start | bytes 32768 | tf_op jit(solution)/shard_map/all_to_all | solution.py:29
  37.6 1.2 convolution_reduce_fusion
  38.8 0.7 copy.71
  39.5 4.9 %all-to-all-done.2 = f32[16,2,8]{2,1,0:T(2,128)S(1)} async-done(((f32[16,2,8]{2,1,0:T(2,128)}), f32[16,2,8]{2,1,0:T(2,128)S(1)}, u32[]{:S(2)}, u32[]{:S(2)}) %all-to-all-start.2) | async-done | bytes 1056 | tf_op jit(solution)/shard_map/all_to_all | solution.py:29
  44.5 0.2 fusion.19
  44.7 0.6 broadcast_in_dim.25
  45.3 8.5 %all-to-all-start.3 = ((f32[8,2,8]{2,1,0:T(2,128)}), f32[8,2,8]{2,1,0:T(2,128)S(1)}, u32[]{:S(2)}, u32[]{:S(2)}) async-start(f32[8,2,8]{2,1,0:T(2,128)} %broadcast_in_dim.25), calls=%async_computation.3 | async-start | bytes 16384 | tf_op jit(solution)/shard_map/all_to_all | solution.py:29
  53.8 2.2 %copy.63 = bf16[256,1280]{0,1:T(8,128)(2,1)} copy(bf16[256,1280]{1,0:T(8,128)(2,1)} %param.19) | data formatting | bytes 1310720 | tf_op args[8]
  56.0 4.4 %all-to-all-done.3 = f32[8,2,8]{2,1,0:T(2,128)S(1)} async-done(((f32[8,2,8]{2,1,0:T(2,128)}), f32[8,2,8]{2,1,0:T(2,128)S(1)}, u32[]{:S(2)}, u32[]{:S(2)}) %all-to-all-start.3) | async-done | bytes 544 | tf_op jit(solution)/shard_map/all_to_all | solution.py:29
  60.5 0.1 mul.110
  60.5 0.1 mul.111
  60.7 0.1 sub.100
  60.8 0.9 fusion.17
  61.6 14.8 %all-gather = bf16[4,320,64]{1,2,0:T(8,128)(2,1)S(1)} all-gather(bf16[1,320,64]{1,2,0:T(8,128)(2,1)S(1)} %fusion.17), channel_id=1, replica_groups=mesh['py'=8,'pz'=4,'px'=4,'chan'=4] {'chan'}, dimensions={0}, use_global_device_ids=true | all-gather | bytes 204800 | tf_op jit(solution)/shard_map/all_gather | solution.py:67
  76.4 0.2 copy.54
  76.6 0.2 reshape.222
  76.8 0.2 convolution_convert_fusion.1
  77.0 0.1 stack.40
  77.1 1.3 convolution_convert_fusion
  78.5 0.1 stack.41
  78.6 0.2 convolution_convert_fusion.2
  78.9 0.1 stack.39
  79.1 0.8 reshape.226
  79.9 3.3 %all-to-all-start.4 = ((bf16[4,2,6144]{2,1,0:T(2,128)(2,1)}), bf16[4,2,6144]{2,1,0:T(2,128)(2,1)S(1)}, u32[]{:S(2)}, u32[]{:S(2)}) async-start(bf16[4,2,6144]{2,1,0:T(2,128)(2,1)} %reshape.226), calls=%async_computation.4 | async-start | bytes 196608 | tf_op jit(solution)/shard_map/all_to_all | solution.py:88
  83.2 4.6 %all-to-all-done.4 = bf16[4,2,6144]{2,1,0:T(2,128)(2,1)S(1)} async-done(((bf16[4,2,6144]{2,1,0:T(2,128)(2,1)}), bf16[4,2,6144]{2,1,0:T(2,128)(2,1)S(1)}, u32[]{:S(2)}, u32[]{:S(2)}) %all-to-all-start.4) | async-done | bytes 98336 | tf_op jit(solution)/shard_map/all_to_all | solution.py:88
  87.9 8.2 %all-to-all-start.6 = ((bf16[256,4,320]{0,2,1:T(8,128)(2,1)}), bf16[256,4,320]{0,2,1:T(8,128)(2,1)S(1)}, u32[]{:S(2)}, u32[]{:S(2)}) async-start(bf16[256,4,320]{0,2,1:T(8,128)(2,1)} %bitcast.30), calls=%async_computation.6 | async-start | bytes 1310720 | tf_op jit(solution)/shard_map/all_to_all | solution.py:135
  96.0 0.2 reshape.227
  96.3 0.2 fusion.28
  96.4 0.1 broadcast_in_dim.30
  96.6 0.1 reshape.218
  96.7 0.2 fusion.15
  96.9 0.1 copy.66
  97.0 2.5 %bitcast_reduce_fusion = (f32[128,256]{1,0:T(8,128)S(1)}, f32[8192,256]{1,0:T(8,128)S(1)}) fusion(bf16[256,64]{1,0:T(8,128)(2,1)S(1)} %bitcast.112, bf16[2,8192,64]{1,2,0:T(8,128)(2,1)} %all-gather.3.cloned.1.call-done), kind=kOutput, calls=%fused_computation.6 | convolution fusion | flops 272596992 | bytes 9601024 | tf_op jit(solution)/shard_map/kd,qd->kq/dot_general | solution.py:95
  99.7 2.2 %convert_reduce_fusion = (f32[256]{0:T(256)S(1)}, bf16[8192,256]{1,0:T(8,128)(2,1)S(1)}) fusion(f32[128,256]{1,0:T(8,128)S(1)} %exponential_select_fusion, f32[8192,256]{1,0:T(8,128)S(1)} %get-tuple-element.17, f32[128,256]{1,0:T(8,128)S(1)} %get-tuple-element.16), kind=kLoop, calls=%fused_computation.7 | loop fusion | flops 14679808 | bytes 12846080 | tf_op jit(solution)/shard_map/reduce_sum | solution.py:122
  101.9 0.8 fusion.5
  102.7 0.1 copy.67
  102.9 0.9 reshape.230
  103.8 9.6 %all-to-all-done.6 = bf16[256,4,320]{0,2,1:T(8,128)(2,1)S(1)} async-done(((bf16[256,4,320]{0,2,1:T(8,128)(2,1)}), bf16[256,4,320]{0,2,1:T(8,128)(2,1)S(1)}, u32[]{:S(2)}, u32[]{:S(2)}) %all-to-all-start.6) | async-done | bytes 655392 | tf_op jit(solution)/shard_map/all_to_all | solution.py:135
  113.4 4.4 %all-to-all-start.5 = ((bf16[16,2,2048]{2,1,0:T(2,128)(2,1)}), bf16[16,2,2048]{2,1,0:T(2,128)(2,1)S(1)}, u32[]{:S(2)}, u32[]{:S(2)}) async-start(bf16[16,2,2048]{2,1,0:T(2,128)(2,1)} %reshape.230), calls=%async_computation.5 | async-start | bytes 262144 | tf_op jit(solution)/shard_map/all_to_all | solution.py:133
  117.9 10.0 %all-to-all-done.5 = bf16[16,2,2048]{2,1,0:T(2,128)(2,1)S(1)} async-done(((bf16[16,2,2048]{2,1,0:T(2,128)(2,1)}), bf16[16,2,2048]{2,1,0:T(2,128)(2,1)S(1)}, u32[]{:S(2)}, u32[]{:S(2)}) %all-to-all-start.5) | async-done | bytes 131104 | tf_op jit(solution)/shard_map/all_to_all | solution.py:133
  127.9 0.2 reshape.231
  128.1 0.2 copy.62
  128.3 0.2 reshape.220
  128.5 1.0 fusion.3
  (46 shorter events, 1.0 us)
Async XLA Ops:
  7.2 69.6 %copy-start = (bf16[1280,256]{1,0:T(8,128)(2,1)S(1)}, bf16[1280,256]{1,0:T(8,128)(2,1)}, u32[]{:S(2)}) copy-start(bf16[1280,256]{1,0:T(8,128)(2,1)} %param.17) | copy-start | bytes 1966084
  7.2 71.5 %copy-start.3 = (bf16[1280,256]{1,0:T(8,128)(2,1)S(1)}, bf16[1280,256]{1,0:T(8,128)(2,1)}, u32[]{:S(2)}) copy-start(bf16[1280,256]{1,0:T(8,128)(2,1)} %param.16) | copy-start | bytes 1966084
  9.9 9.3 %all-to-all-start = ((bf16[4,2,4096]{2,1,0:T(2,128)(2,1)}), bf16[4,2,4096]{2,1,0:T(2,128)(2,1)S(1)}, u32[]{:S(2)}, u32[]{:S(2)}) async-start(bf16[4,2,4096]{2,1,0:T(2,128)(2,1)} %reshape.228), calls=%async_computation | async-start | bytes 131072 | tf_op jit(solution)/shard_map/all_to_all | solution.py:80
  20.3 12.6 %all-to-all-start.1 = ((bf16[4,2,256,64]{2,3,1,0:T(8,128)(2,1)}), bf16[4,2,256,64]{2,3,1,0:T(8,128)(2,1)S(1)}, u32[]{:S(2)}, u32[]{:S(2)}) async-start(bf16[4,2,256,64]{2,3,1,0:T(8,128)(2,1)} %broadcast_in_dim.23), calls=%async_computation.1 | async-start | bytes 524288 | tf_op jit(solution)/shard_map/all_to_all | solution.py:29
  33.5 10.9 %all-to-all-start.2 = ((f32[16,2,8]{2,1,0:T(2,128)}), f32[16,2,8]{2,1,0:T(2,128)S(1)}, u32[]{:S(2)}, u32[]{:S(2)}) async-start(f32[16,2,8]{2,1,0:T(2,128)} %broadcast_in_dim.24), calls=%async_computation.2 | async-start | bytes 32768 | tf_op jit(solution)/shard_map/all_to_all | solution.py:29
  37.5 59.5 %all-gather.3.cloned.1.call-start = ((), (), s32[]{:S(2)}) async-start(), calls=%async_computation.7 | async-start | bytes 2359296 | tf_op jit(solution)/shard_map/all_gather | solution.py:82
  45.3 15.1 %all-to-all-start.3 = ((f32[8,2,8]{2,1,0:T(2,128)}), f32[8,2,8]{2,1,0:T(2,128)S(1)}, u32[]{:S(2)}, u32[]{:S(2)}) async-start(f32[8,2,8]{2,1,0:T(2,128)} %broadcast_in_dim.25), calls=%async_computation.3 | async-start | bytes 16384 | tf_op jit(solution)/shard_map/all_to_all | solution.py:29
  77.0 22.5 %copy-start.4 = (bf16[64,256]{1,0:T(8,128)(2,1)}, bf16[64,256]{1,0:T(8,128)(2,1)S(1)}, u32[]{:S(2)}) copy-start(bf16[64,256]{1,0:T(8,128)(2,1)S(1)} %convolution_convert_fusion.1) | copy-start | bytes 98308
  78.5 21.0 %copy-start.5 = (bf16[64,256]{1,0:T(8,128)(2,1)}, bf16[64,256]{1,0:T(8,128)(2,1)S(1)}, u32[]{:S(2)}) copy-start(bf16[64,256]{1,0:T(8,128)(2,1)S(1)} %convolution_convert_fusion) | copy-start | bytes 98308
  79.9 7.9 %all-to-all-start.4 = ((bf16[4,2,6144]{2,1,0:T(2,128)(2,1)}), bf16[4,2,6144]{2,1,0:T(2,128)(2,1)S(1)}, u32[]{:S(2)}, u32[]{:S(2)}) async-start(bf16[4,2,6144]{2,1,0:T(2,128)(2,1)} %reshape.226), calls=%async_computation.4 | async-start | bytes 196608 | tf_op jit(solution)/shard_map/all_to_all | solution.py:88
  87.9 25.5 %all-to-all-start.6 = ((bf16[256,4,320]{0,2,1:T(8,128)(2,1)}), bf16[256,4,320]{0,2,1:T(8,128)(2,1)S(1)}, u32[]{:S(2)}, u32[]{:S(2)}) async-start(bf16[256,4,320]{0,2,1:T(8,128)(2,1)} %bitcast.30), calls=%async_computation.6 | async-start | bytes 1310720 | tf_op jit(solution)/shard_map/all_to_all | solution.py:135
  99.5 2.4 %copy-start.1 = (bf16[2,8192,64]{1,2,0:T(8,128)(2,1)S(1)}, bf16[2,8192,64]{1,2,0:T(8,128)(2,1)}, u32[]{:S(2)}) copy-start(bf16[2,8192,64]{1,2,0:T(8,128)(2,1)} %all-gather.3.cloned.1.call-done) | copy-start | bytes 6291460
  99.6 28.8 %copy-start.2 = (bf16[64,320]{1,0:T(8,128)(2,1)S(1)}, bf16[64,320]{1,0:T(8,128)(2,1)}, u32[]{:S(2)}) copy-start(bf16[64,320]{1,0:T(8,128)(2,1)} %param.11) | copy-start | bytes 122884
  113.4 14.5 %all-to-all-start.5 = ((bf16[16,2,2048]{2,1,0:T(2,128)(2,1)}), bf16[16,2,2048]{2,1,0:T(2,128)(2,1)S(1)}, u32[]{:S(2)}, u32[]{:S(2)}) async-start(bf16[16,2,2048]{2,1,0:T(2,128)(2,1)} %reshape.230), calls=%async_computation.5 | async-start | bytes 262144 | tf_op jit(solution)/shard_map/all_to_all | solution.py:133
Sparse Core Ops, SparseCore 0:
  40.4 44.5 all-gather.2

commit v14 on v10

--- a/solution.py
+++ b/solution.py
@@ -148,13 +148,11 @@
     numer = stale_num + home_factor[:, None] * home_num
     denom = stale_den + home_factor * home_den
     result = (numer / denom[:, None]).astype(jnp.bfloat16)
-    result = result.reshape(1, split, rows_here, HEAD_DIM)
-    result = jnp.broadcast_to(result, (chan_count, split, rows_here, HEAD_DIM))
-    result = result.reshape(chan_count * split, rows_here, HEAD_DIM)
-    attended = lax.all_to_all(result, ("chan", "px"), 0, 0, tiled=True)
-    attended = jnp.transpose(attended, (1, 0, 2)).reshape(rows_here, chan_count * inner)
-    out_columns = lax.all_to_all(w_out, "chan", 1, 0, tiled=True)
-    projected = jnp.dot(attended, out_columns, preferred_element_type=jnp.float32)
+    result = result.reshape(split, rows_here, 1, HEAD_DIM)
+    attended = lax.all_to_all(result, "px", 0, 2, tiled=True).reshape(rows_here, inner)
+    partial = jnp.dot(attended, w_out, preferred_element_type=jnp.float32)
+    partial = jnp.moveaxis(partial.reshape(rows_here, chan_count, chan_width), 1, 0)
+    projected = jnp.sum(lax.all_to_all(partial, "chan", 0, 0, tiled=True), axis=0)
     mixed = (latent.astype(jnp.float32) + projected).astype(jnp.bfloat16)
     return (mixed, fresh_keys, fresh_values)
 

time: 138 us -> 135 us (0.978)
  blocking collectives: 14.8 us -> 36.1 us
  waiting for transfers between devices: 40.6 us -> 27.2 us
  starting transfers between devices: 40.2 us -> 30.9 us
  local copies, waits for them, and re-layouts: 12.2 us -> 9.56 us
    all_to_all x0 -> x1, blocking collectives: none -> 21.3 us  [local(): lax.all_to_all(partial, 'chan', 0, 0, tiled=True)]
    all_to_all x2 -> x1, waiting for transfers between devices: 19.6 us -> 4.01 us  [local(): lax.all_to_all(result, 'px', 0, 2, tiled=True).reshape(rows_here, inner)]
    all_to_all x2 -> x1, starting transfers between devices: 12.6 us -> 3.26 us  [local(): lax.all_to_all(result, 'px', 0, 2, tiled=True).reshape(rows_here, inner)]
    unnamed x23, local copies, waits for them, and re-layouts: 7.33 us -> 5.12 us
    all_to_all x3, waiting for transfers between devices: 13.1 us -> 15.2 us  [replicated_gather(): return lax.all_to_all(copies, name, 0, 0, tiled=True)]
  transfers between devices with their start and end apart: 8 -> 7, of which waited for: 7 -> 6; matrix products, arithmetic and copies ran while one was open for 14% -> 9% of each run, Pallas kernels for 0% -> 0%
where the time goes in v14:
time: 135 us; the launch traced here: 133 us
  blocking collectives  36.1 us (27%)
  starting transfers between devices  30.9 us (23%)
  waiting for transfers between devices  27.2 us (20%)
  between operations  15.1 us (11%)
  local copies, waits for them, and re-layouts  9.56 us (7%)
  matrix products  8.14 us (6%)
  other arithmetic  6.34 us (5%)
    all_to_all x1, blocking collectives, local(): lax.all_to_all(partial, 'chan', 0, 0, tiled=True)  21.3 us
    all_to_all x3, starting transfers between devices, replicated_gather(): return lax.all_to_all(copies, name, 0, 0, tiled=True)  19.5 us
    all_to_all x3, waiting for transfers between devices, replicated_gather(): return lax.all_to_all(copies, name, 0, 0, tiled=True)  15.2 us
    all_gather x1, blocking collectives, local(): shard_piece = lax.all_gather(normed, 'chan', axis=1, tiled=True)  14.8 us
    unnamed x23, local copies, waits for them, and re-layouts  5.12 us
    all_to_all x1, starting transfers between devices, local(): lax.all_to_all(stacked, 'px', 2, 1, tiled=True)  4.83 us
    all_to_all x1, waiting for transfers between devices, local(): lax.all_to_all(fresh, 'px', 2, 1, tiled=True)  4.66 us
    all_to_all x1, waiting for transfers between devices, local(): lax.all_to_all(result, 'px', 0, 2, tiled=True).reshape(rows_here, inner)  4.01 us
  transfers between devices with their start and end apart: 7, of which 6 were waited for; matrix products, arithmetic and copies ran while one was open for 9% of the time, Pallas kernels for 0%

profile of v14, /device:TPU:1, one launch (start us, length us, event | category | flops | bytes accessed | tf_op | source)
XLA Modules:
  0.0 133.3 jit_solution(4508890753312047174)
XLA Ops:
  7.2 0.9 copy.47
  8.1 0.9 copy.48
  9.0 0.8 reshape.227
  9.8 4.8 %all-to-all-start = ((bf16[4,2,4096]{2,1,0:T(2,128)(2,1)}), bf16[4,2,4096]{2,1,0:T(2,128)(2,1)S(1)}, u32[]{:S(2)}, u32[]{:S(2)}) async-start(bf16[4,2,4096]{2,1,0:T(2,128)(2,1)} %reshape.227), calls=%async_computation | async-start | bytes 131072 | tf_op jit(solution)/shard_map/all_to_all | solution.py:102
  14.7 0.8 convert_reduce_fusion.1
  15.5 0.1 reduce_sum.114
  15.6 0.1 reduce_sum.115
  15.7 0.1 sub.93
  15.8 0.1 sub.94
  15.8 3.3 %all-to-all-done = bf16[4,2,4096]{2,1,0:T(2,128)(2,1)S(1)} async-done(((bf16[4,2,4096]{2,1,0:T(2,128)(2,1)}), bf16[4,2,4096]{2,1,0:T(2,128)(2,1)S(1)}, u32[]{:S(2)}, u32[]{:S(2)}) %all-to-all-start) | async-done | bytes 65568 | tf_op jit(solution)/shard_map/all_to_all | solution.py:102
  19.1 0.1 reshape.228
  19.3 0.1 copy.49
  19.4 0.1 broadcast_in_dim.18
  19.6 0.7 broadcast_in_dim.19
  20.3 7.0 %all-to-all-start.1 = ((bf16[4,2,256,64]{2,3,1,0:T(8,128)(2,1)}), bf16[4,2,256,64]{2,3,1,0:T(8,128)(2,1)S(1)}, u32[]{:S(2)}, u32[]{:S(2)}) async-start(bf16[4,2,256,64]{2,3,1,0:T(8,128)(2,1)} %broadcast_in_dim.19), calls=%async_computation.1 | async-start | bytes 524288 | tf_op jit(solution)/shard_map/all_to_all | solution.py:35
  27.2 0.8 fusion.8
  28.1 0.1 reduce_sum.117
  28.2 0.1 reduce_sum.118
  29.0 0.1 divide_multiply_fusion
  29.1 3.8 %all-to-all-done.1 = bf16[4,2,256,64]{2,3,1,0:T(8,128)(2,1)S(1)} async-done(((bf16[4,2,256,64]{2,3,1,0:T(8,128)(2,1)}), bf16[4,2,256,64]{2,3,1,0:T(8,128)(2,1)S(1)}, u32[]{:S(2)}, u32[]{:S(2)}) %all-to-all-start.1) | async-done | bytes 262176 | tf_op jit(solution)/shard_map/all_to_all | solution.py:35
  32.9 0.6 broadcast_in_dim.20
  33.5 4.0 %all-to-all-start.2 = ((f32[16,2,8]{2,1,0:T(2,128)}), f32[16,2,8]{2,1,0:T(2,128)S(1)}, u32[]{:S(2)}, u32[]{:S(2)}) async-start(f32[16,2,8]{2,1,0:T(2,128)} %broadcast_in_dim.20), calls=%async_computation.2 | async-start | bytes 32768 | tf_op jit(solution)/shard_map/all_to_all | solution.py:35
  37.5 1.2 convolution_reduce_fusion
  38.7 0.8 copy.69
  39.5 4.8 %all-to-all-done.2 = f32[16,2,8]{2,1,0:T(2,128)S(1)} async-done(((f32[16,2,8]{2,1,0:T(2,128)}), f32[16,2,8]{2,1,0:T(2,128)S(1)}, u32[]{:S(2)}, u32[]{:S(2)}) %all-to-all-start.2) | async-done | bytes 1056 | tf_op jit(solution)/shard_map/all_to_all | solution.py:35
  44.4 0.2 fusion.19
  44.7 0.6 broadcast_in_dim.21
  45.3 8.5 %all-to-all-start.3 = ((f32[8,2,8]{2,1,0:T(2,128)}), f32[8,2,8]{2,1,0:T(2,128)S(1)}, u32[]{:S(2)}, u32[]{:S(2)}) async-start(f32[8,2,8]{2,1,0:T(2,128)} %broadcast_in_dim.21), calls=%async_computation.3 | async-start | bytes 16384 | tf_op jit(solution)/shard_map/all_to_all | solution.py:35
  53.7 6.6 %all-to-all-done.3 = f32[8,2,8]{2,1,0:T(2,128)S(1)} async-done(((f32[8,2,8]{2,1,0:T(2,128)}), f32[8,2,8]{2,1,0:T(2,128)S(1)}, u32[]{:S(2)}, u32[]{:S(2)}) %all-to-all-start.3) | async-done | bytes 544 | tf_op jit(solution)/shard_map/all_to_all | solution.py:35
  60.4 0.1 mul.110
  60.5 0.1 mul.111
  60.6 0.1 sub.99
  60.6 0.1 sub.100
  60.7 0.9 fusion.17
  61.6 14.8 %all-gather = bf16[4,320,64]{1,2,0:T(8,128)(2,1)S(1)} all-gather(bf16[1,320,64]{1,2,0:T(8,128)(2,1)S(1)} %fusion.17), channel_id=1, replica_groups=mesh['py'=8,'pz'=4,'px'=4,'chan'=4] {'chan'}, dimensions={0}, use_global_device_ids=true | all-gather | bytes 204800 | tf_op jit(solution)/shard_map/all_gather | solution.py:88
  76.4 0.2 copy.53
  76.5 0.2 reshape.220
  76.7 0.2 convolution_convert_fusion.1
  77.0 0.1 stack.40
  77.1 1.3 %convolution_convert_fusion = bf16[64,256]{1,0:T(8,128)(2,1)S(1)} fusion(bf16[1280,64]{0,1:T(8,128)(2,1)S(1)} %reshape.220, bf16[1280,256]{1,0:T(8,128)(2,1)} %param.18), kind=kOutput, calls=%fused_computation.13 | convolution fusion | flops 41959424 | bytes 851968 | tf_op jit(solution)/shard_map/dot_general | solution.py:91
  78.5 0.1 stack.41
  78.6 1.3 %convolution_convert_fusion.2 = bf16[64,256]{1,0:T(8,128)(2,1)S(1)} fusion(bf16[1280,64]{0,1:T(8,128)(2,1)S(1)} %reshape.220, bf16[1280,256]{1,0:T(8,128)(2,1)} %param.16), kind=kOutput, calls=%fused_computation.15 | convolution fusion | flops 41959424 | bytes 851968 | tf_op jit(solution)/shard_map/dot_general | solution.py:91
  79.9 0.1 stack.39
  80.1 0.8 reshape.225
  81.0 3.3 %all-to-all-start.4 = ((bf16[4,2,6144]{2,1,0:T(2,128)(2,1)}), bf16[4,2,6144]{2,1,0:T(2,128)(2,1)S(1)}, u32[]{:S(2)}, u32[]{:S(2)}) async-start(bf16[4,2,6144]{2,1,0:T(2,128)(2,1)} %reshape.225), calls=%async_computation.4 | async-start | bytes 196608 | tf_op jit(solution)/shard_map/all_to_all | solution.py:110
  84.3 4.7 %all-to-all-done.4 = bf16[4,2,6144]{2,1,0:T(2,128)(2,1)S(1)} async-done(((bf16[4,2,6144]{2,1,0:T(2,128)(2,1)}), bf16[4,2,6144]{2,1,0:T(2,128)(2,1)S(1)}, u32[]{:S(2)}, u32[]{:S(2)}) %all-to-all-start.4) | async-done | bytes 98336 | tf_op jit(solution)/shard_map/all_to_all | solution.py:110
  88.9 0.2 reshape.226
  89.2 0.2 fusion.28
  89.3 0.1 broadcast_in_dim.23
  89.5 0.1 reshape.216
  89.6 0.2 fusion.15
  89.8 0.1 copy.64
  89.9 2.5 %bitcast_reduce_fusion = (f32[128,256]{1,0:T(8,128)S(1)}, f32[8192,256]{1,0:T(8,128)S(1)}) fusion(bf16[256,64]{1,0:T(8,128)(2,1)S(1)} %bitcast.121, bf16[2,8192,64]{1,2,0:T(8,128)(2,1)} %all-gather.3.cloned.1.call-done), kind=kOutput, calls=%fused_computation.6 | convolution fusion | flops 272596992 | bytes 9601024 | tf_op jit(solution)/shard_map/kd,qd->kq/dot_general | solution.py:116
  92.6 2.2 %convert_reduce_fusion = (f32[256]{0:T(256)S(1)}, bf16[8192,256]{1,0:T(8,128)(2,1)S(1)}) fusion(f32[128,256]{1,0:T(8,128)S(1)} %exponential_select_fusion, f32[8192,256]{1,0:T(8,128)S(1)} %get-tuple-element.17, f32[128,256]{1,0:T(8,128)S(1)} %get-tuple-element.16), kind=kLoop, calls=%fused_computation.7 | loop fusion | flops 14679808 | bytes 12846080 | tf_op jit(solution)/shard_map/reduce_sum | solution.py:143
  94.8 0.8 fusion.4
  95.6 0.1 reshape.217
  95.8 0.7 reshape.229
  96.5 3.3 %all-to-all-start.5 = ((bf16[4,2,2048]{2,1,0:T(2,128)(2,1)}), bf16[4,2,2048]{2,1,0:T(2,128)(2,1)S(1)}, u32[]{:S(2)}, u32[]{:S(2)}) async-start(bf16[4,2,2048]{2,1,0:T(2,128)(2,1)} %reshape.229), calls=%async_computation.5 | async-start | bytes 65536 | tf_op jit(solution)/shard_map/all_to_all | solution.py:152
  99.8 0.2 copy.62
  100.0 4.0 %all-to-all-done.5 = bf16[4,2,2048]{2,1,0:T(2,128)(2,1)S(1)} async-done(((bf16[4,2,2048]{2,1,0:T(2,128)(2,1)}), bf16[4,2,2048]{2,1,0:T(2,128)(2,1)S(1)}, u32[]{:S(2)}, u32[]{:S(2)}) %all-to-all-start.5) | async-done | bytes 32800 | tf_op jit(solution)/shard_map/all_to_all | solution.py:152
  104.0 0.1 reshape.230
  104.1 0.3 convolution_bitcast_fusion
  104.5 21.3 %all_to_all.65 = f32[4,64,320]{2,1,0:T(8,128)S(1)} all-to-all(f32[4,64,320]{2,1,0:T(8,128)S(1)} %convolution_bitcast_fusion), channel_id=1, replica_groups=mesh['py'=8,'pz'=4,'px'=4,'chan'=4] {'chan'}, dimensions={0} | all-to-all | bytes 655360 | tf_op jit(solution)/shard_map/all_to_all | solution.py:155
  125.8 0.6 fusion.14
  (44 shorter events, 0.7 us)
Async XLA Ops:
  7.2 69.6 %copy-start = (bf16[1280,256]{1,0:T(8,128)(2,1)S(1)}, bf16[1280,256]{1,0:T(8,128)(2,1)}, u32[]{:S(2)}) copy-start(bf16[1280,256]{1,0:T(8,128)(2,1)} %param.17) | copy-start | bytes 1966084
  9.8 9.3 %all-to-all-start = ((bf16[4,2,4096]{2,1,0:T(2,128)(2,1)}), bf16[4,2,4096]{2,1,0:T(2,128)(2,1)S(1)}, u32[]{:S(2)}, u32[]{:S(2)}) async-start(bf16[4,2,4096]{2,1,0:T(2,128)(2,1)} %reshape.227), calls=%async_computation | async-start | bytes 131072 | tf_op jit(solution)/shard_map/all_to_all | solution.py:102
  20.3 12.6 %all-to-all-start.1 = ((bf16[4,2,256,64]{2,3,1,0:T(8,128)(2,1)}), bf16[4,2,256,64]{2,3,1,0:T(8,128)(2,1)S(1)}, u32[]{:S(2)}, u32[]{:S(2)}) async-start(bf16[4,2,256,64]{2,3,1,0:T(8,128)(2,1)} %broadcast_in_dim.19), calls=%async_computation.1 | async-start | bytes 524288 | tf_op jit(solution)/shard_map/all_to_all | solution.py:35
  33.5 10.9 %all-to-all-start.2 = ((f32[16,2,8]{2,1,0:T(2,128)}), f32[16,2,8]{2,1,0:T(2,128)S(1)}, u32[]{:S(2)}, u32[]{:S(2)}) async-start(f32[16,2,8]{2,1,0:T(2,128)} %broadcast_in_dim.20), calls=%async_computation.2 | async-start | bytes 32768 | tf_op jit(solution)/shard_map/all_to_all | solution.py:35
  37.5 52.4 %all-gather.3.cloned.1.call-start = ((), (), s32[]{:S(2)}) async-start(), calls=%async_computation.7 | async-start | bytes 2359296 | tf_op jit(solution)/shard_map/all_gather | solution.py:104
  45.3 15.1 %all-to-all-start.3 = ((f32[8,2,8]{2,1,0:T(2,128)}), f32[8,2,8]{2,1,0:T(2,128)S(1)}, u32[]{:S(2)}, u32[]{:S(2)}) async-start(f32[8,2,8]{2,1,0:T(2,128)} %broadcast_in_dim.21), calls=%async_computation.3 | async-start | bytes 16384 | tf_op jit(solution)/shard_map/all_to_all | solution.py:35
  77.0 15.5 %copy-start.4 = (bf16[64,256]{1,0:T(8,128)(2,1)}, bf16[64,256]{1,0:T(8,128)(2,1)S(1)}, u32[]{:S(2)}) copy-start(bf16[64,256]{1,0:T(8,128)(2,1)S(1)} %convolution_convert_fusion.1) | copy-start | bytes 98308
  78.4 14.0 %copy-start.5 = (bf16[64,256]{1,0:T(8,128)(2,1)}, bf16[64,256]{1,0:T(8,128)(2,1)S(1)}, u32[]{:S(2)}) copy-start(bf16[64,256]{1,0:T(8,128)(2,1)S(1)} %convolution_convert_fusion) | copy-start | bytes 98308
  81.0 8.0 %all-to-all-start.4 = ((bf16[4,2,6144]{2,1,0:T(2,128)(2,1)}), bf16[4,2,6144]{2,1,0:T(2,128)(2,1)S(1)}, u32[]{:S(2)}, u32[]{:S(2)}) async-start(bf16[4,2,6144]{2,1,0:T(2,128)(2,1)} %reshape.225), calls=%async_computation.4 | async-start | bytes 196608 | tf_op jit(solution)/shard_map/all_to_all | solution.py:110
  92.5 2.4 %copy-start.1 = (bf16[2,8192,64]{1,2,0:T(8,128)(2,1)S(1)}, bf16[2,8192,64]{1,2,0:T(8,128)(2,1)}, u32[]{:S(2)}) copy-start(bf16[2,8192,64]{1,2,0:T(8,128)(2,1)} %all-gather.3.cloned.1.call-done) | copy-start | bytes 6291460
  92.6 7.2 %copy-start.3 = (bf16[256,1280]{1,0:T(8,128)(2,1)S(1)}, bf16[256,1280]{1,0:T(8,128)(2,1)}, u32[]{:S(2)}) copy-start(bf16[256,1280]{1,0:T(8,128)(2,1)} %param.19) | copy-start | bytes 1966084
  92.6 33.3 %copy-start.2 = (bf16[64,320]{1,0:T(8,128)(2,1)S(1)}, bf16[64,320]{1,0:T(8,128)(2,1)}, u32[]{:S(2)}) copy-start(bf16[64,320]{1,0:T(8,128)(2,1)} %param.11) | copy-start | bytes 122884
  96.5 7.5 %all-to-all-start.5 = ((bf16[4,2,2048]{2,1,0:T(2,128)(2,1)}), bf16[4,2,2048]{2,1,0:T(2,128)(2,1)S(1)}, u32[]{:S(2)}, u32[]{:S(2)}) async-start(bf16[4,2,2048]{2,1,0:T(2,128)(2,1)} %reshape.229), calls=%async_computation.5 | async-start | bytes 65536 | tf_op jit(solution)/shard_map/all_to_all | solution.py:152
Sparse Core Ops, SparseCore 0:
  40.4 44.5 all-gather.2

commit v15 on v14

--- a/solution.py
+++ b/solution.py
@@ -72,7 +72,7 @@
     count = rows_here * width
     group_mean = jnp.sum(values, axis=(0, 2)) / count
     spread = jnp.sum(jnp.square(values - group_mean[None, :, None]), axis=(0, 2))
-    for name in (PATCH_AXES[1:], PATCH_AXES[0]):
+    for name in (PATCH_AXES[0], PATCH_AXES[1:]):
         gathered = replicated_gather(jnp.stack([group_mean, spread]), name)
         group_mean = jnp.mean(gathered[:, 0], axis=0)
         offset = gathered[:, 0] - group_mean[None, :]

time: 135 us -> 136 us (level)
  blocking collectives: 36.1 us -> 37.7 us
    all_to_all x1, blocking collectives: 21.3 us -> 22.9 us  [local(): lax.all_to_all(partial, 'chan', 0, 0, tiled=True)]
where the time goes in v15:
time: 136 us; the launch traced here: 135 us
  blocking collectives  37.7 us (28%)
  starting transfers between devices  30.9 us (23%)
  waiting for transfers between devices  27.2 us (20%)
  between operations  15.1 us (11%)
  local copies, waits for them, and re-layouts  9.57 us (7%)
  matrix products  8.14 us (6%)
  other arithmetic  6.33 us (5%)
    all_to_all x1, blocking collectives, local(): lax.all_to_all(partial, 'chan', 0, 0, tiled=True)  22.9 us
    all_to_all x3, starting transfers between devices, replicated_gather(): return lax.all_to_all(copies, name, 0, 0, tiled=True)  19.5 us
    all_to_all x3, waiting for transfers between devices, replicated_gather(): return lax.all_to_all(copies, name, 0, 0, tiled=True)  15.2 us
    all_gather x1, blocking collectives, local(): shard_piece = lax.all_gather(normed, 'chan', axis=1, tiled=True)  14.7 us
    unnamed x23, local copies, waits for them, and re-layouts  5.12 us
    all_to_all x1, starting transfers between devices, local(): lax.all_to_all(stacked, 'px', 2, 1, tiled=True)  4.83 us
    all_to_all x1, waiting for transfers between devices, local(): lax.all_to_all(fresh, 'px', 2, 1, tiled=True)  4.66 us
    all_to_all x1, waiting for transfers between devices, local(): lax.all_to_all(result, 'px', 0, 2, tiled=True).reshape(rows_here, inner)  4.01 us
  transfers between devices with their start and end apart: 7, of which 6 were waited for; matrix products, arithmetic and copies ran while one was open for 9% of the time, Pallas kernels for 0%

profile of v15, /device:TPU:1, one launch (start us, length us, event | category | flops | bytes accessed | tf_op | source)
XLA Modules:
  0.0 134.9 jit_solution(7925959101008994545)
XLA Ops:
  7.2 0.9 copy.47
  8.1 0.9 copy.48
  9.0 0.8 reshape.227
  9.8 4.8 %all-to-all-start = ((bf16[4,2,4096]{2,1,0:T(2,128)(2,1)}), bf16[4,2,4096]{2,1,0:T(2,128)(2,1)S(1)}, u32[]{:S(2)}, u32[]{:S(2)}) async-start(bf16[4,2,4096]{2,1,0:T(2,128)(2,1)} %reshape.227), calls=%async_computation | async-start | bytes 131072 | tf_op jit(solution)/shard_map/all_to_all | solution.py:102
  14.7 0.8 convert_reduce_fusion.1
  15.5 0.1 reduce_sum.114
  15.6 0.1 reduce_sum.115
  15.7 0.1 sub.93
  15.8 0.1 sub.94
  15.8 3.3 %all-to-all-done = bf16[4,2,4096]{2,1,0:T(2,128)(2,1)S(1)} async-done(((bf16[4,2,4096]{2,1,0:T(2,128)(2,1)}), bf16[4,2,4096]{2,1,0:T(2,128)(2,1)S(1)}, u32[]{:S(2)}, u32[]{:S(2)}) %all-to-all-start) | async-done | bytes 65568 | tf_op jit(solution)/shard_map/all_to_all | solution.py:102
  19.1 0.1 reshape.228
  19.3 0.1 copy.49
  19.4 0.1 broadcast_in_dim.18
  19.6 0.7 broadcast_in_dim.19
  20.3 7.0 %all-to-all-start.1 = ((bf16[4,2,256,64]{2,3,1,0:T(8,128)(2,1)}), bf16[4,2,256,64]{2,3,1,0:T(8,128)(2,1)S(1)}, u32[]{:S(2)}, u32[]{:S(2)}) async-start(bf16[4,2,256,64]{2,3,1,0:T(8,128)(2,1)} %broadcast_in_dim.19), calls=%async_computation.1 | async-start | bytes 524288 | tf_op jit(solution)/shard_map/all_to_all | solution.py:35
  27.2 0.8 fusion.8
  28.1 0.1 reduce_sum.117
  28.2 0.1 reduce_sum.118
  29.0 0.1 divide_multiply_fusion
  29.1 3.8 %all-to-all-done.1 = bf16[4,2,256,64]{2,3,1,0:T(8,128)(2,1)S(1)} async-done(((bf16[4,2,256,64]{2,3,1,0:T(8,128)(2,1)}), bf16[4,2,256,64]{2,3,1,0:T(8,128)(2,1)S(1)}, u32[]{:S(2)}, u32[]{:S(2)}) %all-to-all-start.1) | async-done | bytes 262176 | tf_op jit(solution)/shard_map/all_to_all | solution.py:35
  32.9 0.6 broadcast_in_dim.20
  33.5 6.8 %all-to-all-start.2 = ((f32[8,2,8]{2,1,0:T(2,128)}), f32[8,2,8]{2,1,0:T(2,128)S(1)}, u32[]{:S(2)}, u32[]{:S(2)}) async-start(f32[8,2,8]{2,1,0:T(2,128)} %broadcast_in_dim.20), calls=%async_computation.2 | async-start | bytes 16384 | tf_op jit(solution)/shard_map/all_to_all | solution.py:35
  40.4 1.2 convolution_reduce_fusion
  41.5 0.8 copy.69
  42.3 4.6 %all-to-all-done.2 = f32[8,2,8]{2,1,0:T(2,128)S(1)} async-done(((f32[8,2,8]{2,1,0:T(2,128)}), f32[8,2,8]{2,1,0:T(2,128)S(1)}, u32[]{:S(2)}, u32[]{:S(2)}) %all-to-all-start.2) | async-done | bytes 544 | tf_op jit(solution)/shard_map/all_to_all | solution.py:35
  47.0 0.6 broadcast_in_dim.21
  47.6 5.6 %all-to-all-start.3 = ((f32[16,2,8]{2,1,0:T(2,128)}), f32[16,2,8]{2,1,0:T(2,128)S(1)}, u32[]{:S(2)}, u32[]{:S(2)}) async-start(f32[16,2,8]{2,1,0:T(2,128)} %broadcast_in_dim.21), calls=%async_computation.3 | async-start | bytes 32768 | tf_op jit(solution)/shard_map/all_to_all | solution.py:35
  53.3 6.8 %all-to-all-done.3 = f32[16,2,8]{2,1,0:T(2,128)S(1)} async-done(((f32[16,2,8]{2,1,0:T(2,128)}), f32[16,2,8]{2,1,0:T(2,128)S(1)}, u32[]{:S(2)}, u32[]{:S(2)}) %all-to-all-start.3) | async-done | bytes 1056 | tf_op jit(solution)/shard_map/all_to_all | solution.py:35
  60.2 0.2 fusion.19
  60.4 0.1 mul.110
  60.5 0.1 mul.111
  60.6 0.1 sub.99
  60.6 0.1 sub.100
  60.7 0.8 fusion.17
  61.6 14.7 %all-gather = bf16[4,320,64]{1,2,0:T(8,128)(2,1)S(1)} all-gather(bf16[1,320,64]{1,2,0:T(8,128)(2,1)S(1)} %fusion.17), channel_id=1, replica_groups=mesh['py'=8,'pz'=4,'px'=4,'chan'=4] {'chan'}, dimensions={0}, use_global_device_ids=true | all-gather | bytes 204800 | tf_op jit(solution)/shard_map/all_gather | solution.py:88
  76.3 0.2 copy.53
  76.5 0.2 reshape.220
  76.7 0.2 convolution_convert_fusion.1
  76.9 0.1 stack.40
  77.0 1.3 convolution_convert_fusion
  78.4 0.1 stack.41
  78.5 1.3 convolution_convert_fusion.2
  79.9 0.1 stack.39
  80.0 0.8 reshape.225
  80.9 3.3 %all-to-all-start.4 = ((bf16[4,2,6144]{2,1,0:T(2,128)(2,1)}), bf16[4,2,6144]{2,1,0:T(2,128)(2,1)S(1)}, u32[]{:S(2)}, u32[]{:S(2)}) async-start(bf16[4,2,6144]{2,1,0:T(2,128)(2,1)} %reshape.225), calls=%async_computation.4 | async-start | bytes 196608 | tf_op jit(solution)/shard_map/all_to_all | solution.py:110
  84.2 4.7 %all-to-all-done.4 = bf16[4,2,6144]{2,1,0:T(2,128)(2,1)S(1)} async-done(((bf16[4,2,6144]{2,1,0:T(2,128)(2,1)}), bf16[4,2,6144]{2,1,0:T(2,128)(2,1)S(1)}, u32[]{:S(2)}, u32[]{:S(2)}) %all-to-all-start.4) | async-done | bytes 98336 | tf_op jit(solution)/shard_map/all_to_all | solution.py:110
  88.9 0.2 reshape.226
  89.1 0.2 fusion.28
  89.3 0.1 broadcast_in_dim.23
  89.4 0.1 reshape.216
  89.5 0.2 fusion.15
  89.7 0.1 copy.64
  89.8 2.5 %bitcast_reduce_fusion = (f32[128,256]{1,0:T(8,128)S(1)}, f32[8192,256]{1,0:T(8,128)S(1)}) fusion(bf16[256,64]{1,0:T(8,128)(2,1)S(1)} %bitcast.121, bf16[2,8192,64]{1,2,0:T(8,128)(2,1)} %all-gather.3.cloned.1.call-done), kind=kOutput, calls=%fused_computation.6 | convolution fusion | flops 272596992 | bytes 9601024 | tf_op jit(solution)/shard_map/kd,qd->kq/dot_general | solution.py:116
  92.5 2.2 %convert_reduce_fusion = (f32[256]{0:T(256)S(1)}, bf16[8192,256]{1,0:T(8,128)(2,1)S(1)}) fusion(f32[128,256]{1,0:T(8,128)S(1)} %exponential_select_fusion, f32[8192,256]{1,0:T(8,128)S(1)} %get-tuple-element.17, f32[128,256]{1,0:T(8,128)S(1)} %get-tuple-element.16), kind=kLoop, calls=%fused_computation.7 | loop fusion | flops 14679808 | bytes 12846080 | tf_op jit(solution)/shard_map/reduce_sum | solution.py:143
  94.8 0.8 fusion.4
  95.6 0.1 reshape.217
  95.7 0.7 reshape.229
  96.4 3.3 %all-to-all-start.5 = ((bf16[4,2,2048]{2,1,0:T(2,128)(2,1)}), bf16[4,2,2048]{2,1,0:T(2,128)(2,1)S(1)}, u32[]{:S(2)}, u32[]{:S(2)}) async-start(bf16[4,2,2048]{2,1,0:T(2,128)(2,1)} %reshape.229), calls=%async_computation.5 | async-start | bytes 65536 | tf_op jit(solution)/shard_map/all_to_all | solution.py:152
  99.7 0.2 copy.62
  100.0 4.0 %all-to-all-done.5 = bf16[4,2,2048]{2,1,0:T(2,128)(2,1)S(1)} async-done(((bf16[4,2,2048]{2,1,0:T(2,128)(2,1)}), bf16[4,2,2048]{2,1,0:T(2,128)(2,1)S(1)}, u32[]{:S(2)}, u32[]{:S(2)}) %all-to-all-start.5) | async-done | bytes 32800 | tf_op jit(solution)/shard_map/all_to_all | solution.py:152
  104.0 0.1 reshape.230
  104.1 0.3 convolution_bitcast_fusion
  104.4 22.9 %all_to_all.65 = f32[4,64,320]{2,1,0:T(8,128)S(1)} all-to-all(f32[4,64,320]{2,1,0:T(8,128)S(1)} %convolution_bitcast_fusion), channel_id=1, replica_groups=mesh['py'=8,'pz'=4,'px'=4,'chan'=4] {'chan'}, dimensions={0} | all-to-all | bytes 655360 | tf_op jit(solution)/shard_map/all_to_all | solution.py:155
  127.4 0.6 fusion.14
  (44 shorter events, 0.7 us)
Async XLA Ops:
  7.2 69.5 %copy-start = (bf16[1280,256]{1,0:T(8,128)(2,1)S(1)}, bf16[1280,256]{1,0:T(8,128)(2,1)}, u32[]{:S(2)}) copy-start(bf16[1280,256]{1,0:T(8,128)(2,1)} %param.17) | copy-start | bytes 1966084
  9.8 9.3 %all-to-all-start = ((bf16[4,2,4096]{2,1,0:T(2,128)(2,1)}), bf16[4,2,4096]{2,1,0:T(2,128)(2,1)S(1)}, u32[]{:S(2)}, u32[]{:S(2)}) async-start(bf16[4,2,4096]{2,1,0:T(2,128)(2,1)} %reshape.227), calls=%async_computation | async-start | bytes 131072 | tf_op jit(solution)/shard_map/all_to_all | solution.py:102
  20.3 12.6 %all-to-all-start.1 = ((bf16[4,2,256,64]{2,3,1,0:T(8,128)(2,1)}), bf16[4,2,256,64]{2,3,1,0:T(8,128)(2,1)S(1)}, u32[]{:S(2)}, u32[]{:S(2)}) async-start(bf16[4,2,256,64]{2,3,1,0:T(8,128)(2,1)} %broadcast_in_dim.19), calls=%async_computation.1 | async-start | bytes 524288 | tf_op jit(solution)/shard_map/all_to_all | solution.py:35
  33.5 13.4 %all-to-all-start.2 = ((f32[8,2,8]{2,1,0:T(2,128)}), f32[8,2,8]{2,1,0:T(2,128)S(1)}, u32[]{:S(2)}, u32[]{:S(2)}) async-start(f32[8,2,8]{2,1,0:T(2,128)} %broadcast_in_dim.20), calls=%async_computation.2 | async-start | bytes 16384 | tf_op jit(solution)/shard_map/all_to_all | solution.py:35
  40.3 49.5 %all-gather.3.cloned.1.call-start = ((), (), s32[]{:S(2)}) async-start(), calls=%async_computation.7 | async-start | bytes 2359296 | tf_op jit(solution)/shard_map/all_gather | solution.py:104
  47.6 12.5 %all-to-all-start.3 = ((f32[16,2,8]{2,1,0:T(2,128)}), f32[16,2,8]{2,1,0:T(2,128)S(1)}, u32[]{:S(2)}, u32[]{:S(2)}) async-start(f32[16,2,8]{2,1,0:T(2,128)} %broadcast_in_dim.21), calls=%async_computation.3 | async-start | bytes 32768 | tf_op jit(solution)/shard_map/all_to_all | solution.py:35
  76.9 15.5 %copy-start.4 = (bf16[64,256]{1,0:T(8,128)(2,1)}, bf16[64,256]{1,0:T(8,128)(2,1)S(1)}, u32[]{:S(2)}) copy-start(bf16[64,256]{1,0:T(8,128)(2,1)S(1)} %convolution_convert_fusion.1) | copy-start | bytes 98308
  78.4 14.0 %copy-start.5 = (bf16[64,256]{1,0:T(8,128)(2,1)}, bf16[64,256]{1,0:T(8,128)(2,1)S(1)}, u32[]{:S(2)}) copy-start(bf16[64,256]{1,0:T(8,128)(2,1)S(1)} %convolution_convert_fusion) | copy-start | bytes 98308
  80.9 8.0 %all-to-all-start.4 = ((bf16[4,2,6144]{2,1,0:T(2,128)(2,1)}), bf16[4,2,6144]{2,1,0:T(2,128)(2,1)S(1)}, u32[]{:S(2)}, u32[]{:S(2)}) async-start(bf16[4,2,6144]{2,1,0:T(2,128)(2,1)} %reshape.225), calls=%async_computation.4 | async-start | bytes 196608 | tf_op jit(solution)/shard_map/all_to_all | solution.py:110
  92.4 2.4 %copy-start.1 = (bf16[2,8192,64]{1,2,0:T(8,128)(2,1)S(1)}, bf16[2,8192,64]{1,2,0:T(8,128)(2,1)}, u32[]{:S(2)}) copy-start(bf16[2,8192,64]{1,2,0:T(8,128)(2,1)} %all-gather.3.cloned.1.call-done) | copy-start | bytes 6291460
  92.5 7.2 %copy-start.3 = (bf16[256,1280]{1,0:T(8,128)(2,1)S(1)}, bf16[256,1280]{1,0:T(8,128)(2,1)}, u32[]{:S(2)}) copy-start(bf16[256,1280]{1,0:T(8,128)(2,1)} %param.19) | copy-start | bytes 1966084
  92.5 34.9 %copy-start.2 = (bf16[64,320]{1,0:T(8,128)(2,1)S(1)}, bf16[64,320]{1,0:T(8,128)(2,1)}, u32[]{:S(2)}) copy-start(bf16[64,320]{1,0:T(8,128)(2,1)} %param.11) | copy-start | bytes 122884
  96.4 7.5 %all-to-all-start.5 = ((bf16[4,2,2048]{2,1,0:T(2,128)(2,1)}), bf16[4,2,2048]{2,1,0:T(2,128)(2,1)S(1)}, u32[]{:S(2)}, u32[]{:S(2)}) async-start(bf16[4,2,2048]{2,1,0:T(2,128)(2,1)} %reshape.229), calls=%async_computation.5 | async-start | bytes 65536 | tf_op jit(solution)/shard_map/all_to_all | solution.py:152
Sparse Core Ops, SparseCore 0:
  43.2 43.3 all-gather.2
